TPU v7x, 256 devices: a whole 4x4x8 slice. The times are simulated.
256 devices in a mesh: dp: 32 (over z_hi, y, core), mp: 8 (over x, z_lo).
Axes of the slice: x: 4, y: 4, z: 8 (z_hi: 4, z_lo: 2; z = z_hi * 2 + z_lo), core: 2. Of those that a mesh axis runs over, the one named last changes fastest.
Arguments:
- activations: bfloat16 [2, 64, 384, 14336], P(None, 'dp', None, 'mp'), may hold values from -6 to 6
- out_grads: bfloat16 [2, 64, 384, 4096], P(None, 'dp', None, 'mp'), may hold values from -6 to 6
- proj_in: bfloat16 [14336, 64], P('mp'), may hold values from -0.046875 to 0.046875
- proj_out: bfloat16 [4096, 64], P('mp'), may hold values from -0.09375 to 0.09375
- store: bfloat16 [2, 65536, 4096], P(None, ('dp', 'mp')), may hold values from -0.09375 to 0.09375
- ckpt_rate: float32 [2], replicated, may hold values from 0.5 to 2
- store_group: int32 [65536], P(('dp', 'mp')), may hold values from 0 to 15
Outputs:
- scores: float32 [64, 65536], P(None, ('dp', 'mp'))
- group_scores: float32 [64, 16], replicated
All inputs are finite; a program needn't handle non-finite values.
Results may differ from a plain program's by a relative error of at most 0.005.
Values may be sent and summed in bfloat16 or wider, within the bound.
No kernel may reach another device: no remote copies, remote signals or barrier semaphores. Data moves between devices by JAX's collectives and lax.ppermute only.
A program may use at most 64 MiB of HBM per device.

v0:
```python
import jax
import jax.numpy as jnp
from jax import lax
from jax.sharding import PartitionSpec as P

GROUPS = 16


def shards(activations, out_grads, proj_in, proj_out, store, ckpt_rate, store_group):
    rank = proj_in.shape[1]
    seq_len = activations.shape[2]
    ex_local = activations.shape[1]
    scale = 1.0 / jnp.sqrt(jnp.float32(seq_len))
    part_in = jnp.einsum("cesf,fr->cesr", activations, proj_in, preferred_element_type=jnp.float32)
    part_out = jnp.einsum("cesf,fr->cesr", out_grads, proj_out, preferred_element_type=jnp.float32)
    stacked = jnp.concatenate([part_in, part_out], axis=3)
    summed = lax.psum(stacked, "mp")
    low_in = summed[..., :rank].astype(jnp.bfloat16)
    low_grad = summed[..., rank:].astype(jnp.bfloat16)
    outer = jnp.einsum("cesa,cesb->ecab", low_in, low_grad, preferred_element_type=jnp.float32)
    query = (outer.reshape(ex_local, 2, rank * rank) * scale).astype(jnp.bfloat16)
    piece = lax.all_gather(query, "dp", axis=0, tiled=True)
    first = jnp.einsum("qk,rk->qr", piece[:, 0], store[0], preferred_element_type=jnp.float32)
    second = jnp.einsum("qk,rk->qr", piece[:, 1], store[1], preferred_element_type=jnp.float32)
    scores = ckpt_rate[0] * first + ckpt_rate[1] * second
    member = (store_group[:, None] == jnp.arange(GROUPS, dtype=jnp.int32)[None, :]).astype(
        jnp.float32
    )
    partial_totals = jnp.dot(scores, member, precision=lax.Precision.HIGHEST)
    totals = lax.psum(partial_totals, ("dp", "mp"))
    store_rows = store.shape[1] * lax.axis_size("dp") * lax.axis_size("mp")
    group_scores = totals / jnp.sqrt(jnp.float32(store_rows) / jnp.float32(GROUPS))
    return (scores, group_scores)


def solution(mesh):
    placed = (
        P(None, "dp", None, "mp"),
        P(None, "dp", None, "mp"),
        P("mp", None),
        P("mp", None),
        P(None, ("dp", "mp"), None),
        P(),
        P(("dp", "mp")),
    )
    return jax.shard_map(
        shards, mesh=mesh, in_specs=placed, out_specs=(P(None, ("dp", "mp")), P()), check_vma=False
    )
```

profile of v0, /device:TPU:24, one launch (start us, length us, event | category | flops | bytes accessed | tf_op | source)
XLA Modules:
  0.0 201.5 jit_solution(9762679956642732704)
XLA Ops:
  7.2 0.0 copy-start
  7.2 0.0 copy-start.1
  7.2 0.0 all-gather.2.cloned.1.call-start
  7.2 4.4 %fusion.16 = f32[2,2,384,64]{2,3,1,0:T(8,128)S(1)} fusion(bf16[2,2,384,1792]{3,2,1,0:T(8,128)(2,1)} %param.7, bf16[1792,64]{0,1:T(8,128)(2,1)} %param.9), kind=kOutput, calls=%fused_computation.14 | convolution fusion | flops 352321536 | bytes 6127616 | tf_op jit(solution)/shard_map/cesf,fr->cesr/dot_general | solution.py:14
  11.7 0.0 copy-done
  11.7 0.0 copy-done.1
  11.7 0.0 copy-start.3
  11.7 0.6 fusion.21
  12.3 0.1 pad_maximum_fusion
  12.4 47.2 %all-reduce.1 = bf16[2,2,384,128]{2,3,1,0:T(8,128)(2,1)S(1)} all-reduce(f32[2,2,384,128]{2,3,1,0:T(8,128)S(1)} %pad_maximum_fusion), channel_id=1, replica_groups=mesh['dp'=32,'mp'=8] {'mp'}, use_global_device_ids=true, to_apply=%region_0.0 | all-reduce | flops 196608 | bytes 1179648 | tf_op jit(solution)/shard_map/psum | solution.py:17
  59.6 0.2 fusion.6
  59.8 0.7 convert_element_type.10
  60.6 0.0 all-gather.2.cloned.1.call-update
  60.6 0.0 copy-done.3
  60.6 0.6 fusion.26
  61.2 50.5 %all-gather.2.cloned.1.call-done = bf16[64,2,4096]{2,1,0:T(2,128)(2,1)} async-done(((bf16[2,2,4096]{2,1,0:T(2,128)(2,1)}), bf16[64,2,4096]{2,1,0:T(2,128)(2,1)}) %all-gather.2.cloned.1.call-update) | async-done | bytes 1048592 | tf_op jit(solution)/shard_map/all_gather | solution.py:22
  111.7 3.7 %fusion.24 = (bf16[64,1,4096]{2,1,0:T(2,128)(2,1)S(1)}, bf16[64,1,4096]{2,1,0:T(2,128)(2,1)S(1)}) fusion(bf16[64,2,4096]{2,1,0:T(2,128)(2,1)} %all-gather.2.cloned.1.call-done), kind=kLoop, calls=%fused_computation.24 | loop fusion | bytes 2097152 | tf_op jit(solution)/shard_map/slice | solution.py:23
  115.4 0.0 copy-done.5
  115.4 1.6 fusion.13
  117.0 1.6 fusion.10
  118.6 0.0 copy-start.2
  118.6 0.3 fusion.20
  118.9 75.1 %psum.15 = f32[64,16]{0,1:T(8,128)S(1)} all-reduce(f32[64,16]{0,1:T(8,128)S(1)} %fusion.20), channel_id=1, replica_groups=mesh['dp'=32,'mp'=8] {'dp','mp'}, use_global_device_ids=true, to_apply=%region_1.0 | all-reduce | flops 1024 | bytes 8192 | tf_op jit(solution)/shard_map/psum | solution.py:30
  194.0 0.6 broadcast_multiply_fusion
  (5 shorter events, 0.0 us)
Async XLA Ops:
  7.2 4.5 %copy-start = (bf16[2,2,384,512]{3,2,1,0:T(8,128)(2,1)S(1)}, bf16[2,2,384,512]{3,2,1,0:T(8,128)(2,1)}, u32[]{:S(2)}) copy-start(bf16[2,2,384,512]{3,2,1,0:T(8,128)(2,1)} %param.8) | copy-start | bytes 4718596
  7.2 4.5 %copy-start.1 = (bf16[512,64]{0,1:T(8,128)(2,1)S(1)}, bf16[512,64]{0,1:T(8,128)(2,1)}, u32[]{:S(2)}) copy-start(bf16[512,64]{0,1:T(8,128)(2,1)} %param.10) | copy-start | bytes 196612
  7.2 104.5 %all-gather.2.cloned.1.call-start = ((), (), s32[]{:S(2)}) async-start(), calls=%async_computation | async-start | bytes 1081344 | tf_op jit(solution)/shard_map/all_gather | solution.py:22
  11.7 48.9 %copy-start.3 = (f32[2]{0:T(128)S(1)}, f32[2]{0:T(128)}, u32[]{:S(2)}) copy-start(f32[2]{0:T(128)} %param.12) | copy-start | bytes 28
  61.2 57.4 %copy-start.4 = (s32[256]{0:T(256)S(1)}, s32[256]{0:T(256)}, u32[]{:S(2)}) copy-start(s32[256]{0:T(256)} %param.13) | copy-start | bytes 3076
  111.7 3.7 %copy-start.5 = (bf16[2,256,4096]{2,1,0:T(8,128)(2,1)S(1)}, bf16[2,256,4096]{2,1,0:T(8,128)(2,1)}, u32[]{:S(2)}) copy-start(bf16[2,256,4096]{2,1,0:T(8,128)(2,1)} %param.11) | copy-start | bytes 12582916
  118.6 76.0 %copy-start.2 = (f32[64,256]{1,0:T(8,128)}, f32[64,256]{1,0:T(8,128)S(1)}, u32[]{:S(2)}) copy-start(f32[64,256]{1,0:T(8,128)S(1)} %fusion.10) | copy-start | bytes 196612
Sparse Core Ops, SparseCore 0:
  60.7 50.9 all-gather.1
where the time goes:
time: 204 us; the launch traced here: 201 us
  blocking collectives  122 us (60%)
  waiting for transfers between devices  50.5 us (25%)
  between operations  14.2 us (7%)
  matrix products  8.67 us (4%)
  local copies, waits for them, and re-layouts  5.12 us (3%)
    psum x1, blocking collectives, shards(): totals = lax.psum(partial_totals, ('dp', 'mp'))  75.1 us
    all_gather x1, waiting for transfers between devices, shards(): piece = lax.all_gather(query, 'dp', axis=0, tiled=True)  50.5 us
    psum x1, blocking collectives, shards(): summed = lax.psum(stacked, 'mp')  47.2 us
    dot_general x1, matrix products, shards(): jnp.einsum('cesf,fr->cesr', activations, proj_in, preferred_element_type=...  4.43 us
  transfers between devices with their start and end apart: 1, of which 1 were waited for; matrix products, arithmetic and copies ran while one was open for 0% of the time, Pallas kernels for 0%

commit v1 on v0

--- a/solution.py
+++ b/solution.py
@@ -6,20 +6,66 @@
 GROUPS = 16
 
 
+def _bits(n):
+    return n.bit_length() - 1
+
+
+def _swap(axis, n, bit):
+    return [(i, i ^ (1 << bit)) for i in range(n)]
+
+
+def _halving_sum(x, axis, n, dim):
+    me = lax.axis_index(axis)
+    for bit in reversed(range(_bits(n))):
+        half = x.shape[dim] // 2
+        upper = (me >> bit) & 1
+        keep = lax.dynamic_slice_in_dim(x, upper * half, half, axis=dim)
+        send = lax.dynamic_slice_in_dim(x, (1 - upper) * half, half, axis=dim)
+        x = keep + lax.ppermute(send, axis, _swap(axis, n, bit))
+    return x
+
+
+def _doubling_gather(x, steps):
+    for axis, n, bit in steps:
+        upper = ((lax.axis_index(axis) >> bit) & 1) == 1
+        other = lax.ppermute(x, axis, _swap(axis, n, bit))
+        x = jnp.where(upper, jnp.stack([other, x]), jnp.stack([x, other]))
+    return x
+
+
+def _butterfly_sum(x, steps):
+    for axis, n, bit in steps:
+        x = x + lax.ppermute(x, axis, _swap(axis, n, bit))
+    return x
+
+
 def shards(activations, out_grads, proj_in, proj_out, store, ckpt_rate, store_group):
+    n_dp = lax.axis_size("dp")
+    n_mp = lax.axis_size("mp")
     rank = proj_in.shape[1]
     seq_len = activations.shape[2]
     ex_local = activations.shape[1]
-    scale = 1.0 / jnp.sqrt(jnp.float32(seq_len))
     part_in = jnp.einsum("cesf,fr->cesr", activations, proj_in, preferred_element_type=jnp.float32)
     part_out = jnp.einsum("cesf,fr->cesr", out_grads, proj_out, preferred_element_type=jnp.float32)
     stacked = jnp.concatenate([part_in, part_out], axis=3)
-    summed = lax.psum(stacked, "mp")
+    summed = _halving_sum(stacked, "mp", n_mp, 2)
     low_in = summed[..., :rank].astype(jnp.bfloat16)
     low_grad = summed[..., rank:].astype(jnp.bfloat16)
     outer = jnp.einsum("cesa,cesb->ecab", low_in, low_grad, preferred_element_type=jnp.float32)
-    query = (outer.reshape(ex_local, 2, rank * rank) * scale).astype(jnp.bfloat16)
-    piece = lax.all_gather(query, "dp", axis=0, tiled=True)
+    outer = outer.reshape(ex_local, 2, rank * rank)
+    outer = _halving_sum(outer, "mp", n_mp, 2)
+    query = (outer / jnp.sqrt(jnp.float32(seq_len))).astype(jnp.bfloat16)
+    dp_bits, mp_bits = _bits(n_dp), _bits(n_mp)
+    order = [("dp", n_dp, b) for b in reversed(range(1, dp_bits))]
+    order += [("mp", n_mp, b) for b in reversed(range(mp_bits))]
+    order += [("dp", n_dp, 0)]
+    gathered = _doubling_gather(query, order)
+    steps = len(order)
+    lead = {(a, b): steps - 1 - i for i, (a, _, b) in enumerate(order)}
+    dp_axes = [lead[("dp", b)] for b in reversed(range(dp_bits))]
+    mp_axes = [lead[("mp", b)] for b in reversed(range(mp_bits))]
+    perm = dp_axes + [steps] + [steps + 1] + mp_axes + [steps + 2]
+    piece = jnp.transpose(gathered, perm).reshape(n_dp * ex_local, 2, rank * rank)
     first = jnp.einsum("qk,rk->qr", piece[:, 0], store[0], preferred_element_type=jnp.float32)
     second = jnp.einsum("qk,rk->qr", piece[:, 1], store[1], preferred_element_type=jnp.float32)
     scores = ckpt_rate[0] * first + ckpt_rate[1] * second
@@ -27,8 +73,9 @@
         jnp.float32
     )
     partial_totals = jnp.dot(scores, member, precision=lax.Precision.HIGHEST)
-    totals = lax.psum(partial_totals, ("dp", "mp"))
-    store_rows = store.shape[1] * lax.axis_size("dp") * lax.axis_size("mp")
+    reduce_order = [("mp", n_mp, b) for b in range(mp_bits)] + [("dp", n_dp, b) for b in range(dp_bits)]
+    totals = _butterfly_sum(partial_totals, reduce_order)
+    store_rows = store.shape[1] * n_dp * n_mp
     group_scores = totals / jnp.sqrt(jnp.float32(store_rows) / jnp.float32(GROUPS))
     return (scores, group_scores)
 

time: 204 us -> 140 us (0.69)
  blocking collectives: 122 us -> 0 us
  starting transfers between devices: 0.04 us -> 46.5 us
  waiting for transfers between devices: 50.5 us -> 69.6 us
  between operations: 14.2 us -> 0.95 us
  other arithmetic: 0.66 us -> 6.77 us
  matrix products: 8.67 us -> 11.8 us
    psum x2 -> x0, blocking collectives: 122 us -> none  [the longest x1 75.1 us: shards(): totals = lax.psum(partial_totals, ('dp', 'mp'))]
    ppermute x0 -> x22, waiting for transfers between devices: none -> 69.6 us  [the longest x6 28.9 us: _halving_sum(): x = keep + lax.ppermute(send, axis, _swap(axis, n, bit))]
    all_gather x1 -> x0, waiting for transfers between devices: 50.5 us -> none  [shards(): piece = lax.all_gather(query, 'dp', axis=0, tiled=True)]
    ppermute x0 -> x22, starting transfers between devices: none -> 46.5 us  [the longest x8 17.6 us: _doubling_gather(): other = lax.ppermute(x, axis, _swap(axis, n, bit))]
    slice x1 -> x0, local copies, waits for them, and re-layouts: 3.7 us -> none  [shards(): piece[:, 0]]
    select_n x0 -> x14, other arithmetic: none -> 3.05 us  [_doubling_gather(): x = jnp.where(upper, jnp.stack([other, x]), jnp.stack([x, other]))]
  transfers between devices with their start and end apart: 1 -> 22, of which waited for: 1 -> 22; matrix products, arithmetic and copies ran while one was open for 0% -> 2% of each run, Pallas kernels for 0% -> 0%
where the time goes in v1:
time: 140 us; the launch traced here: 139 us
  waiting for transfers between devices  69.6 us (50%)
  starting transfers between devices  46.5 us (33%)
  matrix products  11.8 us (8%)
  other arithmetic  6.77 us (5%)
  local copies, waits for them, and re-layouts  3.77 us (3%)
    ppermute x6, waiting for transfers between devices, _halving_sum(): x = keep + lax.ppermute(send, axis, _swap(axis, n, bit))  28.9 us
    ppermute x8, waiting for transfers between devices, _doubling_gather(): other = lax.ppermute(x, axis, _swap(axis, n, bit))  21.7 us
    ppermute x8, waiting for transfers between devices, _butterfly_sum(): x = x + lax.ppermute(x, axis, _swap(axis, n, bit))  19 us
    ppermute x8, starting transfers between devices, _doubling_gather(): other = lax.ppermute(x, axis, _swap(axis, n, bit))  17.6 us
    ppermute x8, starting transfers between devices, _butterfly_sum(): x = x + lax.ppermute(x, axis, _swap(axis, n, bit))  15.6 us
    ppermute x6, starting transfers between devices, _halving_sum(): x = keep + lax.ppermute(send, axis, _swap(axis, n, bit))  13.3 us
    dot_general x1, matrix products, shards(): jnp.einsum('cesf,fr->cesr', activations, proj_in, preferred_element_type=...  4.44 us
    dot_general x1, matrix products, shards(): jnp.einsum('qk,rk->qr', piece[:, 0], store[0], preferred_element_type=jnp...  3.18 us
  transfers between devices with their start and end apart: 22, of which 22 were waited for; matrix products, arithmetic and copies ran while one was open for 2% of the time, Pallas kernels for 0%

profile of v1, /device:TPU:24, one launch (start us, length us, event | category | flops | bytes accessed | tf_op | source)
XLA Modules:
  0.0 139.4 jit_solution(9599300305977847405)
XLA Ops:
  0.7 4.4 %fusion.19 = f32[2,2,384,64]{2,3,1,0:T(8,128)S(1)} fusion(bf16[2,2,384,1792]{3,2,1,0:T(8,128)(2,1)} %param.7, bf16[1792,64]{0,1:T(8,128)(2,1)} %param.9), kind=kOutput, calls=%fused_computation.28 | convolution fusion | flops 352321536 | bytes 6127616 | tf_op jit(solution)/shard_map/cesf,fr->cesr/dot_general | solution.py:48
  6.0 3.1 %collective-permute-start = (f32[2,2,192,128]{2,3,1,0:T(8,128)S(1)}, f32[2,2,192,128]{2,3,1,0:T(8,128)S(1)}, u32[]{:S(2)}, u32[]{:S(2)}) collective-permute-start(f32[2,2,192,128]{2,3,1,0:T(8,128)S(1)} %fusion.16), channel_id=1, source_target_pairs={{0,4},{1,5},{2,6},{3,7},{4,0},{5,1},{6,2},{7,3},{8,12},{9,13},{10,... | collective-permute-start | bytes 1179656 | tf_op jit(solution)/shard_map/ppermute | solution.py:24
  9.1 12.1 %collective-permute-done = f32[2,2,192,128]{2,3,1,0:T(8,128)S(1)} collective-permute-done((f32[2,2,192,128]{2,3,1,0:T(8,128)S(1)}, f32[2,2,192,128]{2,3,1,0:T(8,128)S(1)}, u32[]{:S(2)}, u32[]{:S(2)}) %collective-permute-start) | collective-permute-done | bytes 393248 | tf_op jit(solution)/shard_map/ppermute | solution.py:24
  23.2 5.7 %collective-permute-done.1 = f32[2,2,96,128]{2,3,1,0:T(8,128)S(1)} collective-permute-done((f32[2,2,96,128]{2,3,1,0:T(8,128)S(1)}, f32[2,2,96,128]{2,3,1,0:T(8,128)S(1)}, u32[]{:S(2)}, u32[]{:S(2)}) %collective-permute-start.1) | collective-permute-done | bytes 196640 | tf_op jit(solution)/shard_map/ppermute | solution.py:24
  31.2 4.6 %collective-permute-done.2 = f32[2,2,48,128]{2,3,1,0:T(8,128)S(1)} collective-permute-done((f32[2,2,48,128]{2,3,1,0:T(8,128)S(1)}, f32[2,2,48,128]{2,3,1,0:T(8,128)S(1)}, u32[]{:S(2)}, u32[]{:S(2)}) %collective-permute-start.2) | collective-permute-done | bytes 98336 | tf_op jit(solution)/shard_map/ppermute | solution.py:24
  36.2 3.1 %collective-permute-start.3 = (f32[2,2,2048]{2,1,0:T(2,128)S(1)}, f32[2,2,2048]{2,1,0:T(2,128)S(1)}, u32[]{:S(2)}, u32[]{:S(2)}) collective-permute-start(f32[2,2,2048]{2,1,0:T(2,128)S(1)} %constant_dynamic-slice_fusion.2), channel_id=1, source_target_pairs={{0,4},{1,5},{2,6},{3,7},{4,0},{5,1},{6,2},{7,3},{8,12},{9,13},{10,... | collective-permute-start | bytes 98312 | tf_op jit(solution)/shard_map/ppermute | solution.py:24
  39.3 2.4 %collective-permute-done.3 = f32[2,2,2048]{2,1,0:T(2,128)S(1)} collective-permute-done((f32[2,2,2048]{2,1,0:T(2,128)S(1)}, f32[2,2,2048]{2,1,0:T(2,128)S(1)}, u32[]{:S(2)}, u32[]{:S(2)}) %collective-permute-start.3) | collective-permute-done | bytes 32800 | tf_op jit(solution)/shard_map/ppermute | solution.py:24
  49.4 7.1 %collective-permute-start.6 = (bf16[2,2,512]{2,1,0:T(2,128)(2,1)S(1)}, bf16[2,2,512]{2,1,0:T(2,128)(2,1)S(1)}, u32[]{:S(2)}, u32[]{:S(2)}) collective-permute-start(bf16[2,2,512]{2,1,0:T(2,128)(2,1)S(1)} %multiply_convert_fusion), channel_id=1, source_target_pairs={{0,128},{8,136},{16,144},{24,152},{32,160},{40,168},{48,176},{56,1... | collective-permute-start | bytes 12296 | tf_op jit(solution)/shard_map/ppermute | solution.py:31
  58.1 2.2 %collective-permute-start.7 = (bf16[2,2,2,512]{3,2,1,0:T(2,128)(2,1)S(1)}, bf16[2,2,2,512]{3,2,1,0:T(2,128)(2,1)S(1)}, u32[]{:S(2)}, u32[]{:S(2)}) collective-permute-start(bf16[2,2,2,512]{3,2,1,0:T(2,128)(2,1)S(1)} %broadcast_select_fusion.14), channel_id=1, source_target_pairs={{0,64},{8,72},{16,80},{24,88},{32,96},{40,104},{48,112},{56,120},{... | collective-permute-start | bytes 24584 | tf_op jit(solution)/shard_map/ppermute | solution.py:31
  60.4 2.4 %collective-permute-done.7 = bf16[2,2,2,512]{3,2,1,0:T(2,128)(2,1)S(1)} collective-permute-done((bf16[2,2,2,512]{3,2,1,0:T(2,128)(2,1)S(1)}, bf16[2,2,2,512]{3,2,1,0:T(2,128)(2,1)S(1)}, u32[]{:S(2)}, u32[]{:S(2)}) %collective-permute-start.7) | collective-permute-done | bytes 8224 | tf_op jit(solution)/shard_map/ppermute | solution.py:31
  64.2 3.9 %collective-permute-done.8 = bf16[2,2,2,2,512]{4,3,2,1,0:T(2,128)(2,1)S(1)} collective-permute-done((bf16[2,2,2,2,512]{4,3,2,1,0:T(2,128)(2,1)S(1)}, bf16[2,2,2,2,512]{4,3,2,1,0:T(2,128)(2,1)S(1)}, u32[]{:S(2)}, u32[]{:S(2)}) %collective-permute-start.8) | collective-permute-done | bytes 16416 | tf_op jit(solution)/shard_map/ppermute | solution.py:31
  69.1 3.1 %collective-permute-done.9 = bf16[2,2,2,2,2,512]{5,4,3,2,1,0:T(2,128)(2,1)S(1)} collective-permute-done((bf16[2,2,2,2,2,512]{5,4,3,2,1,0:T(2,128)(2,1)S(1)}, bf16[2,2,2,2,2,512]{5,4,3,2,1,0:T(2,128)(2,1)S(1)}, u32[]{:S(2)}, u32[]{:S(2)}) %collective-permute-start.9) | collective-permute-done | bytes 32800 | tf_op jit(solution)/shard_map/ppermute | solution.py:31
  72.3 3.1 %collective-permute-start.10 = (bf16[2,2,2,2,2,2,512]{6,5,4,3,2,1,0:T(2,128)(2,1)S(1)}, bf16[2,2,2,2,2,2,512]{6,5,4,3,2,1,0:T(2,128)(2,1)S(1)}, u32[]{:S(2)}, u32[]{:S(2)}) collective-permute-start(bf16[2,2,2,2,2,2,512]{6,5,4,3,2,1,0:T(2,128)(2,1)S(1)} %broadcast_select_fusion.8), channel_id=1, source_target_pairs={{0,4},{1,5},{2,6},{3,7},{4,0},{5,1},{6,2},{7,3},{8,12},{9,13},{10,... | collective-permute-start | bytes 196616 | tf_op jit(solution)/shard_map/ppermute | solution.py:31
  75.5 2.6 %collective-permute-done.10 = bf16[2,2,2,2,2,2,512]{6,5,4,3,2,1,0:T(2,128)(2,1)S(1)} collective-permute-done((bf16[2,2,2,2,2,2,512]{6,5,4,3,2,1,0:T(2,128)(2,1)S(1)}, bf16[2,2,2,2,2,2,512]{6,5,4,3,2,1,0:T(2,128)(2,1)S(1)}, u32[]{:S(2)}, u32[]{:S(2)}) %collective-permute-start.10) | collective-permute-done | bytes 65568 | tf_op jit(solution)/shard_map/ppermute | solution.py:31
  80.2 3.2 %collective-permute-done.11 = bf16[2,2,2,2,2,2,2,512]{7,6,5,4,3,2,1,0:T(2,128)(2,1)S(1)} collective-permute-done((bf16[2,2,2,2,2,2,2,512]{7,6,5,4,3,2,1,0:T(2,128)(2,1)S(1)}, bf16[2,2,2,2,2,2,2,512]{7,6,5,4,3,2,1,0:T(2,128)(2,1)S(1)}, u32[]{:S(2)}, u32[]{:S(2)}) %collective-permute-start.11) | collective-permute-done | bytes 131104 | tf_op jit(solution)/shard_map/ppermute | solution.py:31
  85.6 4.8 %collective-permute-done.12 = bf16[2,2,2,2,2,2,2,2,512]{8,7,6,5,4,3,2,1,0:T(2,128)(2,1)S(1)} collective-permute-done((bf16[2,2,2,2,2,2,2,2,512]{8,7,6,5,4,3,2,1,0:T(2,128)(2,1)S(1)}, bf16[2,2,2,2,2,2,2,2,512]{8,7,6,5,4,3,2,1,0:T(2,128)(2,1)S(1)}, u32[]{:S(2)}, u32[]{:S(2)}) %collective-permute-start.12) | collective-permute-done | bytes 262176 | tf_op jit(solution)/shard_map/ppermute | solution.py:31
  97.5 3.2 %fusion.12 = f32[64,256]{1,0:T(8,128)S(1)} fusion(bf16[2,256,4096]{2,1,0:T(8,128)(2,1)} %param.11, bf16[64,2,4096]{2,0,1:T(8,128)(2,1)} %reshape.773, f32[]{:T(128)} %bitcast.31), kind=kOutput, calls=%fused_computation.9 | convolution fusion | flops 134234112 | bytes 2687488 | tf_op jit(solution)/shard_map/qk,rk->qr/dot_general | solution.py:70
  100.7 3.2 %fusion.9 = f32[64,256]{1,0:T(8,128)S(1)} fusion(f32[64,256]{1,0:T(8,128)S(1)} %fusion.12, bf16[2,256,4096]{2,1,0:T(8,128)(2,1)} %param.11, bf16[64,2,4096]{2,0,1:T(8,128)(2,1)} %reshape.773, f32[]{:T(128)} %bitcast), kind=kOutput, calls=%fused_computation.8 | convolution fusion | flops 134250496 | bytes 2753024 | tf_op jit(solution)/shard_map/qk,rk->qr/dot_general | solution.py:69
  105.2 2.6 %collective-permute-done.14 = f32[64,16]{0,1:T(8,128)S(1)} collective-permute-done((f32[64,16]{0,1:T(8,128)S(1)}, f32[64,16]{0,1:T(8,128)S(1)}, u32[]{:S(2)}, u32[]{:S(2)}) %collective-permute-start.14) | collective-permute-done | bytes 4128 | tf_op jit(solution)/shard_map/ppermute | solution.py:38
  111.5 3.0 %collective-permute-start.16 = (f32[64,16]{0,1:T(8,128)S(1)}, f32[64,16]{0,1:T(8,128)S(1)}, u32[]{:S(2)}, u32[]{:S(2)}) collective-permute-start(f32[64,16]{0,1:T(8,128)S(1)} %add.101), channel_id=1, source_target_pairs={{0,4},{1,5},{2,6},{3,7},{4,0},{5,1},{6,2},{7,3},{8,12},{9,13},{10,... | collective-permute-start | bytes 12296 | tf_op jit(solution)/shard_map/ppermute | solution.py:38
  118.6 2.9 %collective-permute-done.18 = f32[64,16]{0,1:T(8,128)S(1)} collective-permute-done((f32[64,16]{0,1:T(8,128)S(1)}, f32[64,16]{0,1:T(8,128)S(1)}, u32[]{:S(2)}, u32[]{:S(2)}) %collective-permute-start.18) | collective-permute-done | bytes 4128 | tf_op jit(solution)/shard_map/ppermute | solution.py:38
  122.7 3.9 %collective-permute-done.19 = f32[64,16]{0,1:T(8,128)S(1)} collective-permute-done((f32[64,16]{0,1:T(8,128)S(1)}, f32[64,16]{0,1:T(8,128)S(1)}, u32[]{:S(2)}, u32[]{:S(2)}) %collective-permute-start.19) | collective-permute-done | bytes 4128 | tf_op jit(solution)/shard_map/ppermute | solution.py:38
  128.8 2.4 %collective-permute-done.20 = f32[64,16]{0,1:T(8,128)S(1)} collective-permute-done((f32[64,16]{0,1:T(8,128)S(1)}, f32[64,16]{0,1:T(8,128)S(1)}, u32[]{:S(2)}, u32[]{:S(2)}) %collective-permute-start.20) | collective-permute-done | bytes 4128 | tf_op jit(solution)/shard_map/ppermute | solution.py:38
  131.2 5.9 %collective-permute-start.21 = (f32[64,16]{0,1:T(8,128)S(1)}, f32[64,16]{0,1:T(8,128)S(1)}, u32[]{:S(2)}, u32[]{:S(2)}) collective-permute-start(f32[64,16]{0,1:T(8,128)S(1)} %add.106), channel_id=1, source_target_pairs={{0,128},{8,136},{16,144},{24,152},{32,160},{40,168},{48,176},{56,1... | collective-permute-start | bytes 12296 | tf_op jit(solution)/shard_map/ppermute | solution.py:38
  (82 shorter events, 43.3 us)
Async XLA Ops:
  6.0 15.3 %collective-permute-start = (f32[2,2,192,128]{2,3,1,0:T(8,128)S(1)}, f32[2,2,192,128]{2,3,1,0:T(8,128)S(1)}, u32[]{:S(2)}, u32[]{:S(2)}) collective-permute-start(f32[2,2,192,128]{2,3,1,0:T(8,128)S(1)} %fusion.16), channel_id=1, source_target_pairs={{0,4},{1,5},{2,6},{3,7},{4,0},{5,1},{6,2},{7,3},{8,12},{9,13},{10,... | collective-permute-start | bytes 1179656 | tf_op jit(solution)/shard_map/ppermute | solution.py:24
  9.1 82.2 %copy-start.3 = (f32[2]{0:T(128)S(1)}, f32[2]{0:T(128)}, u32[]{:S(2)}) copy-start(f32[2]{0:T(128)} %param.12) | copy-start | bytes 28
  21.6 7.3 %collective-permute-start.1 = (f32[2,2,96,128]{2,3,1,0:T(8,128)S(1)}, f32[2,2,96,128]{2,3,1,0:T(8,128)S(1)}, u32[]{:S(2)}, u32[]{:S(2)}) collective-permute-start(f32[2,2,96,128]{2,3,1,0:T(8,128)S(1)} %constant_dynamic-slice_fusion.4), channel_id=1, source_target_pairs={{0,2},{1,3},{2,0},{3,1},{4,6},{5,7},{6,4},{7,5},{8,10},{9,11},{10,... | collective-permute-start | bytes 589832 | tf_op jit(solution)/shard_map/ppermute | solution.py:24
  29.2 6.6 %collective-permute-start.2 = (f32[2,2,48,128]{2,3,1,0:T(8,128)S(1)}, f32[2,2,48,128]{2,3,1,0:T(8,128)S(1)}, u32[]{:S(2)}, u32[]{:S(2)}) collective-permute-start(f32[2,2,48,128]{2,3,1,0:T(8,128)S(1)} %constant_dynamic-slice_fusion.3), channel_id=1, source_target_pairs={{0,1},{1,0},{2,3},{3,2},{4,5},{5,4},{6,7},{7,6},{8,9},{9,8},{10,11... | collective-permute-start | bytes 294920 | tf_op jit(solution)/shard_map/ppermute | solution.py:24
  36.2 5.5 %collective-permute-start.3 = (f32[2,2,2048]{2,1,0:T(2,128)S(1)}, f32[2,2,2048]{2,1,0:T(2,128)S(1)}, u32[]{:S(2)}, u32[]{:S(2)}) collective-permute-start(f32[2,2,2048]{2,1,0:T(2,128)S(1)} %constant_dynamic-slice_fusion.2), channel_id=1, source_target_pairs={{0,4},{1,5},{2,6},{3,7},{4,0},{5,1},{6,2},{7,3},{8,12},{9,13},{10,... | collective-permute-start | bytes 98312 | tf_op jit(solution)/shard_map/ppermute | solution.py:24
  41.8 3.8 %collective-permute-start.4 = (f32[2,2,1024]{2,1,0:T(2,128)S(1)}, f32[2,2,1024]{2,1,0:T(2,128)S(1)}, u32[]{:S(2)}, u32[]{:S(2)}) collective-permute-start(f32[2,2,1024]{2,1,0:T(2,128)S(1)} %constant_dynamic-slice_fusion.1), channel_id=1, source_target_pairs={{0,2},{1,3},{2,0},{3,1},{4,6},{5,7},{6,4},{7,5},{8,10},{9,11},{10,... | collective-permute-start | bytes 49160 | tf_op jit(solution)/shard_map/ppermute | solution.py:24
  45.6 3.7 %collective-permute-start.5 = (f32[2,2,512]{2,1,0:T(2,128)S(1)}, f32[2,2,512]{2,1,0:T(2,128)S(1)}, u32[]{:S(2)}, u32[]{:S(2)}) collective-permute-start(f32[2,2,512]{2,1,0:T(2,128)S(1)} %constant_dynamic-slice_fusion), channel_id=1, source_target_pairs={{0,1},{1,0},{2,3},{3,2},{4,5},{5,4},{6,7},{7,6},{8,9},{9,8},{10,11... | collective-permute-start | bytes 24584 | tf_op jit(solution)/shard_map/ppermute | solution.py:24
  49.4 8.7 %collective-permute-start.6 = (bf16[2,2,512]{2,1,0:T(2,128)(2,1)S(1)}, bf16[2,2,512]{2,1,0:T(2,128)(2,1)S(1)}, u32[]{:S(2)}, u32[]{:S(2)}) collective-permute-start(bf16[2,2,512]{2,1,0:T(2,128)(2,1)S(1)} %multiply_convert_fusion), channel_id=1, source_target_pairs={{0,128},{8,136},{16,144},{24,152},{32,160},{40,168},{48,176},{56,1... | collective-permute-start | bytes 12296 | tf_op jit(solution)/shard_map/ppermute | solution.py:31
  58.1 4.6 %collective-permute-start.7 = (bf16[2,2,2,512]{3,2,1,0:T(2,128)(2,1)S(1)}, bf16[2,2,2,512]{3,2,1,0:T(2,128)(2,1)S(1)}, u32[]{:S(2)}, u32[]{:S(2)}) collective-permute-start(bf16[2,2,2,512]{3,2,1,0:T(2,128)(2,1)S(1)} %broadcast_select_fusion.14), channel_id=1, source_target_pairs={{0,64},{8,72},{16,80},{24,88},{32,96},{40,104},{48,112},{56,120},{... | collective-permute-start | bytes 24584 | tf_op jit(solution)/shard_map/ppermute | solution.py:31
  62.8 5.3 %collective-permute-start.8 = (bf16[2,2,2,2,512]{4,3,2,1,0:T(2,128)(2,1)S(1)}, bf16[2,2,2,2,512]{4,3,2,1,0:T(2,128)(2,1)S(1)}, u32[]{:S(2)}, u32[]{:S(2)}) collective-permute-start(bf16[2,2,2,2,512]{4,3,2,1,0:T(2,128)(2,1)S(1)} %broadcast_select_fusion.12), channel_id=1, source_target_pairs={{0,32},{8,40},{16,48},{24,56},{32,0},{40,8},{48,16},{56,24},{64,96... | collective-permute-start | bytes 49160 | tf_op jit(solution)/shard_map/ppermute | solution.py:31
  68.2 4.0 %collective-permute-start.9 = (bf16[2,2,2,2,2,512]{5,4,3,2,1,0:T(2,128)(2,1)S(1)}, bf16[2,2,2,2,2,512]{5,4,3,2,1,0:T(2,128)(2,1)S(1)}, u32[]{:S(2)}, u32[]{:S(2)}) collective-permute-start(bf16[2,2,2,2,2,512]{5,4,3,2,1,0:T(2,128)(2,1)S(1)} %broadcast_select_fusion.10), channel_id=1, source_target_pairs={{0,16},{8,24},{16,0},{24,8},{32,48},{40,56},{48,32},{56,40},{64,80... | collective-permute-start | bytes 98312 | tf_op jit(solution)/shard_map/ppermute | solution.py:31
  72.3 5.9 %collective-permute-start.10 = (bf16[2,2,2,2,2,2,512]{6,5,4,3,2,1,0:T(2,128)(2,1)S(1)}, bf16[2,2,2,2,2,2,512]{6,5,4,3,2,1,0:T(2,128)(2,1)S(1)}, u32[]{:S(2)}, u32[]{:S(2)}) collective-permute-start(bf16[2,2,2,2,2,2,512]{6,5,4,3,2,1,0:T(2,128)(2,1)S(1)} %broadcast_select_fusion.8), channel_id=1, source_target_pairs={{0,4},{1,5},{2,6},{3,7},{4,0},{5,1},{6,2},{7,3},{8,12},{9,13},{10,... | collective-permute-start | bytes 196616 | tf_op jit(solution)/shard_map/ppermute | solution.py:31
  78.3 5.1 %collective-permute-start.11 = (bf16[2,2,2,2,2,2,2,512]{7,6,5,4,3,2,1,0:T(2,128)(2,1)S(1)}, bf16[2,2,2,2,2,2,2,512]{7,6,5,4,3,2,1,0:T(2,128)(2,1)S(1)}, u32[]{:S(2)}, u32[]{:S(2)}) collective-permute-start(bf16[2,2,2,2,2,2,2,512]{7,6,5,4,3,2,1,0:T(2,128)(2,1)S(1)} %broadcast_select_fusion.6), channel_id=1, source_target_pairs={{0,2},{1,3},{2,0},{3,1},{4,6},{5,7},{6,4},{7,5},{8,10},{9,11},{10,... | collective-permute-start | bytes 393224 | tf_op jit(solution)/shard_map/ppermute | solution.py:31
  83.8 6.6 %collective-permute-start.12 = (bf16[2,2,2,2,2,2,2,2,512]{8,7,6,5,4,3,2,1,0:T(2,128)(2,1)S(1)}, bf16[2,2,2,2,2,2,2,2,512]{8,7,6,5,4,3,2,1,0:T(2,128)(2,1)S(1)}, u32[]{:S(2)}, u32[]{:S(2)}) collective-permute-start(bf16[2,2,2,2,2,2,2,2,512]{8,7,6,5,4,3,2,1,0:T(2,128)(2,1)S(1)} %broadcast_select_fusion.4), channel_id=1, source_target_pairs={{0,1},{1,0},{2,3},{3,2},{4,5},{5,4},{6,7},{7,6},{8,9},{9,8},{10,11... | collective-permute-start | bytes 786440 | tf_op jit(solution)/shard_map/ppermute | solution.py:31
  91.2 2.0 %collective-permute-start.13 = (bf16[2,2,2,2,2,2,2,2,2,512]{9,8,7,6,5,4,3,2,1,0:T(2,128)(2,1)S(1)}, bf16[2,2,2,2,2,2,2,2,2,512]{9,8,7,6,5,4,3,2,1,0:T(2,128)(2,1)S(1)}, u32[]{:S(2)}, u32[]{:S(2)}) collective-permute-start(bf16[2,2,2,2,2,2,2,2,2,512]{9,8,7,6,5,4,3,2,1,0:T(2,128)(2,1)S(1)} %broadcast_select_fus, ...), channel_id=1, source_target_pairs={{0,8},{8,0},{16,24},{24,16},{32,40},{40,32},{48,56},{56,48},{64,72... | collective-permute-start | bytes 1572872 | tf_op jit(solution)/shard_map/ppermute | solution.py:31
  103.8 35.5 %copy-start.2 = (f32[64,256]{1,0:T(8,128)}, f32[64,256]{1,0:T(8,128)S(1)}, u32[]{:S(2)}) copy-start(f32[64,256]{1,0:T(8,128)S(1)} %fusion.9) | copy-start | bytes 196612
  104.2 3.7 %collective-permute-start.14 = (f32[64,16]{0,1:T(8,128)S(1)}, f32[64,16]{0,1:T(8,128)S(1)}, u32[]{:S(2)}, u32[]{:S(2)}) collective-permute-start(f32[64,16]{0,1:T(8,128)S(1)} %fusion.21), channel_id=1, source_target_pairs={{0,1},{1,0},{2,3},{3,2},{4,5},{5,4},{6,7},{7,6},{8,9},{9,8},{10,11... | collective-permute-start | bytes 12296 | tf_op jit(solution)/shard_map/ppermute | solution.py:38
  107.8 3.7 %collective-permute-start.15 = (f32[64,16]{0,1:T(8,128)S(1)}, f32[64,16]{0,1:T(8,128)S(1)}, u32[]{:S(2)}, u32[]{:S(2)}) collective-permute-start(f32[64,16]{0,1:T(8,128)S(1)} %add.100), channel_id=1, source_target_pairs={{0,2},{1,3},{2,0},{3,1},{4,6},{5,7},{6,4},{7,5},{8,10},{9,11},{10,... | collective-permute-start | bytes 12296 | tf_op jit(solution)/shard_map/ppermute | solution.py:38
  111.5 5.2 %collective-permute-start.16 = (f32[64,16]{0,1:T(8,128)S(1)}, f32[64,16]{0,1:T(8,128)S(1)}, u32[]{:S(2)}, u32[]{:S(2)}) collective-permute-start(f32[64,16]{0,1:T(8,128)S(1)} %add.101), channel_id=1, source_target_pairs={{0,4},{1,5},{2,6},{3,7},{4,0},{5,1},{6,2},{7,3},{8,12},{9,13},{10,... | collective-permute-start | bytes 12296 | tf_op jit(solution)/shard_map/ppermute | solution.py:38
  116.7 1.2 collective-permute-start.17
  117.8 3.7 %collective-permute-start.18 = (f32[64,16]{0,1:T(8,128)S(1)}, f32[64,16]{0,1:T(8,128)S(1)}, u32[]{:S(2)}, u32[]{:S(2)}) collective-permute-start(f32[64,16]{0,1:T(8,128)S(1)} %add.103), channel_id=1, source_target_pairs={{0,16},{8,24},{16,0},{24,8},{32,48},{40,56},{48,32},{56,40},{64,80... | collective-permute-start | bytes 12296 | tf_op jit(solution)/shard_map/ppermute | solution.py:38
  121.5 5.2 %collective-permute-start.19 = (f32[64,16]{0,1:T(8,128)S(1)}, f32[64,16]{0,1:T(8,128)S(1)}, u32[]{:S(2)}, u32[]{:S(2)}) collective-permute-start(f32[64,16]{0,1:T(8,128)S(1)} %add.104), channel_id=1, source_target_pairs={{0,32},{8,40},{16,48},{24,56},{32,0},{40,8},{48,16},{56,24},{64,96... | collective-permute-start | bytes 12296 | tf_op jit(solution)/shard_map/ppermute | solution.py:38
  126.6 4.5 %collective-permute-start.20 = (f32[64,16]{0,1:T(8,128)S(1)}, f32[64,16]{0,1:T(8,128)S(1)}, u32[]{:S(2)}, u32[]{:S(2)}) collective-permute-start(f32[64,16]{0,1:T(8,128)S(1)} %add.105), channel_id=1, source_target_pairs={{0,64},{8,72},{16,80},{24,88},{32,96},{40,104},{48,112},{56,120},{... | collective-permute-start | bytes 12296 | tf_op jit(solution)/shard_map/ppermute | solution.py:38
  131.2 7.6 %collective-permute-start.21 = (f32[64,16]{0,1:T(8,128)S(1)}, f32[64,16]{0,1:T(8,128)S(1)}, u32[]{:S(2)}, u32[]{:S(2)}) collective-permute-start(f32[64,16]{0,1:T(8,128)S(1)} %add.106), channel_id=1, source_target_pairs={{0,128},{8,136},{16,144},{24,152},{32,160},{40,168},{48,176},{56,1... | collective-permute-start | bytes 12296 | tf_op jit(solution)/shard_map/ppermute | solution.py:38
  (3 other events, 17.0 us)

commit v2 on v0

v2 whole, which is shorter than its diff:
```python
import jax
import jax.numpy as jnp
from jax import lax
from jax.sharding import PartitionSpec as P

GROUPS = 16


def _bits(n):
    return n.bit_length() - 1


def _swap(n, bit):
    return [(i, i ^ (1 << bit)) for i in range(n)]


def _halving_sum(x, axis, n, dim, order):
    me = lax.axis_index(axis)
    for bit in order:
        half = x.shape[dim] // 2
        upper = (me >> bit) & 1
        keep = lax.dynamic_slice_in_dim(x, upper * half, half, axis=dim)
        send = lax.dynamic_slice_in_dim(x, (1 - upper) * half, half, axis=dim)
        x = keep + lax.ppermute(send, axis, _swap(n, bit))
    return x


def _butterfly_sum(x, axis, n, order):
    for bit in order:
        x = x + lax.ppermute(x, axis, _swap(n, bit))
    return x


def _join(x, other, upper, dim):
    return jnp.where(upper, jnp.concatenate([other, x], dim), jnp.concatenate([x, other], dim))


def shards(activations, out_grads, proj_in, proj_out, store, ckpt_rate, store_group):
    n_dp = lax.axis_size("dp")
    n_mp = lax.axis_size("mp")
    dp_bits, mp_bits = _bits(n_dp), _bits(n_mp)
    rank = proj_in.shape[1]
    seq_len = activations.shape[2]
    ex_local = activations.shape[1]
    near_first = list(range(mp_bits))

    member = (store_group[:, None] == jnp.arange(GROUPS, dtype=jnp.int32)[None, :]).astype(
        jnp.bfloat16
    )
    group_rows = jnp.einsum("rg,crk->cgk", member, store, preferred_element_type=jnp.float32)
    group_rows = _halving_sum(group_rows, "mp", n_mp, 2, near_first)
    group_rows = _butterfly_sum(group_rows, "dp", n_dp, list(range(dp_bits)))

    part_in = jnp.einsum("cesf,fr->cesr", activations, proj_in, preferred_element_type=jnp.float32)
    part_out = jnp.einsum("cesf,fr->cesr", out_grads, proj_out, preferred_element_type=jnp.float32)
    stacked = jnp.concatenate([part_in, part_out], axis=3)
    summed = _halving_sum(stacked, "mp", n_mp, 2, near_first)
    low_in = summed[..., :rank].astype(jnp.bfloat16)
    low_grad = summed[..., rank:].astype(jnp.bfloat16)
    outer = jnp.einsum("cesa,cesb->ecab", low_in, low_grad, preferred_element_type=jnp.float32)
    outer = outer.reshape(ex_local, 2, rank * rank)
    outer = _halving_sum(outer, "mp", n_mp, 2, near_first)
    query = (outer / jnp.sqrt(jnp.float32(seq_len))).astype(jnp.bfloat16)

    in_slice = jnp.einsum(
        "eck,cgk->ecg", query.astype(jnp.float32), group_rows, precision=lax.Precision.HIGHEST
    )
    group_part = ckpt_rate[0] * in_slice[:, 0] + ckpt_rate[1] * in_slice[:, 1]

    order = [("dp", b) for b in reversed(range(1, dp_bits))]
    order += [("mp", b) for b in reversed(range(mp_bits))]
    order += [("dp", 0)]
    piece, totals = query, group_part
    for axis, bit in order:
        n = n_dp if axis == "dp" else n_mp
        upper = ((lax.axis_index(axis) >> bit) & 1) == 1
        other = lax.ppermute(piece, axis, _swap(n, bit))
        other_totals = lax.ppermute(totals, axis, _swap(n, bit))
        if axis == "dp":
            piece = _join(piece, other, upper, 0)
            totals = _join(totals, other_totals, upper, 0)
        else:
            piece = _join(piece, other, upper, 2)
            totals = totals + other_totals
    first = jnp.einsum("qk,rk->qr", piece[:, 0], store[0], preferred_element_type=jnp.float32)
    second = jnp.einsum("qk,rk->qr", piece[:, 1], store[1], preferred_element_type=jnp.float32)
    scores = ckpt_rate[0] * first + ckpt_rate[1] * second

    def natural(x):
        x = x.reshape((2,) * dp_bits + (ex_local,) + x.shape[1:])
        perm = list(reversed(range(dp_bits))) + list(range(dp_bits, x.ndim))
        return jnp.transpose(x, perm).reshape((n_dp * ex_local,) + x.shape[dp_bits + 1 :])

    scores = natural(scores)
    store_rows = store.shape[1] * n_dp * n_mp
    group_scores = natural(totals) / jnp.sqrt(jnp.float32(store_rows) / jnp.float32(GROUPS))
    return (scores, group_scores)


def solution(mesh):
    placed = (
        P(None, "dp", None, "mp"),
        P(None, "dp", None, "mp"),
        P("mp", None),
        P("mp", None),
        P(None, ("dp", "mp"), None),
        P(),
        P(("dp", "mp")),
    )
    return jax.shard_map(
        shards, mesh=mesh, in_specs=placed, out_specs=(P(None, ("dp", "mp")), P()), check_vma=False
    )
```

time: 204 us -> 141 us (0.69)
  blocking collectives: 122 us -> 0 us
  starting transfers between devices: 0.04 us -> 59.2 us
  between operations: 14.2 us -> 0.97 us
  waiting for transfers between devices: 50.5 us -> 60.3 us
  matrix products: 8.67 us -> 13 us
  local copies, waits for them, and re-layouts: 5.12 us -> 2.58 us
  other arithmetic: 0.66 us -> 2.79 us
    psum x2 -> x0, blocking collectives: 122 us -> none  [the longest x1 75.1 us: shards(): totals = lax.psum(partial_totals, ('dp', 'mp'))]
    ppermute x0 -> x30, waiting for transfers between devices: none -> 60.3 us  [the longest x9 26.9 us: _halving_sum(): x = keep + lax.ppermute(send, axis, _swap(n, bit))]
    ppermute x0 -> x30, starting transfers between devices: none -> 59.2 us  [the longest x9 17.3 us: _halving_sum(): x = keep + lax.ppermute(send, axis, _swap(n, bit))]
    all_gather x1 -> x0, waiting for transfers between devices: 50.5 us -> none  [shards(): piece = lax.all_gather(query, 'dp', axis=0, tiled=True)]
    slice x1 -> x0, local copies, waits for them, and re-layouts: 3.7 us -> none  [shards(): piece[:, 0]]
    dot_general x1 -> x2, matrix products: 0.31 us -> 2.99 us  [the longest x1 2.84 us: shards(): jnp.einsum('rg,crk->cgk', member, store, preferred_element_type=jnp.float32)]
  transfers between devices with their start and end apart: 1 -> 30, of which waited for: 1 -> 22; matrix products, arithmetic and copies ran while one was open for 0% -> 4% of each run, Pallas kernels for 0% -> 0%
where the time goes in v2:
time: 141 us; the launch traced here: 139 us
  waiting for transfers between devices  60.3 us (43%)
  starting transfers between devices  59.2 us (42%)
  matrix products  13 us (9%)
  other arithmetic  2.79 us (2%)
  local copies, waits for them, and re-layouts  2.58 us (2%)
    ppermute x9, waiting for transfers between devices, _halving_sum(): x = keep + lax.ppermute(send, axis, _swap(n, bit))  26.9 us
    ppermute x8, waiting for transfers between devices, shards(): other_totals = lax.ppermute(totals, axis, _swap(n, bit))  19.8 us
    ppermute x9, starting transfers between devices, _halving_sum(): x = keep + lax.ppermute(send, axis, _swap(n, bit))  17.3 us
    ppermute x8, starting transfers between devices, shards(): other = lax.ppermute(piece, axis, _swap(n, bit))  15.8 us
    ppermute x8, starting transfers between devices, shards(): other_totals = lax.ppermute(totals, axis, _swap(n, bit))  14.9 us
    ppermute x5, starting transfers between devices, _butterfly_sum(): x = x + lax.ppermute(x, axis, _swap(n, bit))  11.2 us
    ppermute x8, waiting for transfers between devices, shards(): other = lax.ppermute(piece, axis, _swap(n, bit))  8.19 us
    ppermute x5, waiting for transfers between devices, _butterfly_sum(): x = x + lax.ppermute(x, axis, _swap(n, bit))  5.45 us
  transfers between devices with their start and end apart: 30, of which 22 were waited for; matrix products, arithmetic and copies ran while one was open for 4% of the time, Pallas kernels for 0%

profile of v2, /device:TPU:24, one launch (start us, length us, event | category | flops | bytes accessed | tf_op | source)
XLA Modules:
  0.0 138.8 jit_solution(7146334745252790957)
XLA Ops:
  0.7 4.4 %fusion.18 = f32[2,2,384,64]{2,3,1,0:T(8,128)S(1)} fusion(bf16[2,2,384,1792]{3,2,1,0:T(8,128)(2,1)} %param.7, bf16[1792,64]{0,1:T(8,128)(2,1)} %param.9), kind=kOutput, calls=%fused_computation.26 | convolution fusion | flops 352321536 | bytes 6127616 | tf_op jit(solution)/shard_map/cesf,fr->cesr/dot_general | solution.py:54
  8.0 11.9 %collective-permute-done = f32[2,2,192,128]{2,3,1,0:T(8,128)S(1)} collective-permute-done((f32[2,2,192,128]{2,3,1,0:T(8,128)S(1)}, f32[2,2,192,128]{2,3,1,0:T(8,128)S(1)}, u32[]{:S(2)}, u32[]{:S(2)}) %collective-permute-start) | collective-permute-done | bytes 393248 | tf_op jit(solution)/shard_map/ppermute | solution.py:24
  21.9 5.9 %collective-permute-done.1 = f32[2,2,96,128]{2,3,1,0:T(8,128)S(1)} collective-permute-done((f32[2,2,96,128]{2,3,1,0:T(8,128)S(1)}, f32[2,2,96,128]{2,3,1,0:T(8,128)S(1)}, u32[]{:S(2)}, u32[]{:S(2)}) %collective-permute-start.1) | collective-permute-done | bytes 196640 | tf_op jit(solution)/shard_map/ppermute | solution.py:24
  28.0 3.1 %collective-permute-start.2 = (f32[2,2,48,128]{2,3,1,0:T(8,128)S(1)}, f32[2,2,48,128]{2,3,1,0:T(8,128)S(1)}, u32[]{:S(2)}, u32[]{:S(2)}) collective-permute-start(f32[2,2,48,128]{2,3,1,0:T(8,128)S(1)} %constant_dynamic-slice_fusion.6), channel_id=1, source_target_pairs={{0,4},{1,5},{2,6},{3,7},{4,0},{5,1},{6,2},{7,3},{8,12},{9,13},{10,... | collective-permute-start | bytes 294920 | tf_op jit(solution)/shard_map/ppermute | solution.py:24
  31.1 2.8 %fusion.28 = f32[16,2,4096]{2,0,1:T(8,128)S(1)} fusion(bf16[2,256,4096]{2,1,0:T(8,128)(2,1)} %param.11, s32[256]{0:T(256)S(1)} %copy-done.4), kind=kOutput, calls=%fused_computation.47 | convolution fusion | flops 67112960 | bytes 4719616 | tf_op jit(solution)/shard_map/rg,crk->cgk/dot_general | solution.py:50
  34.0 2.1 %collective-permute-done.2 = f32[2,2,48,128]{2,3,1,0:T(8,128)S(1)} collective-permute-done((f32[2,2,48,128]{2,3,1,0:T(8,128)S(1)}, f32[2,2,48,128]{2,3,1,0:T(8,128)S(1)}, u32[]{:S(2)}, u32[]{:S(2)}) %collective-permute-start.2) | collective-permute-done | bytes 98336 | tf_op jit(solution)/shard_map/ppermute | solution.py:24
  42.3 2.3 %collective-permute-done.14 = f32[2,16,2048]{2,1,0:T(8,128)S(1)} collective-permute-done((f32[2,16,2048]{2,1,0:T(8,128)S(1)}, f32[2,16,2048]{2,1,0:T(8,128)S(1)}, u32[]{:S(2)}, u32[]{:S(2)}) %collective-permute-start.14) | collective-permute-done | bytes 262176 | tf_op jit(solution)/shard_map/ppermute | solution.py:24
  44.7 3.2 %collective-permute-start.5 = (f32[2,2,512]{2,0,1:T(2,128)S(1)}, f32[2,2,512]{2,0,1:T(2,128)S(1)}, u32[]{:S(2)}, u32[]{:S(2)}) collective-permute-start(f32[2,2,512]{2,0,1:T(2,128)S(1)} %constant_dynamic-slice_fusion.2), channel_id=1, source_target_pairs={{0,4},{1,5},{2,6},{3,7},{4,0},{5,1},{6,2},{7,3},{8,12},{9,13},{10,... | collective-permute-start | bytes 24584 | tf_op jit(solution)/shard_map/ppermute | solution.py:24
  50.0 6.6 %collective-permute-start.6 = (bf16[2,2,512]{2,0,1:T(2,128)(2,1)S(1)}, bf16[2,2,512]{2,0,1:T(2,128)(2,1)S(1)}, u32[]{:S(2)}, u32[]{:S(2)}) collective-permute-start(bf16[2,2,512]{2,0,1:T(2,128)(2,1)S(1)} %multiply_convert_fusion), channel_id=1, source_target_pairs={{0,128},{8,136},{16,144},{24,152},{32,160},{40,168},{48,176},{56,1... | collective-permute-start | bytes 12296 | tf_op jit(solution)/shard_map/ppermute | solution.py:77
  58.2 2.7 %collective-permute-start.7 = (bf16[4,2,512]{2,0,1:T(4,128)(2,1)S(1)}, bf16[4,2,512]{2,0,1:T(4,128)(2,1)S(1)}, u32[]{:S(2)}, u32[]{:S(2)}) collective-permute-start(bf16[4,2,512]{2,0,1:T(4,128)(2,1)S(1)} %maximum_select_fusion.9), channel_id=1, source_target_pairs={{0,64},{8,72},{16,80},{24,88},{32,96},{40,104},{48,112},{56,120},{... | collective-permute-start | bytes 24584 | tf_op jit(solution)/shard_map/ppermute | solution.py:77
  61.0 3.1 %collective-permute-start.16 = (f32[2,16,512]{2,1,0:T(8,128)S(1)}, f32[2,16,512]{2,1,0:T(8,128)S(1)}, u32[]{:S(2)}, u32[]{:S(2)}) collective-permute-start(f32[2,16,512]{2,1,0:T(8,128)S(1)} %constant_dynamic-slice_fusion), channel_id=1, source_target_pairs={{0,4},{1,5},{2,6},{3,7},{4,0},{5,1},{6,2},{7,3},{8,12},{9,13},{10,... | collective-permute-start | bytes 196616 | tf_op jit(solution)/shard_map/ppermute | solution.py:24
  66.8 2.6 %collective-permute-done.8 = bf16[8,2,512]{2,0,1:T(8,128)(2,1)S(1)} collective-permute-done((bf16[8,2,512]{2,0,1:T(8,128)(2,1)S(1)}, bf16[8,2,512]{2,0,1:T(8,128)(2,1)S(1)}, u32[]{:S(2)}, u32[]{:S(2)}) %collective-permute-start.8) | collective-permute-done | bytes 16416 | tf_op jit(solution)/shard_map/ppermute | solution.py:77
  73.4 2.1 %collective-permute-start.10 = (bf16[32,2,512]{2,0,1:T(8,128)(2,1)S(1)}, bf16[32,2,512]{2,0,1:T(8,128)(2,1)S(1)}, u32[]{:S(2)}, u32[]{:S(2)}) collective-permute-start(bf16[32,2,512]{2,0,1:T(8,128)(2,1)S(1)} %maximum_select_fusion.4), channel_id=1, source_target_pairs={{0,4},{1,5},{2,6},{3,7},{4,0},{5,1},{6,2},{7,3},{8,12},{9,13},{10,... | collective-permute-start | bytes 196616 | tf_op jit(solution)/shard_map/ppermute | solution.py:77
  77.0 2.3 %collective-permute-done.10 = bf16[32,2,512]{2,0,1:T(8,128)(2,1)S(1)} collective-permute-done((bf16[32,2,512]{2,0,1:T(8,128)(2,1)S(1)}, bf16[32,2,512]{2,0,1:T(8,128)(2,1)S(1)}, u32[]{:S(2)}, u32[]{:S(2)}) %collective-permute-start.10) | collective-permute-done | bytes 65568 | tf_op jit(solution)/shard_map/ppermute | solution.py:77
  81.6 2.6 %collective-permute-start.20 = (f32[2,16,512]{2,1,0:T(8,128)S(1)}, f32[2,16,512]{2,1,0:T(8,128)S(1)}, u32[]{:S(2)}, u32[]{:S(2)}) collective-permute-start(f32[2,16,512]{2,1,0:T(8,128)S(1)} %add.126), channel_id=1, source_target_pairs={{0,64},{8,72},{16,80},{24,88},{32,96},{40,104},{48,112},{56,120},{... | collective-permute-start | bytes 196616 | tf_op jit(solution)/shard_map/ppermute | solution.py:30
  84.9 2.7 %collective-permute-done.20 = f32[2,16,512]{2,1,0:T(8,128)S(1)} collective-permute-done((f32[2,16,512]{2,1,0:T(8,128)S(1)}, f32[2,16,512]{2,1,0:T(8,128)S(1)}, u32[]{:S(2)}, u32[]{:S(2)}) %collective-permute-start.20) | collective-permute-done | bytes 65568 | tf_op jit(solution)/shard_map/ppermute | solution.py:30
  87.5 5.6 %collective-permute-start.21 = (f32[2,16,512]{2,1,0:T(8,128)S(1)}, f32[2,16,512]{2,1,0:T(8,128)S(1)}, u32[]{:S(2)}, u32[]{:S(2)}) collective-permute-start(f32[2,16,512]{2,1,0:T(8,128)S(1)} %add.127), channel_id=1, source_target_pairs={{0,128},{8,136},{16,144},{24,152},{32,160},{40,168},{48,176},{56,1... | collective-permute-start | bytes 196616 | tf_op jit(solution)/shard_map/ppermute | solution.py:30
  97.4 5.6 %collective-permute-start.22 = (f32[2,16]{1,0:T(2,128)S(1)}, f32[2,16]{1,0:T(2,128)S(1)}, u32[]{:S(2)}, u32[]{:S(2)}) collective-permute-start(f32[2,16]{1,0:T(2,128)S(1)} %fusion.32), channel_id=1, source_target_pairs={{0,128},{8,136},{16,144},{24,152},{32,160},{40,168},{48,176},{56,1... | collective-permute-start | bytes 392 | tf_op jit(solution)/shard_map/ppermute | solution.py:78
  105.0 2.6 %collective-permute-start.23 = (f32[4,16]{1,0:T(4,128)S(1)}, f32[4,16]{1,0:T(4,128)S(1)}, u32[]{:S(2)}, u32[]{:S(2)}) collective-permute-start(f32[4,16]{1,0:T(4,128)S(1)} %maximum_select_fusion.12), channel_id=1, source_target_pairs={{0,64},{8,72},{16,80},{24,88},{32,96},{40,104},{48,112},{56,120},{... | collective-permute-start | bytes 776 | tf_op jit(solution)/shard_map/ppermute | solution.py:78
  111.0 3.8 %collective-permute-done.24 = f32[8,16]{1,0:T(8,128)S(1)} collective-permute-done((f32[8,16]{1,0:T(8,128)S(1)}, f32[8,16]{1,0:T(8,128)S(1)}, u32[]{:S(2)}, u32[]{:S(2)}) %collective-permute-start.24) | collective-permute-done | bytes 544 | tf_op jit(solution)/shard_map/ppermute | solution.py:78
  115.7 2.7 %collective-permute-done.25 = f32[16,16]{1,0:T(8,128)S(1)} collective-permute-done((f32[16,16]{1,0:T(8,128)S(1)}, f32[16,16]{1,0:T(8,128)S(1)}, u32[]{:S(2)}, u32[]{:S(2)}) %collective-permute-start.25) | collective-permute-done | bytes 1056 | tf_op jit(solution)/shard_map/ppermute | solution.py:78
  120.3 3.4 %collective-permute-done.26 = f32[32,16]{1,0:T(8,128)S(1)} collective-permute-done((f32[32,16]{1,0:T(8,128)S(1)}, f32[32,16]{1,0:T(8,128)S(1)}, u32[]{:S(2)}, u32[]{:S(2)}) %collective-permute-start.26) | collective-permute-done | bytes 2080 | tf_op jit(solution)/shard_map/ppermute | solution.py:78
  124.3 3.2 %collective-permute-done.27 = f32[32,16]{1,0:T(8,128)S(1)} collective-permute-done((f32[32,16]{1,0:T(8,128)S(1)}, f32[32,16]{1,0:T(8,128)S(1)}, u32[]{:S(2)}, u32[]{:S(2)}) %collective-permute-start.27) | collective-permute-done | bytes 2080 | tf_op jit(solution)/shard_map/ppermute | solution.py:78
  133.3 3.4 %fusion.12 = f32[64,256]{1,0:T(8,128)S(1)} fusion(bf16[2,256,4096]{2,1,0:T(8,128)(2,1)} %param.11, bf16[64,2,4096]{2,0,1:T(8,128)(2,1)S(1)} %maximum_select_fusion, f32[]{:T(128)} %bitcast.7), kind=kOutput, calls=%fused_computation.8 | convolution fusion | flops 134234112 | bytes 2687488 | tf_op jit(solution)/shard_map/qk,rk->qr/dot_general | solution.py:86
  (101 shorter events, 47.2 us)
Async XLA Ops:
  6.0 13.9 %collective-permute-start = (f32[2,2,192,128]{2,3,1,0:T(8,128)S(1)}, f32[2,2,192,128]{2,3,1,0:T(8,128)S(1)}, u32[]{:S(2)}, u32[]{:S(2)}) collective-permute-start(f32[2,2,192,128]{2,3,1,0:T(8,128)S(1)} %fusion.15), channel_id=1, source_target_pairs={{0,1},{1,0},{2,3},{3,2},{4,5},{5,4},{6,7},{7,6},{8,9},{9,8},{10,11... | collective-permute-start | bytes 1179656 | tf_op jit(solution)/shard_map/ppermute | solution.py:24
  20.3 7.5 %collective-permute-start.1 = (f32[2,2,96,128]{2,3,1,0:T(8,128)S(1)}, f32[2,2,96,128]{2,3,1,0:T(8,128)S(1)}, u32[]{:S(2)}, u32[]{:S(2)}) collective-permute-start(f32[2,2,96,128]{2,3,1,0:T(8,128)S(1)} %constant_dynamic-slice_fusion.7), channel_id=1, source_target_pairs={{0,2},{1,3},{2,0},{3,1},{4,6},{5,7},{6,4},{7,5},{8,10},{9,11},{10,... | collective-permute-start | bytes 589832 | tf_op jit(solution)/shard_map/ppermute | solution.py:24
  28.0 8.1 %collective-permute-start.2 = (f32[2,2,48,128]{2,3,1,0:T(8,128)S(1)}, f32[2,2,48,128]{2,3,1,0:T(8,128)S(1)}, u32[]{:S(2)}, u32[]{:S(2)}) collective-permute-start(f32[2,2,48,128]{2,3,1,0:T(8,128)S(1)} %constant_dynamic-slice_fusion.6), channel_id=1, source_target_pairs={{0,4},{1,5},{2,6},{3,7},{4,0},{5,1},{6,2},{7,3},{8,12},{9,13},{10,... | collective-permute-start | bytes 294920 | tf_op jit(solution)/shard_map/ppermute | solution.py:24
  36.6 4.1 %collective-permute-start.3 = (f32[2,2,2048]{2,0,1:T(2,128)S(1)}, f32[2,2,2048]{2,0,1:T(2,128)S(1)}, u32[]{:S(2)}, u32[]{:S(2)}) collective-permute-start(f32[2,2,2048]{2,0,1:T(2,128)S(1)} %copy.60), channel_id=1, source_target_pairs={{0,1},{1,0},{2,3},{3,2},{4,5},{5,4},{6,7},{7,6},{8,9},{9,8},{10,11... | collective-permute-start | bytes 98312 | tf_op jit(solution)/shard_map/ppermute | solution.py:24
  38.2 6.5 %collective-permute-start.14 = (f32[2,16,2048]{2,1,0:T(8,128)S(1)}, f32[2,16,2048]{2,1,0:T(8,128)S(1)}, u32[]{:S(2)}, u32[]{:S(2)}) collective-permute-start(f32[2,16,2048]{2,1,0:T(8,128)S(1)} %dynamic-slice_bitcast_fusion), channel_id=1, source_target_pairs={{0,1},{1,0},{2,3},{3,2},{4,5},{5,4},{6,7},{7,6},{8,9},{9,8},{10,11... | collective-permute-start | bytes 786440 | tf_op jit(solution)/shard_map/ppermute | solution.py:24
  44.7 5.2 %collective-permute-start.5 = (f32[2,2,512]{2,0,1:T(2,128)S(1)}, f32[2,2,512]{2,0,1:T(2,128)S(1)}, u32[]{:S(2)}, u32[]{:S(2)}) collective-permute-start(f32[2,2,512]{2,0,1:T(2,128)S(1)} %constant_dynamic-slice_fusion.2), channel_id=1, source_target_pairs={{0,4},{1,5},{2,6},{3,7},{4,0},{5,1},{6,2},{7,3},{8,12},{9,13},{10,... | collective-permute-start | bytes 24584 | tf_op jit(solution)/shard_map/ppermute | solution.py:24
  47.9 8.7 %collective-permute-start.15 = (f32[2,16,1024]{2,1,0:T(8,128)S(1)}, f32[2,16,1024]{2,1,0:T(8,128)S(1)}, u32[]{:S(2)}, u32[]{:S(2)}) collective-permute-start(f32[2,16,1024]{2,1,0:T(8,128)S(1)} %constant_dynamic-slice_fusion.1), channel_id=1, source_target_pairs={{0,2},{1,3},{2,0},{3,1},{4,6},{5,7},{6,4},{7,5},{8,10},{9,11},{10,... | collective-permute-start | bytes 393224 | tf_op jit(solution)/shard_map/ppermute | solution.py:24
  50.0 8.2 %collective-permute-start.6 = (bf16[2,2,512]{2,0,1:T(2,128)(2,1)S(1)}, bf16[2,2,512]{2,0,1:T(2,128)(2,1)S(1)}, u32[]{:S(2)}, u32[]{:S(2)}) collective-permute-start(bf16[2,2,512]{2,0,1:T(2,128)(2,1)S(1)} %multiply_convert_fusion), channel_id=1, source_target_pairs={{0,128},{8,136},{16,144},{24,152},{32,160},{40,168},{48,176},{56,1... | collective-permute-start | bytes 12296 | tf_op jit(solution)/shard_map/ppermute | solution.py:77
  58.2 5.8 %collective-permute-start.7 = (bf16[4,2,512]{2,0,1:T(4,128)(2,1)S(1)}, bf16[4,2,512]{2,0,1:T(4,128)(2,1)S(1)}, u32[]{:S(2)}, u32[]{:S(2)}) collective-permute-start(bf16[4,2,512]{2,0,1:T(4,128)(2,1)S(1)} %maximum_select_fusion.9), channel_id=1, source_target_pairs={{0,64},{8,72},{16,80},{24,88},{32,96},{40,104},{48,112},{56,120},{... | collective-permute-start | bytes 24584 | tf_op jit(solution)/shard_map/ppermute | solution.py:77
  61.0 5.8 %collective-permute-start.16 = (f32[2,16,512]{2,1,0:T(8,128)S(1)}, f32[2,16,512]{2,1,0:T(8,128)S(1)}, u32[]{:S(2)}, u32[]{:S(2)}) collective-permute-start(f32[2,16,512]{2,1,0:T(8,128)S(1)} %constant_dynamic-slice_fusion), channel_id=1, source_target_pairs={{0,4},{1,5},{2,6},{3,7},{4,0},{5,1},{6,2},{7,3},{8,12},{9,13},{10,... | collective-permute-start | bytes 196616 | tf_op jit(solution)/shard_map/ppermute | solution.py:24
  64.1 5.3 %collective-permute-start.8 = (bf16[8,2,512]{2,0,1:T(8,128)(2,1)S(1)}, bf16[8,2,512]{2,0,1:T(8,128)(2,1)S(1)}, u32[]{:S(2)}, u32[]{:S(2)}) collective-permute-start(bf16[8,2,512]{2,0,1:T(8,128)(2,1)S(1)} %maximum_select_fusion.7), channel_id=1, source_target_pairs={{0,32},{8,40},{16,48},{24,56},{32,0},{40,8},{48,16},{56,24},{64,96... | collective-permute-start | bytes 49160 | tf_op jit(solution)/shard_map/ppermute | solution.py:77
  69.4 4.0 %collective-permute-start.9 = (bf16[16,2,512]{2,0,1:T(8,128)(2,1)S(1)}, bf16[16,2,512]{2,0,1:T(8,128)(2,1)S(1)}, u32[]{:S(2)}, u32[]{:S(2)}) collective-permute-start(bf16[16,2,512]{2,0,1:T(8,128)(2,1)S(1)} %maximum_select_fusion.5), channel_id=1, source_target_pairs={{0,16},{8,24},{16,0},{24,8},{32,48},{40,56},{48,32},{56,40},{64,80... | collective-permute-start | bytes 98312 | tf_op jit(solution)/shard_map/ppermute | solution.py:77
  70.3 5.2 %collective-permute-start.18 = (f32[2,16,512]{2,1,0:T(8,128)S(1)}, f32[2,16,512]{2,1,0:T(8,128)S(1)}, u32[]{:S(2)}, u32[]{:S(2)}) collective-permute-start(f32[2,16,512]{2,1,0:T(8,128)S(1)} %add.124), channel_id=1, source_target_pairs={{0,16},{8,24},{16,0},{24,8},{32,48},{40,56},{48,32},{56,40},{64,80... | collective-permute-start | bytes 196616 | tf_op jit(solution)/shard_map/ppermute | solution.py:30
  73.4 5.9 %collective-permute-start.10 = (bf16[32,2,512]{2,0,1:T(8,128)(2,1)S(1)}, bf16[32,2,512]{2,0,1:T(8,128)(2,1)S(1)}, u32[]{:S(2)}, u32[]{:S(2)}) collective-permute-start(bf16[32,2,512]{2,0,1:T(8,128)(2,1)S(1)} %maximum_select_fusion.4), channel_id=1, source_target_pairs={{0,4},{1,5},{2,6},{3,7},{4,0},{5,1},{6,2},{7,3},{8,12},{9,13},{10,... | collective-permute-start | bytes 196616 | tf_op jit(solution)/shard_map/ppermute | solution.py:77
  75.5 6.0 %collective-permute-start.19 = (f32[2,16,512]{2,1,0:T(8,128)S(1)}, f32[2,16,512]{2,1,0:T(8,128)S(1)}, u32[]{:S(2)}, u32[]{:S(2)}) collective-permute-start(f32[2,16,512]{2,1,0:T(8,128)S(1)} %add.125), channel_id=1, source_target_pairs={{0,32},{8,40},{16,48},{24,56},{32,0},{40,8},{48,16},{56,24},{64,96... | collective-permute-start | bytes 196616 | tf_op jit(solution)/shard_map/ppermute | solution.py:30
  79.3 13.8 %collective-permute-start.11 = (bf16[32,2,1024]{2,0,1:T(8,128)(2,1)S(1)}, bf16[32,2,1024]{2,0,1:T(8,128)(2,1)S(1)}, u32[]{:S(2)}, u32[]{:S(2)}) collective-permute-start(bf16[32,2,1024]{2,0,1:T(8,128)(2,1)S(1)} %maximum_select_fusion.3), channel_id=1, source_target_pairs={{0,2},{1,3},{2,0},{3,1},{4,6},{5,7},{6,4},{7,5},{8,10},{9,11},{10,... | collective-permute-start | bytes 393224 | tf_op jit(solution)/shard_map/ppermute | solution.py:77
  81.6 6.0 %collective-permute-start.20 = (f32[2,16,512]{2,1,0:T(8,128)S(1)}, f32[2,16,512]{2,1,0:T(8,128)S(1)}, u32[]{:S(2)}, u32[]{:S(2)}) collective-permute-start(f32[2,16,512]{2,1,0:T(8,128)S(1)} %add.126), channel_id=1, source_target_pairs={{0,64},{8,72},{16,80},{24,88},{32,96},{40,104},{48,112},{56,120},{... | collective-permute-start | bytes 196616 | tf_op jit(solution)/shard_map/ppermute | solution.py:30
  87.5 8.4 %collective-permute-start.21 = (f32[2,16,512]{2,1,0:T(8,128)S(1)}, f32[2,16,512]{2,1,0:T(8,128)S(1)}, u32[]{:S(2)}, u32[]{:S(2)}) collective-permute-start(f32[2,16,512]{2,1,0:T(8,128)S(1)} %add.127), channel_id=1, source_target_pairs={{0,128},{8,136},{16,144},{24,152},{32,160},{40,168},{48,176},{56,1... | collective-permute-start | bytes 196616 | tf_op jit(solution)/shard_map/ppermute | solution.py:30
  93.2 9.8 %collective-permute-start.12 = (bf16[32,2,2048]{2,0,1:T(8,128)(2,1)S(1)}, bf16[32,2,2048]{2,0,1:T(8,128)(2,1)S(1)}, u32[]{:S(2)}, u32[]{:S(2)}) collective-permute-start(bf16[32,2,2048]{2,0,1:T(8,128)(2,1)S(1)} %maximum_select_fusion.2), channel_id=1, source_target_pairs={{0,1},{1,0},{2,3},{3,2},{4,5},{5,4},{6,7},{7,6},{8,9},{9,8},{10,11... | collective-permute-start | bytes 786440 | tf_op jit(solution)/shard_map/ppermute | solution.py:77
  97.4 7.6 %collective-permute-start.22 = (f32[2,16]{1,0:T(2,128)S(1)}, f32[2,16]{1,0:T(2,128)S(1)}, u32[]{:S(2)}, u32[]{:S(2)}) collective-permute-start(f32[2,16]{1,0:T(2,128)S(1)} %fusion.32), channel_id=1, source_target_pairs={{0,128},{8,136},{16,144},{24,152},{32,160},{40,168},{48,176},{56,1... | collective-permute-start | bytes 392 | tf_op jit(solution)/shard_map/ppermute | solution.py:78
  103.1 30.0 %collective-permute-start.13 = (bf16[32,2,4096]{2,0,1:T(8,128)(2,1)S(1)}, bf16[32,2,4096]{2,0,1:T(8,128)(2,1)S(1)}, u32[]{:S(2)}, u32[]{:S(2)}) collective-permute-start(bf16[32,2,4096]{2,0,1:T(8,128)(2,1)S(1)} %maximum_select_fusion.1), channel_id=1, source_target_pairs={{0,8},{8,0},{16,24},{24,16},{32,40},{40,32},{48,56},{56,48},{64,72... | collective-permute-start | bytes 1572872 | tf_op jit(solution)/shard_map/ppermute | solution.py:77
  105.0 4.6 %collective-permute-start.23 = (f32[4,16]{1,0:T(4,128)S(1)}, f32[4,16]{1,0:T(4,128)S(1)}, u32[]{:S(2)}, u32[]{:S(2)}) collective-permute-start(f32[4,16]{1,0:T(4,128)S(1)} %maximum_select_fusion.12), channel_id=1, source_target_pairs={{0,64},{8,72},{16,80},{24,88},{32,96},{40,104},{48,112},{56,120},{... | collective-permute-start | bytes 776 | tf_op jit(solution)/shard_map/ppermute | solution.py:78
  109.6 5.2 %collective-permute-start.24 = (f32[8,16]{1,0:T(8,128)S(1)}, f32[8,16]{1,0:T(8,128)S(1)}, u32[]{:S(2)}, u32[]{:S(2)}) collective-permute-start(f32[8,16]{1,0:T(8,128)S(1)} %maximum_select_fusion.11), channel_id=1, source_target_pairs={{0,32},{8,40},{16,48},{24,56},{32,0},{40,8},{48,16},{56,24},{64,96... | collective-permute-start | bytes 1544 | tf_op jit(solution)/shard_map/ppermute | solution.py:78
  118.4 5.2 %collective-permute-start.26 = (f32[32,16]{1,0:T(8,128)S(1)}, f32[32,16]{1,0:T(8,128)S(1)}, u32[]{:S(2)}, u32[]{:S(2)}) collective-permute-start(f32[32,16]{1,0:T(8,128)S(1)} %maximum_select_fusion.8), channel_id=1, source_target_pairs={{0,4},{1,5},{2,6},{3,7},{4,0},{5,1},{6,2},{7,3},{8,12},{9,13},{10,... | collective-permute-start | bytes 6152 | tf_op jit(solution)/shard_map/ppermute | solution.py:78
  (11 other events, 105.2 us)

commit v3 on v2

v3 whole, which is shorter than its diff:
```python
import jax
import jax.numpy as jnp
from jax import lax
from jax.sharding import PartitionSpec as P

GROUPS = 16


def _bits(n):
    return n.bit_length() - 1


def _swap(n, bit):
    return [(i, i ^ (1 << bit)) for i in range(n)]


def _halving_sum(x, axis, n, dim, order):
    me = lax.axis_index(axis)
    for bit in order:
        half = x.shape[dim] // 2
        upper = (me >> bit) & 1
        keep = lax.dynamic_slice_in_dim(x, upper * half, half, axis=dim)
        send = lax.dynamic_slice_in_dim(x, (1 - upper) * half, half, axis=dim)
        x = keep + lax.ppermute(send, axis, _swap(n, bit))
    return x


def _butterfly_sum(x, axis, n, order):
    for bit in order:
        x = x + lax.ppermute(x, axis, _swap(n, bit))
    return x


def _join(x, other, upper, dim):
    return jnp.where(upper, jnp.concatenate([other, x], dim), jnp.concatenate([x, other], dim))


def _doubling_gather(x, axis, n, dim, order):
    me = lax.axis_index(axis)
    for bit in order:
        upper = ((me >> bit) & 1) == 1
        x = _join(x, lax.ppermute(x, axis, _swap(n, bit)), upper, dim)
    return x


def shards(activations, out_grads, proj_in, proj_out, store, ckpt_rate, store_group):
    n_dp = lax.axis_size("dp")
    n_mp = lax.axis_size("mp")
    dp_bits, mp_bits = _bits(n_dp), _bits(n_mp)
    rank = proj_in.shape[1]
    seq_len = activations.shape[2]
    ex_local = activations.shape[1]

    part_in = jnp.einsum("cesf,fr->cesr", activations, proj_in, preferred_element_type=jnp.float32)
    part_out = jnp.einsum("cesf,fr->cesr", out_grads, proj_out, preferred_element_type=jnp.float32)
    stacked = jnp.concatenate([part_in, part_out], axis=3)
    summed = _halving_sum(stacked, "mp", n_mp, 2, list(range(mp_bits)))
    low = _doubling_gather(summed.astype(jnp.bfloat16), "mp", n_mp, 2, list(reversed(range(mp_bits))))
    outer = jnp.einsum(
        "cesa,cesb->ecab", low[..., :rank], low[..., rank:], preferred_element_type=jnp.float32
    )
    outer = outer.reshape(ex_local, 2, rank * rank)
    query = (outer / jnp.sqrt(jnp.float32(seq_len))).astype(jnp.bfloat16)
    piece = _doubling_gather(query, "dp", n_dp, 0, list(reversed(range(dp_bits))))
    first = jnp.einsum("qk,rk->qr", piece[:, 0], store[0], preferred_element_type=jnp.float32)
    second = jnp.einsum("qk,rk->qr", piece[:, 1], store[1], preferred_element_type=jnp.float32)
    scores = ckpt_rate[0] * first + ckpt_rate[1] * second
    member = (store_group[:, None] == jnp.arange(GROUPS, dtype=jnp.int32)[None, :]).astype(
        jnp.float32
    )
    partial_totals = jnp.dot(scores, member, precision=lax.Precision.HIGHEST)
    totals = _butterfly_sum(partial_totals, "mp", n_mp, list(range(mp_bits)))
    totals = _butterfly_sum(totals, "dp", n_dp, list(range(dp_bits)))

    def natural(x):
        x = x.reshape((2,) * dp_bits + (ex_local,) + x.shape[1:])
        perm = list(reversed(range(dp_bits))) + list(range(dp_bits, x.ndim))
        return jnp.transpose(x, perm).reshape((n_dp * ex_local,) + x.shape[dp_bits + 1 :])

    scores = natural(scores)
    store_rows = store.shape[1] * n_dp * n_mp
    group_scores = natural(totals) / jnp.sqrt(jnp.float32(store_rows) / jnp.float32(GROUPS))
    return (scores, group_scores)


def solution(mesh):
    placed = (
        P(None, "dp", None, "mp"),
        P(None, "dp", None, "mp"),
        P("mp", None),
        P("mp", None),
        P(None, ("dp", "mp"), None),
        P(),
        P(("dp", "mp")),
    )
    return jax.shard_map(
        shards, mesh=mesh, in_specs=placed, out_specs=(P(None, ("dp", "mp")), P()), check_vma=False
    )
```

time: 141 us -> 128 us (0.908)
  starting transfers between devices: 59.2 us -> 40.2 us
  waiting for transfers between devices: 60.3 us -> 71.6 us
  matrix products: 13 us -> 9.95 us
    ppermute x5 -> x8, waiting for transfers between devices: 5.45 us -> 18.8 us  [_butterfly_sum(): x = x + lax.ppermute(x, axis, _swap(n, bit))]
    ppermute x16 -> x8, starting transfers between devices: 30.7 us -> 18.2 us  [_doubling_gather(): x = _join(x, lax.ppermute(x, axis, _swap(n, bit)), upper, dim)]
    ppermute x9 -> x3, starting transfers between devices: 17.3 us -> 6.69 us  [_halving_sum(): x = keep + lax.ppermute(send, axis, _swap(n, bit))]
    ppermute x9 -> x3, waiting for transfers between devices: 26.9 us -> 22.8 us  [_halving_sum(): x = keep + lax.ppermute(send, axis, _swap(n, bit))]
    ppermute x5 -> x8, starting transfers between devices: 11.2 us -> 15.2 us  [_butterfly_sum(): x = x + lax.ppermute(x, axis, _swap(n, bit))]
    dot_general x3 -> x2, matrix products: 3.13 us -> 0.51 us  [the longest x1 0.31 us: shards(): partial_totals = jnp.dot(scores, member, precision=lax.Precision.HIGHEST)]
    ppermute x16 -> x8, waiting for transfers between devices: 28 us -> 30 us  [_doubling_gather(): x = _join(x, lax.ppermute(x, axis, _swap(n, bit)), upper, dim)]
  transfers between devices with their start and end apart: 30 -> 19, of which waited for: 22 -> 19; matrix products, arithmetic and copies ran while one was open for 4% -> 1% of each run, Pallas kernels for 0% -> 0%
where the time goes in v3:
time: 128 us; the launch traced here: 127 us
  waiting for transfers between devices  71.6 us (56%)
  starting transfers between devices  40.2 us (31%)
  matrix products  9.95 us (8%)
  local copies, waits for them, and re-layouts  2.57 us (2%)
  other arithmetic  2.04 us (2%)
    ppermute x8, waiting for transfers between devices, _doubling_gather(): x = _join(x, lax.ppermute(x, axis, _swap(n, bit)), upper, dim)  30 us
    ppermute x3, waiting for transfers between devices, _halving_sum(): x = keep + lax.ppermute(send, axis, _swap(n, bit))  22.8 us
    ppermute x8, waiting for transfers between devices, _butterfly_sum(): x = x + lax.ppermute(x, axis, _swap(n, bit))  18.8 us
    ppermute x8, starting transfers between devices, _doubling_gather(): x = _join(x, lax.ppermute(x, axis, _swap(n, bit)), upper, dim)  18.2 us
    ppermute x8, starting transfers between devices, _butterfly_sum(): x = x + lax.ppermute(x, axis, _swap(n, bit))  15.2 us
    ppermute x3, starting transfers between devices, _halving_sum(): x = keep + lax.ppermute(send, axis, _swap(n, bit))  6.69 us
    dot_general x1, matrix products, shards(): jnp.einsum('cesf,fr->cesr', activations, proj_in, preferred_element_type=...  4.44 us
    dot_general x1, matrix products, shards(): jnp.einsum('qk,rk->qr', piece[:, 1], store[1], preferred_element_type=jnp...  3 us
  transfers between devices with their start and end apart: 19, of which 19 were waited for; matrix products, arithmetic and copies ran while one was open for 1% of the time, Pallas kernels for 0%

profile of v3, /device:TPU:24, one launch (start us, length us, event | category | flops | bytes accessed | tf_op | source)
XLA Modules:
  0.0 127.2 jit_solution(9290281840706320359)
XLA Ops:
  0.7 4.4 %fusion.19 = f32[2,2,384,64]{2,3,1,0:T(8,128)S(1)} fusion(bf16[2,2,384,1792]{3,2,1,0:T(8,128)(2,1)} %param.7, bf16[1792,64]{0,1:T(8,128)(2,1)} %param.9), kind=kOutput, calls=%fused_computation.27 | convolution fusion | flops 352321536 | bytes 6127616 | tf_op jit(solution)/shard_map/cesf,fr->cesr/dot_general | solution.py:54
  6.0 2.0 %collective-permute-start = (f32[2,2,192,128]{2,3,1,0:T(8,128)S(1)}, f32[2,2,192,128]{2,3,1,0:T(8,128)S(1)}, u32[]{:S(2)}, u32[]{:S(2)}) collective-permute-start(f32[2,2,192,128]{2,3,1,0:T(8,128)S(1)} %fusion.16), channel_id=1, source_target_pairs={{0,1},{1,0},{2,3},{3,2},{4,5},{5,4},{6,7},{7,6},{8,9},{9,8},{10,11... | collective-permute-start | bytes 1179656 | tf_op jit(solution)/shard_map/ppermute | solution.py:24
  8.0 11.9 %collective-permute-done = f32[2,2,192,128]{2,3,1,0:T(8,128)S(1)} collective-permute-done((f32[2,2,192,128]{2,3,1,0:T(8,128)S(1)}, f32[2,2,192,128]{2,3,1,0:T(8,128)S(1)}, u32[]{:S(2)}, u32[]{:S(2)}) %collective-permute-start) | collective-permute-done | bytes 393248 | tf_op jit(solution)/shard_map/ppermute | solution.py:24
  21.9 5.9 %collective-permute-done.1 = f32[2,2,96,128]{2,3,1,0:T(8,128)S(1)} collective-permute-done((f32[2,2,96,128]{2,3,1,0:T(8,128)S(1)}, f32[2,2,96,128]{2,3,1,0:T(8,128)S(1)}, u32[]{:S(2)}, u32[]{:S(2)}) %collective-permute-start.1) | collective-permute-done | bytes 196640 | tf_op jit(solution)/shard_map/ppermute | solution.py:24
  28.0 3.1 %collective-permute-start.2 = (f32[2,2,48,128]{2,3,1,0:T(8,128)S(1)}, f32[2,2,48,128]{2,3,1,0:T(8,128)S(1)}, u32[]{:S(2)}, u32[]{:S(2)}) collective-permute-start(f32[2,2,48,128]{2,3,1,0:T(8,128)S(1)} %constant_dynamic-slice_fusion), channel_id=1, source_target_pairs={{0,4},{1,5},{2,6},{3,7},{4,0},{5,1},{6,2},{7,3},{8,12},{9,13},{10,... | collective-permute-start | bytes 294920 | tf_op jit(solution)/shard_map/ppermute | solution.py:24
  31.1 5.0 %collective-permute-done.2 = f32[2,2,48,128]{2,3,1,0:T(8,128)S(1)} collective-permute-done((f32[2,2,48,128]{2,3,1,0:T(8,128)S(1)}, f32[2,2,48,128]{2,3,1,0:T(8,128)S(1)}, u32[]{:S(2)}, u32[]{:S(2)}) %collective-permute-start.2) | collective-permute-done | bytes 98336 | tf_op jit(solution)/shard_map/ppermute | solution.py:24
  36.3 3.1 %collective-permute-start.3 = (bf16[2,2,48,128]{2,3,1,0:T(8,128)(2,1)S(1)}, bf16[2,2,48,128]{2,3,1,0:T(8,128)(2,1)S(1)}, u32[]{:S(2)}, u32[]{:S(2)}) collective-permute-start(bf16[2,2,48,128]{2,3,1,0:T(8,128)(2,1)S(1)} %add_convert_fusion), channel_id=1, source_target_pairs={{0,4},{1,5},{2,6},{3,7},{4,0},{5,1},{6,2},{7,3},{8,12},{9,13},{10,... | collective-permute-start | bytes 147464 | tf_op jit(solution)/shard_map/ppermute | solution.py:42
  39.4 3.4 %collective-permute-done.3 = bf16[2,2,48,128]{2,3,1,0:T(8,128)(2,1)S(1)} collective-permute-done((bf16[2,2,48,128]{2,3,1,0:T(8,128)(2,1)S(1)}, bf16[2,2,48,128]{2,3,1,0:T(8,128)(2,1)S(1)}, u32[]{:S(2)}, u32[]{:S(2)}) %collective-permute-start.3) | collective-permute-done | bytes 49184 | tf_op jit(solution)/shard_map/ppermute | solution.py:42
  44.5 3.5 %collective-permute-done.4 = bf16[2,2,96,128]{2,3,1,0:T(8,128)(2,1)S(1)} collective-permute-done((bf16[2,2,96,128]{2,3,1,0:T(8,128)(2,1)S(1)}, bf16[2,2,96,128]{2,3,1,0:T(8,128)(2,1)S(1)}, u32[]{:S(2)}, u32[]{:S(2)}) %collective-permute-start.4) | collective-permute-done | bytes 98336 | tf_op jit(solution)/shard_map/ppermute | solution.py:42
  48.3 1.9 %collective-permute-start.5 = (bf16[2,2,192,128]{2,3,1,0:T(8,128)(2,1)S(1)}, bf16[2,2,192,128]{2,3,1,0:T(8,128)(2,1)S(1)}, u32[]{:S(2)}, u32[]{:S(2)}) collective-permute-start(bf16[2,2,192,128]{2,3,1,0:T(8,128)(2,1)S(1)} %maximum_select_fusion.3), channel_id=1, source_target_pairs={{0,1},{1,0},{2,3},{3,2},{4,5},{5,4},{6,7},{7,6},{8,9},{9,8},{10,11... | collective-permute-start | bytes 589832 | tf_op jit(solution)/shard_map/ppermute | solution.py:42
  50.2 4.5 %collective-permute-done.5 = bf16[2,2,192,128]{2,3,1,0:T(8,128)(2,1)S(1)} collective-permute-done((bf16[2,2,192,128]{2,3,1,0:T(8,128)(2,1)S(1)}, bf16[2,2,192,128]{2,3,1,0:T(8,128)(2,1)S(1)}, u32[]{:S(2)}, u32[]{:S(2)}) %collective-permute-start.5) | collective-permute-done | bytes 196640 | tf_op jit(solution)/shard_map/ppermute | solution.py:42
  55.5 7.9 %collective-permute-start.6 = (bf16[2,2,4096]{2,0,1:T(2,128)(2,1)S(1)}, bf16[2,2,4096]{2,0,1:T(2,128)(2,1)S(1)}, u32[]{:S(2)}, u32[]{:S(2)}) collective-permute-start(bf16[2,2,4096]{2,0,1:T(2,128)(2,1)S(1)} %copy.15), channel_id=1, source_target_pairs={{0,128},{8,136},{16,144},{24,152},{32,160},{40,168},{48,176},{56,1... | collective-permute-start | bytes 98312 | tf_op jit(solution)/shard_map/ppermute | solution.py:42
  66.8 4.5 %collective-permute-done.7 = bf16[4,2,4096]{2,0,1:T(4,128)(2,1)S(1)} collective-permute-done((bf16[4,2,4096]{2,0,1:T(4,128)(2,1)S(1)}, bf16[4,2,4096]{2,0,1:T(4,128)(2,1)S(1)}, u32[]{:S(2)}, u32[]{:S(2)}) %collective-permute-start.7) | collective-permute-done | bytes 65568 | tf_op jit(solution)/shard_map/ppermute | solution.py:42
  72.8 5.2 %collective-permute-done.8 = bf16[8,2,4096]{2,0,1:T(8,128)(2,1)S(1)} collective-permute-done((bf16[8,2,4096]{2,0,1:T(8,128)(2,1)S(1)}, bf16[8,2,4096]{2,0,1:T(8,128)(2,1)S(1)}, u32[]{:S(2)}, u32[]{:S(2)}) %collective-permute-start.8) | collective-permute-done | bytes 131104 | tf_op jit(solution)/shard_map/ppermute | solution.py:42
  78.9 5.6 %collective-permute-done.9 = bf16[16,2,4096]{2,0,1:T(8,128)(2,1)S(1)} collective-permute-done((bf16[16,2,4096]{2,0,1:T(8,128)(2,1)S(1)}, bf16[16,2,4096]{2,0,1:T(8,128)(2,1)S(1)}, u32[]{:S(2)}, u32[]{:S(2)}) %collective-permute-start.9) | collective-permute-done | bytes 262176 | tf_op jit(solution)/shard_map/ppermute | solution.py:42
  86.8 3.0 %fusion.13 = f32[64,256]{1,0:T(8,128)S(1)} fusion(bf16[2,256,4096]{2,1,0:T(8,128)(2,1)} %param.11, bf16[64,2,4096]{2,0,1:T(8,128)(2,1)S(1)} %maximum_select_fusion, f32[]{:T(128)} %bitcast.7), kind=kOutput, calls=%fused_computation.10 | convolution fusion | flops 134234112 | bytes 2687488 | tf_op jit(solution)/shard_map/qk,rk->qr/dot_general | solution.py:66
  91.6 3.6 %collective-permute-done.11 = f32[64,16]{0,1:T(8,128)S(1)} collective-permute-done((f32[64,16]{0,1:T(8,128)S(1)}, f32[64,16]{0,1:T(8,128)S(1)}, u32[]{:S(2)}, u32[]{:S(2)}) %collective-permute-start.11) | collective-permute-done | bytes 4128 | tf_op jit(solution)/shard_map/ppermute | solution.py:30
  96.7 2.2 %collective-permute-done.12 = f32[64,16]{0,1:T(8,128)S(1)} collective-permute-done((f32[64,16]{0,1:T(8,128)S(1)}, f32[64,16]{0,1:T(8,128)S(1)}, u32[]{:S(2)}, u32[]{:S(2)}) %collective-permute-start.12) | collective-permute-done | bytes 4128 | tf_op jit(solution)/shard_map/ppermute | solution.py:30
  98.9 3.8 %collective-permute-start.13 = (f32[64,16]{0,1:T(8,128)S(1)}, f32[64,16]{0,1:T(8,128)S(1)}, u32[]{:S(2)}, u32[]{:S(2)}) collective-permute-start(f32[64,16]{0,1:T(8,128)S(1)} %add.65), channel_id=1, source_target_pairs={{0,4},{1,5},{2,6},{3,7},{4,0},{5,1},{6,2},{7,3},{8,12},{9,13},{10,... | collective-permute-start | bytes 12296 | tf_op jit(solution)/shard_map/ppermute | solution.py:30
  106.2 2.9 %collective-permute-done.15 = f32[64,16]{0,1:T(8,128)S(1)} collective-permute-done((f32[64,16]{0,1:T(8,128)S(1)}, f32[64,16]{0,1:T(8,128)S(1)}, u32[]{:S(2)}, u32[]{:S(2)}) %collective-permute-start.15) | collective-permute-done | bytes 4128 | tf_op jit(solution)/shard_map/ppermute | solution.py:30
  110.3 3.9 %collective-permute-done.16 = f32[64,16]{0,1:T(8,128)S(1)} collective-permute-done((f32[64,16]{0,1:T(8,128)S(1)}, f32[64,16]{0,1:T(8,128)S(1)}, u32[]{:S(2)}, u32[]{:S(2)}) %collective-permute-start.16) | collective-permute-done | bytes 4128 | tf_op jit(solution)/shard_map/ppermute | solution.py:30
  114.3 2.0 %collective-permute-start.17 = (f32[64,16]{0,1:T(8,128)S(1)}, f32[64,16]{0,1:T(8,128)S(1)}, u32[]{:S(2)}, u32[]{:S(2)}) collective-permute-start(f32[64,16]{0,1:T(8,128)S(1)} %add.69), channel_id=1, source_target_pairs={{0,64},{8,72},{16,80},{24,88},{32,96},{40,104},{48,112},{56,120},{... | collective-permute-start | bytes 12296 | tf_op jit(solution)/shard_map/ppermute | solution.py:30
  116.3 2.5 %collective-permute-done.17 = f32[64,16]{0,1:T(8,128)S(1)} collective-permute-done((f32[64,16]{0,1:T(8,128)S(1)}, f32[64,16]{0,1:T(8,128)S(1)}, u32[]{:S(2)}, u32[]{:S(2)}) %collective-permute-start.17) | collective-permute-done | bytes 4128 | tf_op jit(solution)/shard_map/ppermute | solution.py:30
  118.8 5.9 %collective-permute-start.18 = (f32[64,16]{0,1:T(8,128)S(1)}, f32[64,16]{0,1:T(8,128)S(1)}, u32[]{:S(2)}, u32[]{:S(2)}) collective-permute-start(f32[64,16]{0,1:T(8,128)S(1)} %add.70), channel_id=1, source_target_pairs={{0,128},{8,136},{16,144},{24,152},{32,160},{40,168},{48,176},{56,1... | collective-permute-start | bytes 12296 | tf_op jit(solution)/shard_map/ppermute | solution.py:30
  (62 shorter events, 24.4 us)
Async XLA Ops:
  0.6 4.5 %copy-start = (bf16[2,2,384,512]{3,2,1,0:T(8,128)(2,1)S(1)}, bf16[2,2,384,512]{3,2,1,0:T(8,128)(2,1)}, u32[]{:S(2)}) copy-start(bf16[2,2,384,512]{3,2,1,0:T(8,128)(2,1)} %param.8) | copy-start | bytes 4718596
  0.7 4.5 %copy-start.1 = (bf16[512,64]{0,1:T(8,128)(2,1)S(1)}, bf16[512,64]{0,1:T(8,128)(2,1)}, u32[]{:S(2)}) copy-start(bf16[512,64]{0,1:T(8,128)(2,1)} %param.10) | copy-start | bytes 196612
  6.0 13.9 %collective-permute-start = (f32[2,2,192,128]{2,3,1,0:T(8,128)S(1)}, f32[2,2,192,128]{2,3,1,0:T(8,128)S(1)}, u32[]{:S(2)}, u32[]{:S(2)}) collective-permute-start(f32[2,2,192,128]{2,3,1,0:T(8,128)S(1)} %fusion.16), channel_id=1, source_target_pairs={{0,1},{1,0},{2,3},{3,2},{4,5},{5,4},{6,7},{7,6},{8,9},{9,8},{10,11... | collective-permute-start | bytes 1179656 | tf_op jit(solution)/shard_map/ppermute | solution.py:24
  20.3 7.5 %collective-permute-start.1 = (f32[2,2,96,128]{2,3,1,0:T(8,128)S(1)}, f32[2,2,96,128]{2,3,1,0:T(8,128)S(1)}, u32[]{:S(2)}, u32[]{:S(2)}) collective-permute-start(f32[2,2,96,128]{2,3,1,0:T(8,128)S(1)} %constant_dynamic-slice_fusion.1), channel_id=1, source_target_pairs={{0,2},{1,3},{2,0},{3,1},{4,6},{5,7},{6,4},{7,5},{8,10},{9,11},{10,... | collective-permute-start | bytes 589832 | tf_op jit(solution)/shard_map/ppermute | solution.py:24
  28.0 8.1 %collective-permute-start.2 = (f32[2,2,48,128]{2,3,1,0:T(8,128)S(1)}, f32[2,2,48,128]{2,3,1,0:T(8,128)S(1)}, u32[]{:S(2)}, u32[]{:S(2)}) collective-permute-start(f32[2,2,48,128]{2,3,1,0:T(8,128)S(1)} %constant_dynamic-slice_fusion), channel_id=1, source_target_pairs={{0,4},{1,5},{2,6},{3,7},{4,0},{5,1},{6,2},{7,3},{8,12},{9,13},{10,... | collective-permute-start | bytes 294920 | tf_op jit(solution)/shard_map/ppermute | solution.py:24
  36.3 6.6 %collective-permute-start.3 = (bf16[2,2,48,128]{2,3,1,0:T(8,128)(2,1)S(1)}, bf16[2,2,48,128]{2,3,1,0:T(8,128)(2,1)S(1)}, u32[]{:S(2)}, u32[]{:S(2)}) collective-permute-start(bf16[2,2,48,128]{2,3,1,0:T(8,128)(2,1)S(1)} %add_convert_fusion), channel_id=1, source_target_pairs={{0,4},{1,5},{2,6},{3,7},{4,0},{5,1},{6,2},{7,3},{8,12},{9,13},{10,... | collective-permute-start | bytes 147464 | tf_op jit(solution)/shard_map/ppermute | solution.py:42
  43.0 5.1 %collective-permute-start.4 = (bf16[2,2,96,128]{2,3,1,0:T(8,128)(2,1)S(1)}, bf16[2,2,96,128]{2,3,1,0:T(8,128)(2,1)S(1)}, u32[]{:S(2)}, u32[]{:S(2)}) collective-permute-start(bf16[2,2,96,128]{2,3,1,0:T(8,128)(2,1)S(1)} %maximum_select_fusion.5), channel_id=1, source_target_pairs={{0,2},{1,3},{2,0},{3,1},{4,6},{5,7},{6,4},{7,5},{8,10},{9,11},{10,... | collective-permute-start | bytes 294920 | tf_op jit(solution)/shard_map/ppermute | solution.py:42
  48.3 6.5 %collective-permute-start.5 = (bf16[2,2,192,128]{2,3,1,0:T(8,128)(2,1)S(1)}, bf16[2,2,192,128]{2,3,1,0:T(8,128)(2,1)S(1)}, u32[]{:S(2)}, u32[]{:S(2)}) collective-permute-start(bf16[2,2,192,128]{2,3,1,0:T(8,128)(2,1)S(1)} %maximum_select_fusion.3), channel_id=1, source_target_pairs={{0,1},{1,0},{2,3},{3,2},{4,5},{5,4},{6,7},{7,6},{8,9},{9,8},{10,11... | collective-permute-start | bytes 589832 | tf_op jit(solution)/shard_map/ppermute | solution.py:42
  50.2 34.5 %copy-start.2 = (f32[2]{0:T(128)S(1)}, f32[2]{0:T(128)}, u32[]{:S(2)}) copy-start(f32[2]{0:T(128)} %param.12) | copy-start | bytes 28
  55.5 9.8 %collective-permute-start.6 = (bf16[2,2,4096]{2,0,1:T(2,128)(2,1)S(1)}, bf16[2,2,4096]{2,0,1:T(2,128)(2,1)S(1)}, u32[]{:S(2)}, u32[]{:S(2)}) collective-permute-start(bf16[2,2,4096]{2,0,1:T(2,128)(2,1)S(1)} %copy.15), channel_id=1, source_target_pairs={{0,128},{8,136},{16,144},{24,152},{32,160},{40,168},{48,176},{56,1... | collective-permute-start | bytes 98312 | tf_op jit(solution)/shard_map/ppermute | solution.py:42
  65.4 6.0 %collective-permute-start.7 = (bf16[4,2,4096]{2,0,1:T(4,128)(2,1)S(1)}, bf16[4,2,4096]{2,0,1:T(4,128)(2,1)S(1)}, u32[]{:S(2)}, u32[]{:S(2)}) collective-permute-start(bf16[4,2,4096]{2,0,1:T(4,128)(2,1)S(1)} %maximum_select_fusion.7), channel_id=1, source_target_pairs={{0,64},{8,72},{16,80},{24,88},{32,96},{40,104},{48,112},{56,120},{... | collective-permute-start | bytes 196616 | tf_op jit(solution)/shard_map/ppermute | solution.py:42
  71.4 6.6 %collective-permute-start.8 = (bf16[8,2,4096]{2,0,1:T(8,128)(2,1)S(1)}, bf16[8,2,4096]{2,0,1:T(8,128)(2,1)S(1)}, u32[]{:S(2)}, u32[]{:S(2)}) collective-permute-start(bf16[8,2,4096]{2,0,1:T(8,128)(2,1)S(1)} %maximum_select_fusion.6), channel_id=1, source_target_pairs={{0,32},{8,40},{16,48},{24,56},{32,0},{40,8},{48,16},{56,24},{64,96... | collective-permute-start | bytes 393224 | tf_op jit(solution)/shard_map/ppermute | solution.py:42
  78.0 6.5 %collective-permute-start.9 = (bf16[16,2,4096]{2,0,1:T(8,128)(2,1)S(1)}, bf16[16,2,4096]{2,0,1:T(8,128)(2,1)S(1)}, u32[]{:S(2)}, u32[]{:S(2)}) collective-permute-start(bf16[16,2,4096]{2,0,1:T(8,128)(2,1)S(1)} %maximum_select_fusion.4), channel_id=1, source_target_pairs={{0,16},{8,24},{16,0},{24,8},{32,48},{40,56},{48,32},{56,40},{64,80... | collective-permute-start | bytes 786440 | tf_op jit(solution)/shard_map/ppermute | solution.py:42
  84.6 2.0 %collective-permute-start.10 = (bf16[32,2,4096]{2,0,1:T(8,128)(2,1)S(1)}, bf16[32,2,4096]{2,0,1:T(8,128)(2,1)S(1)}, u32[]{:S(2)}, u32[]{:S(2)}) collective-permute-start(bf16[32,2,4096]{2,0,1:T(8,128)(2,1)S(1)} %maximum_select_fusion.1), channel_id=1, source_target_pairs={{0,8},{8,0},{16,24},{24,16},{32,40},{40,32},{48,56},{56,48},{64,72... | collective-permute-start | bytes 1572872 | tf_op jit(solution)/shard_map/ppermute | solution.py:42
  85.3 4.5 %copy-start.4 = (bf16[2,256,4096]{2,1,0:T(8,128)(2,1)S(1)}, bf16[2,256,4096]{2,1,0:T(8,128)(2,1)}, u32[]{:S(2)}) copy-start(bf16[2,256,4096]{2,1,0:T(8,128)(2,1)} %param.11) | copy-start | bytes 12582916
  89.8 1.4 %copy-start.3 = (s32[256]{0:T(256)S(1)}, s32[256]{0:T(256)}, u32[]{:S(2)}) copy-start(s32[256]{0:T(256)} %param.13) | copy-start | bytes 3076
  91.6 3.7 %collective-permute-start.11 = (f32[64,16]{0,1:T(8,128)S(1)}, f32[64,16]{0,1:T(8,128)S(1)}, u32[]{:S(2)}, u32[]{:S(2)}) collective-permute-start(f32[64,16]{0,1:T(8,128)S(1)} %fusion.23), channel_id=1, source_target_pairs={{0,1},{1,0},{2,3},{3,2},{4,5},{5,4},{6,7},{7,6},{8,9},{9,8},{10,11... | collective-permute-start | bytes 12296 | tf_op jit(solution)/shard_map/ppermute | solution.py:30
  95.2 3.7 %collective-permute-start.12 = (f32[64,16]{0,1:T(8,128)S(1)}, f32[64,16]{0,1:T(8,128)S(1)}, u32[]{:S(2)}, u32[]{:S(2)}) collective-permute-start(f32[64,16]{0,1:T(8,128)S(1)} %add.64), channel_id=1, source_target_pairs={{0,2},{1,3},{2,0},{3,1},{4,6},{5,7},{6,4},{7,5},{8,10},{9,11},{10,... | collective-permute-start | bytes 12296 | tf_op jit(solution)/shard_map/ppermute | solution.py:30
  98.9 5.4 %collective-permute-start.13 = (f32[64,16]{0,1:T(8,128)S(1)}, f32[64,16]{0,1:T(8,128)S(1)}, u32[]{:S(2)}, u32[]{:S(2)}) collective-permute-start(f32[64,16]{0,1:T(8,128)S(1)} %add.65), channel_id=1, source_target_pairs={{0,4},{1,5},{2,6},{3,7},{4,0},{5,1},{6,2},{7,3},{8,12},{9,13},{10,... | collective-permute-start | bytes 12296 | tf_op jit(solution)/shard_map/ppermute | solution.py:30
  104.3 1.2 collective-permute-start.14
  105.5 3.7 %collective-permute-start.15 = (f32[64,16]{0,1:T(8,128)S(1)}, f32[64,16]{0,1:T(8,128)S(1)}, u32[]{:S(2)}, u32[]{:S(2)}) collective-permute-start(f32[64,16]{0,1:T(8,128)S(1)} %add.67), channel_id=1, source_target_pairs={{0,16},{8,24},{16,0},{24,8},{32,48},{40,56},{48,32},{56,40},{64,80... | collective-permute-start | bytes 12296 | tf_op jit(solution)/shard_map/ppermute | solution.py:30
  109.1 5.2 %collective-permute-start.16 = (f32[64,16]{0,1:T(8,128)S(1)}, f32[64,16]{0,1:T(8,128)S(1)}, u32[]{:S(2)}, u32[]{:S(2)}) collective-permute-start(f32[64,16]{0,1:T(8,128)S(1)} %add.68), channel_id=1, source_target_pairs={{0,32},{8,40},{16,48},{24,56},{32,0},{40,8},{48,16},{56,24},{64,96... | collective-permute-start | bytes 12296 | tf_op jit(solution)/shard_map/ppermute | solution.py:30
  114.3 4.5 %collective-permute-start.17 = (f32[64,16]{0,1:T(8,128)S(1)}, f32[64,16]{0,1:T(8,128)S(1)}, u32[]{:S(2)}, u32[]{:S(2)}) collective-permute-start(f32[64,16]{0,1:T(8,128)S(1)} %add.69), channel_id=1, source_target_pairs={{0,64},{8,72},{16,80},{24,88},{32,96},{40,104},{48,112},{56,120},{... | collective-permute-start | bytes 12296 | tf_op jit(solution)/shard_map/ppermute | solution.py:30
  118.8 7.6 %collective-permute-start.18 = (f32[64,16]{0,1:T(8,128)S(1)}, f32[64,16]{0,1:T(8,128)S(1)}, u32[]{:S(2)}, u32[]{:S(2)}) collective-permute-start(f32[64,16]{0,1:T(8,128)S(1)} %add.70), channel_id=1, source_target_pairs={{0,128},{8,136},{16,144},{24,152},{32,160},{40,168},{48,176},{56,1... | collective-permute-start | bytes 12296 | tf_op jit(solution)/shard_map/ppermute | solution.py:30

commit v4 on v3

--- a/solution.py
+++ b/solution.py
@@ -54,8 +54,13 @@
     part_in = jnp.einsum("cesf,fr->cesr", activations, proj_in, preferred_element_type=jnp.float32)
     part_out = jnp.einsum("cesf,fr->cesr", out_grads, proj_out, preferred_element_type=jnp.float32)
     stacked = jnp.concatenate([part_in, part_out], axis=3)
-    summed = _halving_sum(stacked, "mp", n_mp, 2, list(range(mp_bits)))
-    low = _doubling_gather(summed.astype(jnp.bfloat16), "mp", n_mp, 2, list(reversed(range(mp_bits))))
+    c, e, t, r = stacked.shape
+    shares = lax.all_to_all(
+        stacked.reshape(c, e, n_mp, t // n_mp, r), "mp", 2, 2, tiled=True
+    )
+    summed = shares.sum(2).astype(jnp.bfloat16)
+    copies = jnp.broadcast_to(summed[:, :, None], (c, e, n_mp, t // n_mp, r))
+    low = lax.all_to_all(copies, "mp", 2, 2, tiled=True).reshape(c, e, t, r)
     outer = jnp.einsum(
         "cesa,cesb->ecab", low[..., :rank], low[..., rank:], preferred_element_type=jnp.float32
     )

time: 128 us -> 108 us (0.84)
  waiting for transfers between devices: 71.6 us -> 41.6 us
  blocking collectives: 0 us -> 29.1 us
  starting transfers between devices: 40.2 us -> 22.3 us
  other arithmetic: 2.04 us -> 0.71 us
    all_to_all x0 -> x2, blocking collectives: none -> 29.1 us  [the longest x1 18.4 us: shards(): lax.all_to_all(stacked.reshape(c, e, n_mp, t // n_mp, r), 'mp', 2, 2, til...]
    ppermute x3 -> x0, waiting for transfers between devices: 22.8 us -> none  [_halving_sum(): x = keep + lax.ppermute(send, axis, _swap(n, bit))]
    ppermute x8 -> x5, waiting for transfers between devices: 30 us -> 18.4 us  [_doubling_gather(): x = _join(x, lax.ppermute(x, axis, _swap(n, bit)), upper, dim)]
    ppermute x3 -> x0, starting transfers between devices: 6.69 us -> none  [_halving_sum(): x = keep + lax.ppermute(send, axis, _swap(n, bit))]
    ppermute x8 -> x5, starting transfers between devices: 18.2 us -> 11.8 us  [_doubling_gather(): x = _join(x, lax.ppermute(x, axis, _swap(n, bit)), upper, dim)]
    ppermute x8, starting transfers between devices: 15.2 us -> 10.6 us  [_butterfly_sum(): x = x + lax.ppermute(x, axis, _swap(n, bit))]
    ppermute x8, waiting for transfers between devices: 18.8 us -> 23.2 us  [_butterfly_sum(): x = x + lax.ppermute(x, axis, _swap(n, bit))]
  transfers between devices with their start and end apart: 19 -> 13, of which waited for: 19 -> 13; matrix products, arithmetic and copies ran while one was open for 1% -> 1% of each run, Pallas kernels for 0% -> 0%
where the time goes in v4:
time: 108 us
  waiting for transfers between devices  41.6 us (39%)
  blocking collectives  29.1 us (27%)
  starting transfers between devices  22.3 us (21%)
  matrix products  10 us (9%)
  local copies, waits for them, and re-layouts  2.85 us (3%)
    ppermute x8, waiting for transfers between devices, _butterfly_sum(): x = x + lax.ppermute(x, axis, _swap(n, bit))  23.2 us
    all_to_all x1, blocking collectives, shards(): lax.all_to_all(stacked.reshape(c, e, n_mp, t // n_mp, r), 'mp', 2, 2, til...  18.4 us
    ppermute x5, waiting for transfers between devices, _doubling_gather(): x = _join(x, lax.ppermute(x, axis, _swap(n, bit)), upper, dim)  18.4 us
    ppermute x5, starting transfers between devices, _doubling_gather(): x = _join(x, lax.ppermute(x, axis, _swap(n, bit)), upper, dim)  11.8 us
    all_to_all x1, blocking collectives, shards(): low = lax.all_to_all(copies, 'mp', 2, 2, tiled=True).reshape(c, e, t, r)  10.7 us
    ppermute x8, starting transfers between devices, _butterfly_sum(): x = x + lax.ppermute(x, axis, _swap(n, bit))  10.6 us
    dot_general x1, matrix products, shards(): jnp.einsum('cesf,fr->cesr', activations, proj_in, preferred_element_type=...  4.44 us
    dot_general x1, matrix products, shards(): jnp.einsum('qk,rk->qr', piece[:, 1], store[1], preferred_element_type=jnp...  3 us
  transfers between devices with their start and end apart: 13, of which 13 were waited for; matrix products, arithmetic and copies ran while one was open for 1% of the time, Pallas kernels for 0%

profile of v4, /device:TPU:24, one launch (start us, length us, event | category | flops | bytes accessed | tf_op | source)
XLA Modules:
  0.0 107.5 jit_solution(6453061630637621905)
XLA Ops:
  0.7 4.4 %fusion.18 = f32[2,2,384,64]{2,3,1,0:T(8,128)S(1)} fusion(bf16[2,2,384,1792]{3,2,1,0:T(8,128)(2,1)} %param.7, bf16[1792,64]{0,1:T(8,128)(2,1)} %param.9), kind=kOutput, calls=%fused_computation.19 | convolution fusion | flops 352321536 | bytes 6127616 | tf_op jit(solution)/shard_map/cesf,fr->cesr/dot_general | solution.py:54
  6.1 18.4 %all_to_all.10 = f32[2,2,8,48,128]{4,3,1,0,2:T(8,128)S(1)} all-to-all(f32[2,2,8,48,128]{4,3,1,0,2:T(8,128)S(1)} %copy.22), channel_id=1, replica_groups=mesh['dp'=32,'mp'=8] {'mp'}, dimensions={2} | all-to-all | bytes 1572864 | tf_op jit(solution)/shard_map/all_to_all | solution.py:58
  24.7 10.7 %all_to_all.11 = bf16[2,2,8,48,128]{4,3,1,0,2:T(8,128)(2,1)S(1)} all-to-all(bf16[2,2,8,48,128]{4,3,1,0,2:T(8,128)(2,1)S(1)} %broadcast_in_dim.2), channel_id=1, replica_groups=mesh['dp'=32,'mp'=8] {'mp'}, dimensions={2} | all-to-all | bytes 786432 | tf_op jit(solution)/shard_map/all_to_all | solution.py:63
  36.0 6.4 %collective-permute-start = (bf16[2,2,4096]{2,0,1:T(2,128)(2,1)S(1)}, bf16[2,2,4096]{2,0,1:T(2,128)(2,1)S(1)}, u32[]{:S(2)}, u32[]{:S(2)}) collective-permute-start(bf16[2,2,4096]{2,0,1:T(2,128)(2,1)S(1)} %copy.26), channel_id=1, source_target_pairs={{0,128},{8,136},{16,144},{24,152},{32,160},{40,168},{48,176},{56,1... | collective-permute-start | bytes 98312 | tf_op jit(solution)/shard_map/ppermute | solution.py:42
  42.4 1.9 %collective-permute-done = bf16[2,2,4096]{2,0,1:T(2,128)(2,1)S(1)} collective-permute-done((bf16[2,2,4096]{2,0,1:T(2,128)(2,1)S(1)}, bf16[2,2,4096]{2,0,1:T(2,128)(2,1)S(1)}, u32[]{:S(2)}, u32[]{:S(2)}) %collective-permute-start) | collective-permute-done | bytes 32800 | tf_op jit(solution)/shard_map/ppermute | solution.py:42
  44.4 3.1 %collective-permute-start.1 = (bf16[4,2,4096]{2,0,1:T(4,128)(2,1)S(1)}, bf16[4,2,4096]{2,0,1:T(4,128)(2,1)S(1)}, u32[]{:S(2)}, u32[]{:S(2)}) collective-permute-start(bf16[4,2,4096]{2,0,1:T(4,128)(2,1)S(1)} %maximum_select_fusion.4), channel_id=1, source_target_pairs={{0,64},{8,72},{16,80},{24,88},{32,96},{40,104},{48,112},{56,120},{... | collective-permute-start | bytes 196616 | tf_op jit(solution)/shard_map/ppermute | solution.py:42
  47.6 2.9 %collective-permute-done.1 = bf16[4,2,4096]{2,0,1:T(4,128)(2,1)S(1)} collective-permute-done((bf16[4,2,4096]{2,0,1:T(4,128)(2,1)S(1)}, bf16[4,2,4096]{2,0,1:T(4,128)(2,1)S(1)}, u32[]{:S(2)}, u32[]{:S(2)}) %collective-permute-start.1) | collective-permute-done | bytes 65568 | tf_op jit(solution)/shard_map/ppermute | solution.py:42
  50.6 1.3 %collective-permute-start.2 = (bf16[8,2,4096]{2,0,1:T(8,128)(2,1)S(1)}, bf16[8,2,4096]{2,0,1:T(8,128)(2,1)S(1)}, u32[]{:S(2)}, u32[]{:S(2)}) collective-permute-start(bf16[8,2,4096]{2,0,1:T(8,128)(2,1)S(1)} %maximum_select_fusion.3), channel_id=1, source_target_pairs={{0,32},{8,40},{16,48},{24,56},{32,0},{40,8},{48,16},{56,24},{64,96... | collective-permute-start | bytes 393224 | tf_op jit(solution)/shard_map/ppermute | solution.py:42
  52.0 6.6 %collective-permute-done.2 = bf16[8,2,4096]{2,0,1:T(8,128)(2,1)S(1)} collective-permute-done((bf16[8,2,4096]{2,0,1:T(8,128)(2,1)S(1)}, bf16[8,2,4096]{2,0,1:T(8,128)(2,1)S(1)}, u32[]{:S(2)}, u32[]{:S(2)}) %collective-permute-start.2) | collective-permute-done | bytes 131104 | tf_op jit(solution)/shard_map/ppermute | solution.py:42
  59.5 5.6 %collective-permute-done.3 = bf16[16,2,4096]{2,0,1:T(8,128)(2,1)S(1)} collective-permute-done((bf16[16,2,4096]{2,0,1:T(8,128)(2,1)S(1)}, bf16[16,2,4096]{2,0,1:T(8,128)(2,1)S(1)}, u32[]{:S(2)}, u32[]{:S(2)}) %collective-permute-start.3) | collective-permute-done | bytes 262176 | tf_op jit(solution)/shard_map/ppermute | solution.py:42
  65.9 1.3 %collective-permute-done.4 = bf16[32,2,4096]{2,0,1:T(8,128)(2,1)S(1)} collective-permute-done((bf16[32,2,4096]{2,0,1:T(8,128)(2,1)S(1)}, bf16[32,2,4096]{2,0,1:T(8,128)(2,1)S(1)}, u32[]{:S(2)}, u32[]{:S(2)}) %collective-permute-start.4) | collective-permute-done | bytes 524320 | tf_op jit(solution)/shard_map/ppermute | solution.py:42
  67.4 3.0 %fusion.13 = f32[64,256]{1,0:T(8,128)S(1)} fusion(bf16[2,256,4096]{2,1,0:T(8,128)(2,1)} %param.11, bf16[64,2,4096]{2,0,1:T(8,128)(2,1)S(1)} %maximum_select_fusion, f32[]{:T(128)} %bitcast.9), kind=kOutput, calls=%fused_computation.10 | convolution fusion | flops 134234112 | bytes 2687488 | tf_op jit(solution)/shard_map/qk,rk->qr/dot_general | solution.py:71
  70.4 1.4 %fusion.10 = f32[64,256]{1,0:T(8,128)S(1)} fusion(f32[64,256]{1,0:T(8,128)S(1)} %fusion.13, bf16[2,256,4096]{2,1,0:T(8,128)(2,1)S(1)} %copy-done.4, bf16[64,2,4096]{2,0,1:T(8,128)(2,1)S(1)} %maximum_select_fusion, f32[]{:T(128)} %bitcast), kind=kOutput, calls=%fused_computation.9 | convolution fusion | flops 134250496 | bytes 2752516 | tf_op jit(solution)/shard_map/qk,rk->qr/dot_general | solution.py:70
  72.2 3.6 %collective-permute-done.5 = f32[64,16]{0,1:T(8,128)S(1)} collective-permute-done((f32[64,16]{0,1:T(8,128)S(1)}, f32[64,16]{0,1:T(8,128)S(1)}, u32[]{:S(2)}, u32[]{:S(2)}) %collective-permute-start.5) | collective-permute-done | bytes 4128 | tf_op jit(solution)/shard_map/ppermute | solution.py:30
  76.1 3.4 %collective-permute-done.6 = f32[64,16]{0,1:T(8,128)S(1)} collective-permute-done((f32[64,16]{0,1:T(8,128)S(1)}, f32[64,16]{0,1:T(8,128)S(1)}, u32[]{:S(2)}, u32[]{:S(2)}) %collective-permute-start.6) | collective-permute-done | bytes 4128 | tf_op jit(solution)/shard_map/ppermute | solution.py:30
  79.5 1.2 %collective-permute-start.7 = (f32[64,16]{0,1:T(8,128)S(1)}, f32[64,16]{0,1:T(8,128)S(1)}, u32[]{:S(2)}, u32[]{:S(2)}) collective-permute-start(f32[64,16]{0,1:T(8,128)S(1)} %add.29), channel_id=1, source_target_pairs={{0,4},{1,5},{2,6},{3,7},{4,0},{5,1},{6,2},{7,3},{8,12},{9,13},{10,... | collective-permute-start | bytes 12296 | tf_op jit(solution)/shard_map/ppermute | solution.py:30
  80.7 4.0 %collective-permute-done.7 = f32[64,16]{0,1:T(8,128)S(1)} collective-permute-done((f32[64,16]{0,1:T(8,128)S(1)}, f32[64,16]{0,1:T(8,128)S(1)}, u32[]{:S(2)}, u32[]{:S(2)}) %collective-permute-start.7) | collective-permute-done | bytes 4128 | tf_op jit(solution)/shard_map/ppermute | solution.py:30
  86.6 2.9 %collective-permute-done.9 = f32[64,16]{0,1:T(8,128)S(1)} collective-permute-done((f32[64,16]{0,1:T(8,128)S(1)}, f32[64,16]{0,1:T(8,128)S(1)}, u32[]{:S(2)}, u32[]{:S(2)}) %collective-permute-start.9) | collective-permute-done | bytes 4128 | tf_op jit(solution)/shard_map/ppermute | solution.py:30
  89.5 1.2 %collective-permute-start.10 = (f32[64,16]{0,1:T(8,128)S(1)}, f32[64,16]{0,1:T(8,128)S(1)}, u32[]{:S(2)}, u32[]{:S(2)}) collective-permute-start(f32[64,16]{0,1:T(8,128)S(1)} %add.32), channel_id=1, source_target_pairs={{0,32},{8,40},{16,48},{24,56},{32,0},{40,8},{48,16},{56,24},{64,96... | collective-permute-start | bytes 12296 | tf_op jit(solution)/shard_map/ppermute | solution.py:30
  90.7 3.9 %collective-permute-done.10 = f32[64,16]{0,1:T(8,128)S(1)} collective-permute-done((f32[64,16]{0,1:T(8,128)S(1)}, f32[64,16]{0,1:T(8,128)S(1)}, u32[]{:S(2)}, u32[]{:S(2)}) %collective-permute-start.10) | collective-permute-done | bytes 4128 | tf_op jit(solution)/shard_map/ppermute | solution.py:30
  94.6 1.7 %collective-permute-start.11 = (f32[64,16]{0,1:T(8,128)S(1)}, f32[64,16]{0,1:T(8,128)S(1)}, u32[]{:S(2)}, u32[]{:S(2)}) collective-permute-start(f32[64,16]{0,1:T(8,128)S(1)} %add.33), channel_id=1, source_target_pairs={{0,64},{8,72},{16,80},{24,88},{32,96},{40,104},{48,112},{56,120},{... | collective-permute-start | bytes 12296 | tf_op jit(solution)/shard_map/ppermute | solution.py:30
  96.4 2.8 %collective-permute-done.11 = f32[64,16]{0,1:T(8,128)S(1)} collective-permute-done((f32[64,16]{0,1:T(8,128)S(1)}, f32[64,16]{0,1:T(8,128)S(1)}, u32[]{:S(2)}, u32[]{:S(2)}) %collective-permute-start.11) | collective-permute-done | bytes 4128 | tf_op jit(solution)/shard_map/ppermute | solution.py:30
  99.2 5.4 %collective-permute-start.12 = (f32[64,16]{0,1:T(8,128)S(1)}, f32[64,16]{0,1:T(8,128)S(1)}, u32[]{:S(2)}, u32[]{:S(2)}) collective-permute-start(f32[64,16]{0,1:T(8,128)S(1)} %add.34), channel_id=1, source_target_pairs={{0,128},{8,136},{16,144},{24,152},{32,160},{40,168},{48,176},{56,1... | collective-permute-start | bytes 12296 | tf_op jit(solution)/shard_map/ppermute | solution.py:30
  105.3 1.5 %collective-permute-done.12 = f32[64,16]{0,1:T(8,128)S(1)} collective-permute-done((f32[64,16]{0,1:T(8,128)S(1)}, f32[64,16]{0,1:T(8,128)S(1)}, u32[]{:S(2)}, u32[]{:S(2)}) %collective-permute-start.12) | collective-permute-done | bytes 4128 | tf_op jit(solution)/shard_map/ppermute | solution.py:30
  (49 shorter events, 7.9 us)
Async XLA Ops:
  0.6 4.5 %copy-start = (bf16[2,2,384,512]{3,2,1,0:T(8,128)(2,1)S(1)}, bf16[2,2,384,512]{3,2,1,0:T(8,128)(2,1)}, u32[]{:S(2)}) copy-start(bf16[2,2,384,512]{3,2,1,0:T(8,128)(2,1)} %param.8) | copy-start | bytes 4718596
  0.6 4.5 %copy-start.1 = (bf16[512,64]{0,1:T(8,128)(2,1)S(1)}, bf16[512,64]{0,1:T(8,128)(2,1)}, u32[]{:S(2)}) copy-start(bf16[512,64]{0,1:T(8,128)(2,1)} %param.10) | copy-start | bytes 196612
  35.4 29.9 %copy-start.2 = (f32[2]{0:T(128)S(1)}, f32[2]{0:T(128)}, u32[]{:S(2)}) copy-start(f32[2]{0:T(128)} %param.12) | copy-start | bytes 28
  36.0 8.3 %collective-permute-start = (bf16[2,2,4096]{2,0,1:T(2,128)(2,1)S(1)}, bf16[2,2,4096]{2,0,1:T(2,128)(2,1)S(1)}, u32[]{:S(2)}, u32[]{:S(2)}) collective-permute-start(bf16[2,2,4096]{2,0,1:T(2,128)(2,1)S(1)} %copy.26), channel_id=1, source_target_pairs={{0,128},{8,136},{16,144},{24,152},{32,160},{40,168},{48,176},{56,1... | collective-permute-start | bytes 98312 | tf_op jit(solution)/shard_map/ppermute | solution.py:42
  44.4 6.1 %collective-permute-start.1 = (bf16[4,2,4096]{2,0,1:T(4,128)(2,1)S(1)}, bf16[4,2,4096]{2,0,1:T(4,128)(2,1)S(1)}, u32[]{:S(2)}, u32[]{:S(2)}) collective-permute-start(bf16[4,2,4096]{2,0,1:T(4,128)(2,1)S(1)} %maximum_select_fusion.4), channel_id=1, source_target_pairs={{0,64},{8,72},{16,80},{24,88},{32,96},{40,104},{48,112},{56,120},{... | collective-permute-start | bytes 196616 | tf_op jit(solution)/shard_map/ppermute | solution.py:42
  50.6 8.0 %collective-permute-start.2 = (bf16[8,2,4096]{2,0,1:T(8,128)(2,1)S(1)}, bf16[8,2,4096]{2,0,1:T(8,128)(2,1)S(1)}, u32[]{:S(2)}, u32[]{:S(2)}) collective-permute-start(bf16[8,2,4096]{2,0,1:T(8,128)(2,1)S(1)} %maximum_select_fusion.3), channel_id=1, source_target_pairs={{0,32},{8,40},{16,48},{24,56},{32,0},{40,8},{48,16},{56,24},{64,96... | collective-permute-start | bytes 393224 | tf_op jit(solution)/shard_map/ppermute | solution.py:42
  58.7 6.5 %collective-permute-start.3 = (bf16[16,2,4096]{2,0,1:T(8,128)(2,1)S(1)}, bf16[16,2,4096]{2,0,1:T(8,128)(2,1)S(1)}, u32[]{:S(2)}, u32[]{:S(2)}) collective-permute-start(bf16[16,2,4096]{2,0,1:T(8,128)(2,1)S(1)} %maximum_select_fusion.2), channel_id=1, source_target_pairs={{0,16},{8,24},{16,0},{24,8},{32,48},{40,56},{48,32},{56,40},{64,80... | collective-permute-start | bytes 786440 | tf_op jit(solution)/shard_map/ppermute | solution.py:42
  65.2 2.0 %collective-permute-start.4 = (bf16[32,2,4096]{2,0,1:T(8,128)(2,1)S(1)}, bf16[32,2,4096]{2,0,1:T(8,128)(2,1)S(1)}, u32[]{:S(2)}, u32[]{:S(2)}) collective-permute-start(bf16[32,2,4096]{2,0,1:T(8,128)(2,1)S(1)} %maximum_select_fusion.1), channel_id=1, source_target_pairs={{0,8},{8,0},{16,24},{24,16},{32,40},{40,32},{48,56},{56,48},{64,72... | collective-permute-start | bytes 1572872 | tf_op jit(solution)/shard_map/ppermute | solution.py:42
  65.9 4.5 %copy-start.4 = (bf16[2,256,4096]{2,1,0:T(8,128)(2,1)S(1)}, bf16[2,256,4096]{2,1,0:T(8,128)(2,1)}, u32[]{:S(2)}) copy-start(bf16[2,256,4096]{2,1,0:T(8,128)(2,1)} %param.11) | copy-start | bytes 12582916
  70.4 1.4 %copy-start.3 = (s32[256]{0:T(256)S(1)}, s32[256]{0:T(256)}, u32[]{:S(2)}) copy-start(s32[256]{0:T(256)} %param.13) | copy-start | bytes 3076
  72.2 3.7 %collective-permute-start.5 = (f32[64,16]{0,1:T(8,128)S(1)}, f32[64,16]{0,1:T(8,128)S(1)}, u32[]{:S(2)}, u32[]{:S(2)}) collective-permute-start(f32[64,16]{0,1:T(8,128)S(1)} %fusion.20), channel_id=1, source_target_pairs={{0,1},{1,0},{2,3},{3,2},{4,5},{5,4},{6,7},{7,6},{8,9},{9,8},{10,11... | collective-permute-start | bytes 12296 | tf_op jit(solution)/shard_map/ppermute | solution.py:30
  75.8 3.7 %collective-permute-start.6 = (f32[64,16]{0,1:T(8,128)S(1)}, f32[64,16]{0,1:T(8,128)S(1)}, u32[]{:S(2)}, u32[]{:S(2)}) collective-permute-start(f32[64,16]{0,1:T(8,128)S(1)} %add.28), channel_id=1, source_target_pairs={{0,2},{1,3},{2,0},{3,1},{4,6},{5,7},{6,4},{7,5},{8,10},{9,11},{10,... | collective-permute-start | bytes 12296 | tf_op jit(solution)/shard_map/ppermute | solution.py:30
  79.5 5.2 %collective-permute-start.7 = (f32[64,16]{0,1:T(8,128)S(1)}, f32[64,16]{0,1:T(8,128)S(1)}, u32[]{:S(2)}, u32[]{:S(2)}) collective-permute-start(f32[64,16]{0,1:T(8,128)S(1)} %add.29), channel_id=1, source_target_pairs={{0,4},{1,5},{2,6},{3,7},{4,0},{5,1},{6,2},{7,3},{8,12},{9,13},{10,... | collective-permute-start | bytes 12296 | tf_op jit(solution)/shard_map/ppermute | solution.py:30
  84.7 1.2 %collective-permute-start.8 = (f32[64,16]{0,1:T(8,128)S(1)}, f32[64,16]{0,1:T(8,128)S(1)}, u32[]{:S(2)}, u32[]{:S(2)}) collective-permute-start(f32[64,16]{0,1:T(8,128)S(1)} %add.30), channel_id=1, source_target_pairs={{0,8},{8,0},{16,24},{24,16},{32,40},{40,32},{48,56},{56,48},{64,72... | collective-permute-start | bytes 12296 | tf_op jit(solution)/shard_map/ppermute | solution.py:30
  85.8 3.7 %collective-permute-start.9 = (f32[64,16]{0,1:T(8,128)S(1)}, f32[64,16]{0,1:T(8,128)S(1)}, u32[]{:S(2)}, u32[]{:S(2)}) collective-permute-start(f32[64,16]{0,1:T(8,128)S(1)} %add.31), channel_id=1, source_target_pairs={{0,16},{8,24},{16,0},{24,8},{32,48},{40,56},{48,32},{56,40},{64,80... | collective-permute-start | bytes 12296 | tf_op jit(solution)/shard_map/ppermute | solution.py:30
  89.5 5.2 %collective-permute-start.10 = (f32[64,16]{0,1:T(8,128)S(1)}, f32[64,16]{0,1:T(8,128)S(1)}, u32[]{:S(2)}, u32[]{:S(2)}) collective-permute-start(f32[64,16]{0,1:T(8,128)S(1)} %add.32), channel_id=1, source_target_pairs={{0,32},{8,40},{16,48},{24,56},{32,0},{40,8},{48,16},{56,24},{64,96... | collective-permute-start | bytes 12296 | tf_op jit(solution)/shard_map/ppermute | solution.py:30
  94.6 4.5 %collective-permute-start.11 = (f32[64,16]{0,1:T(8,128)S(1)}, f32[64,16]{0,1:T(8,128)S(1)}, u32[]{:S(2)}, u32[]{:S(2)}) collective-permute-start(f32[64,16]{0,1:T(8,128)S(1)} %add.33), channel_id=1, source_target_pairs={{0,64},{8,72},{16,80},{24,88},{32,96},{40,104},{48,112},{56,120},{... | collective-permute-start | bytes 12296 | tf_op jit(solution)/shard_map/ppermute | solution.py:30
  99.2 7.6 %collective-permute-start.12 = (f32[64,16]{0,1:T(8,128)S(1)}, f32[64,16]{0,1:T(8,128)S(1)}, u32[]{:S(2)}, u32[]{:S(2)}) collective-permute-start(f32[64,16]{0,1:T(8,128)S(1)} %add.34), channel_id=1, source_target_pairs={{0,128},{8,136},{16,144},{24,152},{32,160},{40,168},{48,176},{56,1... | collective-permute-start | bytes 12296 | tf_op jit(solution)/shard_map/ppermute | solution.py:30

commit v5 on v4

--- a/solution.py
+++ b/solution.py
@@ -74,7 +74,8 @@
         jnp.float32
     )
     partial_totals = jnp.dot(scores, member, precision=lax.Precision.HIGHEST)
-    totals = _butterfly_sum(partial_totals, "mp", n_mp, list(range(mp_bits)))
+    copies = jnp.broadcast_to(partial_totals[None], (n_mp,) + partial_totals.shape)
+    totals = lax.all_to_all(copies, "mp", 0, 0, tiled=True).sum(0)
     totals = _butterfly_sum(totals, "dp", n_dp, list(range(dp_bits)))
 
     def natural(x):

time: 108 us -> 106 us (0.981)
  waiting for transfers between devices: 41.6 us -> 30.1 us
  blocking collectives: 29.1 us -> 37.8 us
    ppermute x8 -> x5, waiting for transfers between devices: 23.2 us -> 11.7 us  [_butterfly_sum(): x = x + lax.ppermute(x, axis, _swap(n, bit))]
    all_to_all x0 -> x1, blocking collectives: none -> 8.63 us  [shards(): totals = lax.all_to_all(copies, 'mp', 0, 0, tiled=True).sum(0)]
    ppermute x8 -> x5, starting transfers between devices: 10.6 us -> 9.75 us  [_butterfly_sum(): x = x + lax.ppermute(x, axis, _swap(n, bit))]
  transfers between devices with their start and end apart: 13 -> 10, of which waited for: 13 -> 10; matrix products, arithmetic and copies ran while one was open for 1% -> 1% of each run, Pallas kernels for 0% -> 0%
where the time goes in v5:
time: 106 us; the launch traced here: 105 us
  blocking collectives  37.8 us (36%)
  waiting for transfers between devices  30.1 us (28%)
  starting transfers between devices  21.5 us (20%)
  matrix products  10 us (9%)
  local copies, waits for them, and re-layouts  3.56 us (3%)
  other arithmetic  1.43 us (1%)
    all_to_all x1, blocking collectives, shards(): lax.all_to_all(stacked.reshape(c, e, n_mp, t // n_mp, r), 'mp', 2, 2, til...  18.4 us
    ppermute x5, waiting for transfers between devices, _doubling_gather(): x = _join(x, lax.ppermute(x, axis, _swap(n, bit)), upper, dim)  18.4 us
    ppermute x5, starting transfers between devices, _doubling_gather(): x = _join(x, lax.ppermute(x, axis, _swap(n, bit)), upper, dim)  11.8 us
    ppermute x5, waiting for transfers between devices, _butterfly_sum(): x = x + lax.ppermute(x, axis, _swap(n, bit))  11.7 us
    all_to_all x1, blocking collectives, shards(): low = lax.all_to_all(copies, 'mp', 2, 2, tiled=True).reshape(c, e, t, r)  10.7 us
    ppermute x5, starting transfers between devices, _butterfly_sum(): x = x + lax.ppermute(x, axis, _swap(n, bit))  9.75 us
    all_to_all x1, blocking collectives, shards(): totals = lax.all_to_all(copies, 'mp', 0, 0, tiled=True).sum(0)  8.63 us
    dot_general x1, matrix products, shards(): jnp.einsum('cesf,fr->cesr', activations, proj_in, preferred_element_type=...  4.44 us
  transfers between devices with their start and end apart: 10, of which 10 were waited for; matrix products, arithmetic and copies ran while one was open for 1% of the time, Pallas kernels for 0%

profile of v5, /device:TPU:24, one launch (start us, length us, event | category | flops | bytes accessed | tf_op | source)
XLA Modules:
  0.0 105.3 jit_solution(13246392972064674046)
XLA Ops:
  0.7 4.4 %fusion.18 = f32[2,2,384,64]{2,3,1,0:T(8,128)S(1)} fusion(bf16[2,2,384,1792]{3,2,1,0:T(8,128)(2,1)} %param.7, bf16[1792,64]{0,1:T(8,128)(2,1)} %param.9), kind=kOutput, calls=%fused_computation.19 | convolution fusion | flops 352321536 | bytes 6127616 | tf_op jit(solution)/shard_map/cesf,fr->cesr/dot_general | solution.py:54
  6.1 18.4 %all_to_all.15 = f32[2,2,8,48,128]{4,3,1,0,2:T(8,128)S(1)} all-to-all(f32[2,2,8,48,128]{4,3,1,0,2:T(8,128)S(1)} %copy.33), channel_id=1, replica_groups=mesh['dp'=32,'mp'=8] {'mp'}, dimensions={2} | all-to-all | bytes 1572864 | tf_op jit(solution)/shard_map/all_to_all | solution.py:58
  24.7 10.7 %all_to_all.16 = bf16[2,2,8,48,128]{4,3,1,0,2:T(8,128)(2,1)S(1)} all-to-all(bf16[2,2,8,48,128]{4,3,1,0,2:T(8,128)(2,1)S(1)} %broadcast_in_dim.4), channel_id=1, replica_groups=mesh['dp'=32,'mp'=8] {'mp'}, dimensions={2} | all-to-all | bytes 786432 | tf_op jit(solution)/shard_map/all_to_all | solution.py:63
  36.0 6.4 %collective-permute-start = (bf16[2,2,4096]{2,0,1:T(2,128)(2,1)S(1)}, bf16[2,2,4096]{2,0,1:T(2,128)(2,1)S(1)}, u32[]{:S(2)}, u32[]{:S(2)}) collective-permute-start(bf16[2,2,4096]{2,0,1:T(2,128)(2,1)S(1)} %copy.37), channel_id=1, source_target_pairs={{0,128},{8,136},{16,144},{24,152},{32,160},{40,168},{48,176},{56,1... | collective-permute-start | bytes 98312 | tf_op jit(solution)/shard_map/ppermute | solution.py:42
  42.4 1.9 %collective-permute-done = bf16[2,2,4096]{2,0,1:T(2,128)(2,1)S(1)} collective-permute-done((bf16[2,2,4096]{2,0,1:T(2,128)(2,1)S(1)}, bf16[2,2,4096]{2,0,1:T(2,128)(2,1)S(1)}, u32[]{:S(2)}, u32[]{:S(2)}) %collective-permute-start) | collective-permute-done | bytes 32800 | tf_op jit(solution)/shard_map/ppermute | solution.py:42
  44.4 3.1 %collective-permute-start.1 = (bf16[4,2,4096]{2,0,1:T(4,128)(2,1)S(1)}, bf16[4,2,4096]{2,0,1:T(4,128)(2,1)S(1)}, u32[]{:S(2)}, u32[]{:S(2)}) collective-permute-start(bf16[4,2,4096]{2,0,1:T(4,128)(2,1)S(1)} %maximum_select_fusion.4), channel_id=1, source_target_pairs={{0,64},{8,72},{16,80},{24,88},{32,96},{40,104},{48,112},{56,120},{... | collective-permute-start | bytes 196616 | tf_op jit(solution)/shard_map/ppermute | solution.py:42
  47.6 2.9 %collective-permute-done.1 = bf16[4,2,4096]{2,0,1:T(4,128)(2,1)S(1)} collective-permute-done((bf16[4,2,4096]{2,0,1:T(4,128)(2,1)S(1)}, bf16[4,2,4096]{2,0,1:T(4,128)(2,1)S(1)}, u32[]{:S(2)}, u32[]{:S(2)}) %collective-permute-start.1) | collective-permute-done | bytes 65568 | tf_op jit(solution)/shard_map/ppermute | solution.py:42
  50.6 1.3 %collective-permute-start.2 = (bf16[8,2,4096]{2,0,1:T(8,128)(2,1)S(1)}, bf16[8,2,4096]{2,0,1:T(8,128)(2,1)S(1)}, u32[]{:S(2)}, u32[]{:S(2)}) collective-permute-start(bf16[8,2,4096]{2,0,1:T(8,128)(2,1)S(1)} %maximum_select_fusion.3), channel_id=1, source_target_pairs={{0,32},{8,40},{16,48},{24,56},{32,0},{40,8},{48,16},{56,24},{64,96... | collective-permute-start | bytes 393224 | tf_op jit(solution)/shard_map/ppermute | solution.py:42
  52.0 6.6 %collective-permute-done.2 = bf16[8,2,4096]{2,0,1:T(8,128)(2,1)S(1)} collective-permute-done((bf16[8,2,4096]{2,0,1:T(8,128)(2,1)S(1)}, bf16[8,2,4096]{2,0,1:T(8,128)(2,1)S(1)}, u32[]{:S(2)}, u32[]{:S(2)}) %collective-permute-start.2) | collective-permute-done | bytes 131104 | tf_op jit(solution)/shard_map/ppermute | solution.py:42
  58.7 0.8 collective-permute-start.3
  59.5 5.6 %collective-permute-done.3 = bf16[16,2,4096]{2,0,1:T(8,128)(2,1)S(1)} collective-permute-done((bf16[16,2,4096]{2,0,1:T(8,128)(2,1)S(1)}, bf16[16,2,4096]{2,0,1:T(8,128)(2,1)S(1)}, u32[]{:S(2)}, u32[]{:S(2)}) %collective-permute-start.3) | collective-permute-done | bytes 262176 | tf_op jit(solution)/shard_map/ppermute | solution.py:42
  65.9 1.3 %collective-permute-done.4 = bf16[32,2,4096]{2,0,1:T(8,128)(2,1)S(1)} collective-permute-done((bf16[32,2,4096]{2,0,1:T(8,128)(2,1)S(1)}, bf16[32,2,4096]{2,0,1:T(8,128)(2,1)S(1)}, u32[]{:S(2)}, u32[]{:S(2)}) %collective-permute-start.4) | collective-permute-done | bytes 524320 | tf_op jit(solution)/shard_map/ppermute | solution.py:42
  67.4 3.0 %fusion.13 = f32[64,256]{1,0:T(8,128)S(1)} fusion(bf16[2,256,4096]{2,1,0:T(8,128)(2,1)} %param.11, bf16[64,2,4096]{2,0,1:T(8,128)(2,1)S(1)} %maximum_select_fusion, f32[]{:T(128)} %bitcast.9), kind=kOutput, calls=%fused_computation.10 | convolution fusion | flops 134234112 | bytes 2687488 | tf_op jit(solution)/shard_map/qk,rk->qr/dot_general | solution.py:71
  70.4 1.4 %fusion.10 = f32[64,256]{1,0:T(8,128)S(1)} fusion(f32[64,256]{1,0:T(8,128)S(1)} %fusion.13, bf16[2,256,4096]{2,1,0:T(8,128)(2,1)S(1)} %copy-done.4, bf16[64,2,4096]{2,0,1:T(8,128)(2,1)S(1)} %maximum_select_fusion, f32[]{:T(128)} %bitcast), kind=kOutput, calls=%fused_computation.9 | convolution fusion | flops 134250496 | bytes 2752516 | tf_op jit(solution)/shard_map/qk,rk->qr/dot_general | solution.py:70
  72.3 8.6 %all_to_all.17 = f32[8,1,1024]{2,1,0:T(1,128)S(1)} all-to-all(f32[8,1,1024]{2,1,0:T(1,128)S(1)} %reshape.37), channel_id=1, replica_groups=mesh['dp'=32,'mp'=8] {'mp'}, dimensions={0} | all-to-all | bytes 65536 | tf_op jit(solution)/shard_map/all_to_all | solution.py:78
  82.4 1.2 %collective-permute-done.5 = f32[64,16]{0,1:T(8,128)S(1)} collective-permute-done((f32[64,16]{0,1:T(8,128)S(1)}, f32[64,16]{0,1:T(8,128)S(1)}, u32[]{:S(2)}, u32[]{:S(2)}) %collective-permute-start.5) | collective-permute-done | bytes 4128 | tf_op jit(solution)/shard_map/ppermute | solution.py:30
  83.5 0.7 collective-permute-start.6
  84.3 2.9 %collective-permute-done.6 = f32[64,16]{0,1:T(8,128)S(1)} collective-permute-done((f32[64,16]{0,1:T(8,128)S(1)}, f32[64,16]{0,1:T(8,128)S(1)}, u32[]{:S(2)}, u32[]{:S(2)}) %collective-permute-start.6) | collective-permute-done | bytes 4128 | tf_op jit(solution)/shard_map/ppermute | solution.py:30
  87.2 1.2 %collective-permute-start.7 = (f32[64,16]{0,1:T(8,128)S(1)}, f32[64,16]{0,1:T(8,128)S(1)}, u32[]{:S(2)}, u32[]{:S(2)}) collective-permute-start(f32[64,16]{0,1:T(8,128)S(1)} %add.20), channel_id=1, source_target_pairs={{0,32},{8,40},{16,48},{24,56},{32,0},{40,8},{48,16},{56,24},{64,96... | collective-permute-start | bytes 12296 | tf_op jit(solution)/shard_map/ppermute | solution.py:30
  88.4 3.9 %collective-permute-done.7 = f32[64,16]{0,1:T(8,128)S(1)} collective-permute-done((f32[64,16]{0,1:T(8,128)S(1)}, f32[64,16]{0,1:T(8,128)S(1)}, u32[]{:S(2)}, u32[]{:S(2)}) %collective-permute-start.7) | collective-permute-done | bytes 4128 | tf_op jit(solution)/shard_map/ppermute | solution.py:30
  92.3 2.3 %collective-permute-start.8 = (f32[64,16]{0,1:T(8,128)S(1)}, f32[64,16]{0,1:T(8,128)S(1)}, u32[]{:S(2)}, u32[]{:S(2)}) collective-permute-start(f32[64,16]{0,1:T(8,128)S(1)} %add.21), channel_id=1, source_target_pairs={{0,64},{8,72},{16,80},{24,88},{32,96},{40,104},{48,112},{56,120},{... | collective-permute-start | bytes 12296 | tf_op jit(solution)/shard_map/ppermute | solution.py:30
  94.7 2.2 %collective-permute-done.8 = f32[64,16]{0,1:T(8,128)S(1)} collective-permute-done((f32[64,16]{0,1:T(8,128)S(1)}, f32[64,16]{0,1:T(8,128)S(1)}, u32[]{:S(2)}, u32[]{:S(2)}) %collective-permute-start.8) | collective-permute-done | bytes 4128 | tf_op jit(solution)/shard_map/ppermute | solution.py:30
  96.9 5.4 %collective-permute-start.9 = (f32[64,16]{0,1:T(8,128)S(1)}, f32[64,16]{0,1:T(8,128)S(1)}, u32[]{:S(2)}, u32[]{:S(2)}) collective-permute-start(f32[64,16]{0,1:T(8,128)S(1)} %add.22), channel_id=1, source_target_pairs={{0,128},{8,136},{16,144},{24,152},{32,160},{40,168},{48,176},{56,1... | collective-permute-start | bytes 12296 | tf_op jit(solution)/shard_map/ppermute | solution.py:30
  103.0 1.5 %collective-permute-done.9 = f32[64,16]{0,1:T(8,128)S(1)} collective-permute-done((f32[64,16]{0,1:T(8,128)S(1)}, f32[64,16]{0,1:T(8,128)S(1)}, u32[]{:S(2)}, u32[]{:S(2)}) %collective-permute-start.9) | collective-permute-done | bytes 4128 | tf_op jit(solution)/shard_map/ppermute | solution.py:30
  (47 shorter events, 6.4 us)
Async XLA Ops:
  0.6 4.5 %copy-start = (bf16[2,2,384,512]{3,2,1,0:T(8,128)(2,1)S(1)}, bf16[2,2,384,512]{3,2,1,0:T(8,128)(2,1)}, u32[]{:S(2)}) copy-start(bf16[2,2,384,512]{3,2,1,0:T(8,128)(2,1)} %param.8) | copy-start | bytes 4718596
  0.6 4.5 %copy-start.1 = (bf16[512,64]{0,1:T(8,128)(2,1)S(1)}, bf16[512,64]{0,1:T(8,128)(2,1)}, u32[]{:S(2)}) copy-start(bf16[512,64]{0,1:T(8,128)(2,1)} %param.10) | copy-start | bytes 196612
  35.4 29.9 %copy-start.2 = (f32[2]{0:T(128)S(1)}, f32[2]{0:T(128)}, u32[]{:S(2)}) copy-start(f32[2]{0:T(128)} %param.12) | copy-start | bytes 28
  36.0 8.3 %collective-permute-start = (bf16[2,2,4096]{2,0,1:T(2,128)(2,1)S(1)}, bf16[2,2,4096]{2,0,1:T(2,128)(2,1)S(1)}, u32[]{:S(2)}, u32[]{:S(2)}) collective-permute-start(bf16[2,2,4096]{2,0,1:T(2,128)(2,1)S(1)} %copy.37), channel_id=1, source_target_pairs={{0,128},{8,136},{16,144},{24,152},{32,160},{40,168},{48,176},{56,1... | collective-permute-start | bytes 98312 | tf_op jit(solution)/shard_map/ppermute | solution.py:42
  44.4 6.1 %collective-permute-start.1 = (bf16[4,2,4096]{2,0,1:T(4,128)(2,1)S(1)}, bf16[4,2,4096]{2,0,1:T(4,128)(2,1)S(1)}, u32[]{:S(2)}, u32[]{:S(2)}) collective-permute-start(bf16[4,2,4096]{2,0,1:T(4,128)(2,1)S(1)} %maximum_select_fusion.4), channel_id=1, source_target_pairs={{0,64},{8,72},{16,80},{24,88},{32,96},{40,104},{48,112},{56,120},{... | collective-permute-start | bytes 196616 | tf_op jit(solution)/shard_map/ppermute | solution.py:42
  50.6 8.0 %collective-permute-start.2 = (bf16[8,2,4096]{2,0,1:T(8,128)(2,1)S(1)}, bf16[8,2,4096]{2,0,1:T(8,128)(2,1)S(1)}, u32[]{:S(2)}, u32[]{:S(2)}) collective-permute-start(bf16[8,2,4096]{2,0,1:T(8,128)(2,1)S(1)} %maximum_select_fusion.3), channel_id=1, source_target_pairs={{0,32},{8,40},{16,48},{24,56},{32,0},{40,8},{48,16},{56,24},{64,96... | collective-permute-start | bytes 393224 | tf_op jit(solution)/shard_map/ppermute | solution.py:42
  58.7 6.5 %collective-permute-start.3 = (bf16[16,2,4096]{2,0,1:T(8,128)(2,1)S(1)}, bf16[16,2,4096]{2,0,1:T(8,128)(2,1)S(1)}, u32[]{:S(2)}, u32[]{:S(2)}) collective-permute-start(bf16[16,2,4096]{2,0,1:T(8,128)(2,1)S(1)} %maximum_select_fusion.2), channel_id=1, source_target_pairs={{0,16},{8,24},{16,0},{24,8},{32,48},{40,56},{48,32},{56,40},{64,80... | collective-permute-start | bytes 786440 | tf_op jit(solution)/shard_map/ppermute | solution.py:42
  65.2 2.0 %collective-permute-start.4 = (bf16[32,2,4096]{2,0,1:T(8,128)(2,1)S(1)}, bf16[32,2,4096]{2,0,1:T(8,128)(2,1)S(1)}, u32[]{:S(2)}, u32[]{:S(2)}) collective-permute-start(bf16[32,2,4096]{2,0,1:T(8,128)(2,1)S(1)} %maximum_select_fusion.1), channel_id=1, source_target_pairs={{0,8},{8,0},{16,24},{24,16},{32,40},{40,32},{48,56},{56,48},{64,72... | collective-permute-start | bytes 1572872 | tf_op jit(solution)/shard_map/ppermute | solution.py:42
  65.9 4.5 %copy-start.4 = (bf16[2,256,4096]{2,1,0:T(8,128)(2,1)S(1)}, bf16[2,256,4096]{2,1,0:T(8,128)(2,1)}, u32[]{:S(2)}) copy-start(bf16[2,256,4096]{2,1,0:T(8,128)(2,1)} %param.11) | copy-start | bytes 12582916
  70.4 1.4 %copy-start.3 = (s32[256]{0:T(256)S(1)}, s32[256]{0:T(256)}, u32[]{:S(2)}) copy-start(s32[256]{0:T(256)} %param.13) | copy-start | bytes 3076
  82.3 1.3 %collective-permute-start.5 = (f32[64,16]{0,1:T(8,128)S(1)}, f32[64,16]{0,1:T(8,128)S(1)}, u32[]{:S(2)}, u32[]{:S(2)}) collective-permute-start(f32[64,16]{0,1:T(8,128)S(1)} %bitcast_reduce_fusion), channel_id=1, source_target_pairs={{0,8},{8,0},{16,24},{24,16},{32,40},{40,32},{48,56},{56,48},{64,72... | collective-permute-start | bytes 12296 | tf_op jit(solution)/shard_map/ppermute | solution.py:30
  83.5 3.7 %collective-permute-start.6 = (f32[64,16]{0,1:T(8,128)S(1)}, f32[64,16]{0,1:T(8,128)S(1)}, u32[]{:S(2)}, u32[]{:S(2)}) collective-permute-start(f32[64,16]{0,1:T(8,128)S(1)} %add.19), channel_id=1, source_target_pairs={{0,16},{8,24},{16,0},{24,8},{32,48},{40,56},{48,32},{56,40},{64,80... | collective-permute-start | bytes 12296 | tf_op jit(solution)/shard_map/ppermute | solution.py:30
  87.2 5.2 %collective-permute-start.7 = (f32[64,16]{0,1:T(8,128)S(1)}, f32[64,16]{0,1:T(8,128)S(1)}, u32[]{:S(2)}, u32[]{:S(2)}) collective-permute-start(f32[64,16]{0,1:T(8,128)S(1)} %add.20), channel_id=1, source_target_pairs={{0,32},{8,40},{16,48},{24,56},{32,0},{40,8},{48,16},{56,24},{64,96... | collective-permute-start | bytes 12296 | tf_op jit(solution)/shard_map/ppermute | solution.py:30
  92.3 4.5 %collective-permute-start.8 = (f32[64,16]{0,1:T(8,128)S(1)}, f32[64,16]{0,1:T(8,128)S(1)}, u32[]{:S(2)}, u32[]{:S(2)}) collective-permute-start(f32[64,16]{0,1:T(8,128)S(1)} %add.21), channel_id=1, source_target_pairs={{0,64},{8,72},{16,80},{24,88},{32,96},{40,104},{48,112},{56,120},{... | collective-permute-start | bytes 12296 | tf_op jit(solution)/shard_map/ppermute | solution.py:30
  96.9 7.6 %collective-permute-start.9 = (f32[64,16]{0,1:T(8,128)S(1)}, f32[64,16]{0,1:T(8,128)S(1)}, u32[]{:S(2)}, u32[]{:S(2)}) collective-permute-start(f32[64,16]{0,1:T(8,128)S(1)} %add.22), channel_id=1, source_target_pairs={{0,128},{8,136},{16,144},{24,152},{32,160},{40,168},{48,176},{56,1... | collective-permute-start | bytes 12296 | tf_op jit(solution)/shard_map/ppermute | solution.py:30

commit v6 on v5

--- a/solution.py
+++ b/solution.py
@@ -66,14 +66,27 @@
     )
     outer = outer.reshape(ex_local, 2, rank * rank)
     query = (outer / jnp.sqrt(jnp.float32(seq_len))).astype(jnp.bfloat16)
-    piece = _doubling_gather(query, "dp", n_dp, 0, list(reversed(range(dp_bits))))
-    first = jnp.einsum("qk,rk->qr", piece[:, 0], store[0], preferred_element_type=jnp.float32)
-    second = jnp.einsum("qk,rk->qr", piece[:, 1], store[1], preferred_element_type=jnp.float32)
-    scores = ckpt_rate[0] * first + ckpt_rate[1] * second
     member = (store_group[:, None] == jnp.arange(GROUPS, dtype=jnp.int32)[None, :]).astype(
         jnp.float32
     )
-    partial_totals = jnp.dot(scores, member, precision=lax.Precision.HIGHEST)
+
+    def score(block):
+        first = jnp.einsum("qk,rk->qr", block[:, 0], store[0], preferred_element_type=jnp.float32)
+        second = jnp.einsum("qk,rk->qr", block[:, 1], store[1], preferred_element_type=jnp.float32)
+        rows = ckpt_rate[0] * first + ckpt_rate[1] * second
+        return rows, jnp.dot(rows, member, precision=lax.Precision.HIGHEST)
+
+    me = lax.axis_index("dp")
+    piece = query
+    scores, partial_totals = score(query)
+    for bit in reversed(range(dp_bits)):
+        upper = ((me >> bit) & 1) == 1
+        other = lax.ppermute(piece, "dp", _swap(n_dp, bit))
+        if bit:
+            piece = _join(piece, other, upper, 0)
+        other_scores, other_totals = score(other)
+        scores = _join(scores, other_scores, upper, 0)
+        partial_totals = _join(partial_totals, other_totals, upper, 0)
     copies = jnp.broadcast_to(partial_totals[None], (n_mp,) + partial_totals.shape)
     totals = lax.all_to_all(copies, "mp", 0, 0, tiled=True).sum(0)
     totals = _butterfly_sum(totals, "dp", n_dp, list(range(dp_bits)))

time: 106 us -> 117 us (1.10); the launches traced: 105 us -> 115 us
  matrix products: 10 us -> 29.9 us
  blocking collectives: 37.8 us -> 27.2 us
  starting transfers between devices: 21.5 us -> 19.1 us
  local copies, waits for them, and re-layouts: 3.56 us -> 5.87 us
    dot_general x3 -> x18, matrix products: 4.72 us -> 23.8 us  [the longest x6 11.1 us: score(): jnp.einsum('qk,rk->qr', block[:, 0], store[0], preferred_element_type=jnp...]
    all_to_all x1 -> x0, blocking collectives: 10.7 us -> none  [shards(): low = lax.all_to_all(copies, 'mp', 2, 2, tiled=True).reshape(c, e, t, r)]
    ppermute x5, waiting for transfers between devices: 18.4 us -> 7.77 us  [shards(): other = lax.ppermute(piece, 'dp', _swap(n_dp, bit))]
    all_to_all x0 -> x1, waiting for transfers between devices: none -> 7.32 us  [shards(): low = lax.all_to_all(copies, 'mp', 2, 2, tiled=True).reshape(c, e, t, r)]
    ppermute x5, starting transfers between devices: 9.75 us -> 6.06 us  [_butterfly_sum(): x = x + lax.ppermute(x, axis, _swap(n, bit))]
    ppermute x5, waiting for transfers between devices: 11.7 us -> 15.3 us  [_butterfly_sum(): x = x + lax.ppermute(x, axis, _swap(n, bit))]
    all_to_all x0 -> x1, starting transfers between devices: none -> 3.58 us  [shards(): low = lax.all_to_all(copies, 'mp', 2, 2, tiled=True).reshape(c, e, t, r)]
    ppermute x5, starting transfers between devices: 11.8 us -> 9.44 us  [shards(): other = lax.ppermute(piece, 'dp', _swap(n_dp, bit))]
  transfers between devices with their start and end apart: 10 -> 11, of which waited for: 10 -> 8; matrix products, arithmetic and copies ran while one was open for 1% -> 17% of each run, Pallas kernels for 0% -> 0%
where the time goes in v6:
time: 117 us; the launch traced here: 115 us
  waiting for transfers between devices  30.4 us (26%)
  matrix products  29.9 us (26%)
  blocking collectives  27.2 us (23%)
  starting transfers between devices  19.1 us (16%)
  local copies, waits for them, and re-layouts  5.87 us (5%)
  other arithmetic  1.65 us (1%)
    all_to_all x1, blocking collectives, shards(): lax.all_to_all(stacked.reshape(c, e, n_mp, t // n_mp, r), 'mp', 2, 2, til...  18.4 us
    ppermute x5, waiting for transfers between devices, _butterfly_sum(): x = x + lax.ppermute(x, axis, _swap(n, bit))  15.3 us
    dot_general x6, matrix products, score(): jnp.einsum('qk,rk->qr', block[:, 0], store[0], preferred_element_type=jnp...  11.1 us
    dot_general x6, matrix products, score(): jnp.einsum('qk,rk->qr', block[:, 1], store[1], preferred_element_type=jnp...  11 us
    ppermute x5, starting transfers between devices, shards(): other = lax.ppermute(piece, 'dp', _swap(n_dp, bit))  9.44 us
    all_to_all x1, blocking collectives, shards(): totals = lax.all_to_all(copies, 'mp', 0, 0, tiled=True).sum(0)  8.81 us
    ppermute x5, waiting for transfers between devices, shards(): other = lax.ppermute(piece, 'dp', _swap(n_dp, bit))  7.77 us
    all_to_all x1, waiting for transfers between devices, shards(): low = lax.all_to_all(copies, 'mp', 2, 2, tiled=True).reshape(c, e, t, r)  7.32 us
  transfers between devices with their start and end apart: 11, of which 8 were waited for; matrix products, arithmetic and copies ran while one was open for 17% of the time, Pallas kernels for 0%

profile of v6, /device:TPU:24, one launch (start us, length us, event | category | flops | bytes accessed | tf_op | source)
XLA Modules:
  0.0 115.0 jit_solution(16618046277976069121)
XLA Ops:
  0.6 1.4 %copy-done = bf16[2,2,384,512]{3,2,1,0:T(8,128)(2,1)S(1)} copy-done((bf16[2,2,384,512]{3,2,1,0:T(8,128)(2,1)S(1)}, bf16[2,2,384,512]{3,2,1,0:T(8,128)(2,1)}, u32[]{:S(2)}) %copy-start) | copy-done | bytes 1572888
  2.0 1.4 %fusion.101 = f32[2,2,384,64]{2,3,1,0:T(8,128)S(1)} fusion(bf16[2,2,384,512]{3,2,1,0:T(8,128)(2,1)S(1)} %copy-done, bf16[512,64]{0,1:T(8,128)(2,1)} %param.10), kind=kOutput, calls=%fused_computation.79 | convolution fusion | flops 100663296 | bytes 2031616 | tf_op jit(solution)/shard_map/cesf,fr->cesr/dot_general | solution.py:55
  3.5 4.3 %fusion.93 = f32[2,2,384,64]{2,3,1,0:T(8,128)S(1)} fusion(bf16[2,2,384,1792]{3,2,1,0:T(8,128)(2,1)} %param.7, bf16[1792,64]{0,1:T(8,128)(2,1)} %param.9), kind=kOutput, calls=%fused_computation.63 | convolution fusion | flops 352321536 | bytes 6127616 | tf_op jit(solution)/shard_map/cesf,fr->cesr/dot_general | solution.py:54
  8.2 18.4 %all_to_all.15 = f32[2,2,8,48,128]{4,3,1,0,2:T(8,128)S(1)} all-to-all(f32[2,2,8,48,128]{4,3,1,0,2:T(8,128)S(1)} %copy.59), channel_id=1, replica_groups=mesh['dp'=32,'mp'=8] {'mp'}, dimensions={2} | all-to-all | bytes 1572864 | tf_op jit(solution)/shard_map/all_to_all | solution.py:58
  27.5 3.6 %all-to-all-start.1 = ((bf16[2,2,8,48,128]{4,3,1,0,2:T(8,128)(2,1)}), bf16[2,2,8,48,128]{4,3,1,0,2:T(8,128)(2,1)S(1)}, u32[]{:S(2)}, u32[]{:S(2)}) async-start(bf16[2,2,8,48,128]{4,3,1,0,2:T(8,128)(2,1)} %broadcast_in_dim.4), calls=%async_computation.1 | async-start | bytes 786432 | tf_op jit(solution)/shard_map/all_to_all | solution.py:63
  31.7 7.3 %all-to-all-done.1 = bf16[2,2,8,48,128]{4,3,1,0,2:T(8,128)(2,1)S(1)} async-done(((bf16[2,2,8,48,128]{4,3,1,0,2:T(8,128)(2,1)}), bf16[2,2,8,48,128]{4,3,1,0,2:T(8,128)(2,1)S(1)}, u32[]{:S(2)}, u32[]{:S(2)}) %all-to-all-start.1) | async-done | bytes 393248 | tf_op jit(solution)/shard_map/all_to_all | solution.py:63
  39.7 6.4 %collective-permute-start = (bf16[2,2,4096]{2,0,1:T(2,128)(2,1)S(1)}, bf16[2,2,4096]{2,0,1:T(2,128)(2,1)S(1)}, u32[]{:S(2)}, u32[]{:S(2)}) collective-permute-start(bf16[2,2,4096]{2,0,1:T(2,128)(2,1)S(1)} %copy.63), channel_id=1, source_target_pairs={{0,128},{8,136},{16,144},{24,152},{32,160},{40,168},{48,176},{56,1... | collective-permute-start | bytes 98312 | tf_op jit(solution)/shard_map/ppermute | solution.py:84
  46.1 2.9 %fusion.76 = f32[2,256]{1,0:T(2,128)S(1)} fusion(bf16[2,256,4096]{2,1,0:T(8,128)(2,1)} %param.11, bf16[2,2,4096]{2,0,1:T(2,128)(2,1)S(1)} %copy.63, f32[]{:T(128)} %bitcast.9), kind=kOutput, calls=%fused_computation.43 | convolution fusion | flops 4194816 | bytes 2116096 | tf_op jit(solution)/shard_map/qk,rk->qr/dot_general | solution.py:75
  49.0 2.9 %fusion.70 = f32[2,256]{1,0:T(2,128)S(1)} fusion(f32[2,256]{1,0:T(2,128)S(1)} %fusion.76, bf16[2,256,4096]{2,1,0:T(8,128)(2,1)} %param.11, bf16[2,2,4096]{2,0,1:T(2,128)(2,1)S(1)} %copy.63, f32[]{:T(128)} %bitcast), kind=kOutput, calls=%fused_computation.41 | convolution fusion | flops 4195328 | bytes 2118144 | tf_op jit(solution)/shard_map/qk,rk->qr/dot_general | solution.py:74
  55.3 1.6 %collective-permute-start.1 = (bf16[4,2,4096]{2,0,1:T(4,128)(2,1)S(1)}, bf16[4,2,4096]{2,0,1:T(4,128)(2,1)S(1)}, u32[]{:S(2)}, u32[]{:S(2)}) collective-permute-start(bf16[4,2,4096]{2,0,1:T(4,128)(2,1)S(1)} %maximum_select_fusion.3), channel_id=1, source_target_pairs={{0,64},{8,72},{16,80},{24,88},{32,96},{40,104},{48,112},{56,120},{... | collective-permute-start | bytes 196616 | tf_op jit(solution)/shard_map/ppermute | solution.py:84
  56.8 4.4 %collective-permute-done.1 = bf16[4,2,4096]{2,0,1:T(4,128)(2,1)S(1)} collective-permute-done((bf16[4,2,4096]{2,0,1:T(4,128)(2,1)S(1)}, bf16[4,2,4096]{2,0,1:T(4,128)(2,1)S(1)}, u32[]{:S(2)}, u32[]{:S(2)}) %collective-permute-start.1) | collective-permute-done | bytes 65568 | tf_op jit(solution)/shard_map/ppermute | solution.py:84
  62.7 2.9 %fusion.58 = f32[4,256]{1,0:T(4,128)S(1)} fusion(bf16[2,256,4096]{2,1,0:T(8,128)(2,1)} %param.11, bf16[4,2,4096]{2,0,1:T(4,128)(2,1)S(1)} %collective-permute-done.1, f32[]{:T(128)} %bitcast.9), kind=kOutput, calls=%fused_computation.37 | convolution fusion | flops 8389632 | bytes 2134528 | tf_op jit(solution)/shard_map/qk,rk->qr/dot_general | solution.py:75
  65.6 2.9 %fusion.55 = f32[4,256]{1,0:T(4,128)S(1)} fusion(f32[4,256]{1,0:T(4,128)S(1)} %fusion.58, bf16[2,256,4096]{2,1,0:T(8,128)(2,1)} %param.11, bf16[4,2,4096]{2,0,1:T(4,128)(2,1)S(1)} %collective-permute-done.1, f32[]{:T(128)} %bitcast), kind=kOutput, calls=%fused_computation.36 | convolution fusion | flops 8390656 | bytes 2138624 | tf_op jit(solution)/shard_map/qk,rk->qr/dot_general | solution.py:74
  72.0 3.4 %collective-permute-done.3 = bf16[16,2,4096]{2,0,1:T(8,128)(2,1)S(1)} collective-permute-done((bf16[16,2,4096]{2,0,1:T(8,128)(2,1)S(1)}, bf16[16,2,4096]{2,0,1:T(8,128)(2,1)S(1)}, u32[]{:S(2)}, u32[]{:S(2)}) %collective-permute-start.3) | collective-permute-done | bytes 262176 | tf_op jit(solution)/shard_map/ppermute | solution.py:84
  78.6 1.4 %fusion.31 = f32[32,256]{1,0:T(8,128)S(1)} fusion(bf16[2,256,4096]{2,1,0:T(8,128)(2,1)S(1)} %copy-done.2, bf16[32,2,4096]{2,0,1:T(8,128)(2,1)S(1)} %collective-permute-done.4, f32[]{:T(128)} %bitcast.9), kind=kOutput, calls=%fused_computation.28 | convolution fusion | flops 67117056 | bytes 2392068 | tf_op jit(solution)/shard_map/qk,rk->qr/dot_general | solution.py:75
  80.0 1.4 %fusion.28 = f32[32,256]{1,0:T(8,128)S(1)} fusion(f32[32,256]{1,0:T(8,128)S(1)} %fusion.31, bf16[2,256,4096]{2,1,0:T(8,128)(2,1)S(1)} %copy-done.2, bf16[32,2,4096]{2,0,1:T(8,128)(2,1)S(1)} %collective-permute-done.4, f32[]{:T(128)} %bitcast), kind=kOutput, calls=%fused_computation.27 | convolution fusion | flops 67125248 | bytes 2424836 | tf_op jit(solution)/shard_map/qk,rk->qr/dot_general | solution.py:74
  81.9 8.8 %all_to_all.16 = f32[8,1,1024]{2,1,0:T(1,128)S(1)} all-to-all(f32[8,1,1024]{2,1,0:T(1,128)S(1)} %reshape.82), channel_id=1, replica_groups=mesh['dp'=32,'mp'=8] {'mp'}, dimensions={0} | all-to-all | bytes 65536 | tf_op jit(solution)/shard_map/all_to_all | solution.py:91
  93.3 3.6 %collective-permute-done.6 = f32[64,16]{0,1:T(8,128)S(1)} collective-permute-done((f32[64,16]{0,1:T(8,128)S(1)}, f32[64,16]{0,1:T(8,128)S(1)}, u32[]{:S(2)}, u32[]{:S(2)}) %collective-permute-start.6) | collective-permute-done | bytes 4128 | tf_op jit(solution)/shard_map/ppermute | solution.py:30
  97.0 2.3 %collective-permute-start.7 = (f32[64,16]{0,1:T(8,128)S(1)}, f32[64,16]{0,1:T(8,128)S(1)}, u32[]{:S(2)}, u32[]{:S(2)}) collective-permute-start(f32[64,16]{0,1:T(8,128)S(1)} %add.40), channel_id=1, source_target_pairs={{0,32},{8,40},{16,48},{24,56},{32,0},{40,8},{48,16},{56,24},{64,96... | collective-permute-start | bytes 12296 | tf_op jit(solution)/shard_map/ppermute | solution.py:30
  99.3 2.9 %collective-permute-done.7 = f32[64,16]{0,1:T(8,128)S(1)} collective-permute-done((f32[64,16]{0,1:T(8,128)S(1)}, f32[64,16]{0,1:T(8,128)S(1)}, u32[]{:S(2)}, u32[]{:S(2)}) %collective-permute-start.7) | collective-permute-done | bytes 4128 | tf_op jit(solution)/shard_map/ppermute | solution.py:30
  102.1 1.6 %collective-permute-start.8 = (f32[64,16]{0,1:T(8,128)S(1)}, f32[64,16]{0,1:T(8,128)S(1)}, u32[]{:S(2)}, u32[]{:S(2)}) collective-permute-start(f32[64,16]{0,1:T(8,128)S(1)} %add.41), channel_id=1, source_target_pairs={{0,64},{8,72},{16,80},{24,88},{32,96},{40,104},{48,112},{56,120},{... | collective-permute-start | bytes 12296 | tf_op jit(solution)/shard_map/ppermute | solution.py:30
  103.7 2.9 %collective-permute-done.8 = f32[64,16]{0,1:T(8,128)S(1)} collective-permute-done((f32[64,16]{0,1:T(8,128)S(1)}, f32[64,16]{0,1:T(8,128)S(1)}, u32[]{:S(2)}, u32[]{:S(2)}) %collective-permute-start.8) | collective-permute-done | bytes 4128 | tf_op jit(solution)/shard_map/ppermute | solution.py:30
  106.7 2.1 %collective-permute-start.9 = (f32[64,16]{0,1:T(8,128)S(1)}, f32[64,16]{0,1:T(8,128)S(1)}, u32[]{:S(2)}, u32[]{:S(2)}) collective-permute-start(f32[64,16]{0,1:T(8,128)S(1)} %add.42), channel_id=1, source_target_pairs={{0,128},{8,136},{16,144},{24,152},{32,160},{40,168},{48,176},{56,1... | collective-permute-start | bytes 12296 | tf_op jit(solution)/shard_map/ppermute | solution.py:30
  109.5 4.7 %collective-permute-done.9 = f32[64,16]{0,1:T(8,128)S(1)} collective-permute-done((f32[64,16]{0,1:T(8,128)S(1)}, f32[64,16]{0,1:T(8,128)S(1)}, u32[]{:S(2)}, u32[]{:S(2)}) %collective-permute-start.9) | collective-permute-done | bytes 4128 | tf_op jit(solution)/shard_map/ppermute | solution.py:30
  (75 shorter events, 18.7 us)
Async XLA Ops:
  0.6 1.4 %copy-start = (bf16[2,2,384,512]{3,2,1,0:T(8,128)(2,1)S(1)}, bf16[2,2,384,512]{3,2,1,0:T(8,128)(2,1)}, u32[]{:S(2)}) copy-start(bf16[2,2,384,512]{3,2,1,0:T(8,128)(2,1)} %param.8) | copy-start | bytes 4718596
  7.8 23.3 %copy-start.3 = (f32[2]{0:T(128)S(1)}, f32[2]{0:T(128)}, u32[]{:S(2)}) copy-start(f32[2]{0:T(128)} %param.12) | copy-start | bytes 28
  27.5 24.4 %copy-start.4 = (s32[256]{0:T(256)S(1)}, s32[256]{0:T(256)}, u32[]{:S(2)}) copy-start(s32[256]{0:T(256)} %param.13) | copy-start | bytes 3076
  27.5 11.5 %all-to-all-start.1 = ((bf16[2,2,8,48,128]{4,3,1,0,2:T(8,128)(2,1)}), bf16[2,2,8,48,128]{4,3,1,0,2:T(8,128)(2,1)S(1)}, u32[]{:S(2)}, u32[]{:S(2)}) async-start(bf16[2,2,8,48,128]{4,3,1,0,2:T(8,128)(2,1)} %broadcast_in_dim.4), calls=%async_computation.1 | async-start | bytes 786432 | tf_op jit(solution)/shard_map/all_to_all | solution.py:63
  39.6 12.5 %copy-start.1 = (bf16[2,256,4096]{2,1,0:T(8,128)(2,1)S(1)}, bf16[2,256,4096]{2,1,0:T(8,128)(2,1)}, u32[]{:S(2)}) copy-start(bf16[2,256,4096]{2,1,0:T(8,128)(2,1)} %param.11) | copy-start | bytes 12582916
  39.7 12.4 %collective-permute-start = (bf16[2,2,4096]{2,0,1:T(2,128)(2,1)S(1)}, bf16[2,2,4096]{2,0,1:T(2,128)(2,1)S(1)}, u32[]{:S(2)}, u32[]{:S(2)}) collective-permute-start(bf16[2,2,4096]{2,0,1:T(2,128)(2,1)S(1)} %copy.63), channel_id=1, source_target_pairs={{0,128},{8,136},{16,144},{24,152},{32,160},{40,168},{48,176},{56,1... | collective-permute-start | bytes 98312 | tf_op jit(solution)/shard_map/ppermute | solution.py:84
  55.1 13.9 %copy-start.2 = (bf16[2,256,4096]{2,1,0:T(8,128)(2,1)S(1)}, bf16[2,256,4096]{2,1,0:T(8,128)(2,1)}, u32[]{:S(2)}) copy-start(bf16[2,256,4096]{2,1,0:T(8,128)(2,1)} %param.11) | copy-start | bytes 12582916
  55.3 6.0 %collective-permute-start.1 = (bf16[4,2,4096]{2,0,1:T(4,128)(2,1)S(1)}, bf16[4,2,4096]{2,0,1:T(4,128)(2,1)S(1)}, u32[]{:S(2)}, u32[]{:S(2)}) collective-permute-start(bf16[4,2,4096]{2,0,1:T(4,128)(2,1)S(1)} %maximum_select_fusion.3), channel_id=1, source_target_pairs={{0,64},{8,72},{16,80},{24,88},{32,96},{40,104},{48,112},{56,120},{... | collective-permute-start | bytes 196616 | tf_op jit(solution)/shard_map/ppermute | solution.py:84
  61.4 7.5 %collective-permute-start.2 = (bf16[8,2,4096]{2,0,1:T(8,128)(2,1)S(1)}, bf16[8,2,4096]{2,0,1:T(8,128)(2,1)S(1)}, u32[]{:S(2)}, u32[]{:S(2)}) collective-permute-start(bf16[8,2,4096]{2,0,1:T(8,128)(2,1)S(1)} %maximum_select_fusion.2), channel_id=1, source_target_pairs={{0,32},{8,40},{16,48},{24,56},{32,0},{40,8},{48,16},{56,24},{64,96... | collective-permute-start | bytes 393224 | tf_op jit(solution)/shard_map/ppermute | solution.py:84
  68.9 6.5 %collective-permute-start.3 = (bf16[16,2,4096]{2,0,1:T(8,128)(2,1)S(1)}, bf16[16,2,4096]{2,0,1:T(8,128)(2,1)S(1)}, u32[]{:S(2)}, u32[]{:S(2)}) collective-permute-start(bf16[16,2,4096]{2,0,1:T(8,128)(2,1)S(1)} %maximum_select_fusion.1), channel_id=1, source_target_pairs={{0,16},{8,24},{16,0},{24,8},{32,48},{40,56},{48,32},{56,40},{64,80... | collective-permute-start | bytes 786440 | tf_op jit(solution)/shard_map/ppermute | solution.py:84
  75.5 3.1 %collective-permute-start.4 = (bf16[32,2,4096]{2,0,1:T(8,128)(2,1)S(1)}, bf16[32,2,4096]{2,0,1:T(8,128)(2,1)S(1)}, u32[]{:S(2)}, u32[]{:S(2)}) collective-permute-start(bf16[32,2,4096]{2,0,1:T(8,128)(2,1)S(1)} %maximum_select_fusion), channel_id=1, source_target_pairs={{0,8},{8,0},{16,24},{24,16},{32,40},{40,32},{48,56},{56,48},{64,72... | collective-permute-start | bytes 1572872 | tf_op jit(solution)/shard_map/ppermute | solution.py:84
  92.0 1.3 %collective-permute-start.5 = (f32[64,16]{0,1:T(8,128)S(1)}, f32[64,16]{0,1:T(8,128)S(1)}, u32[]{:S(2)}, u32[]{:S(2)}) collective-permute-start(f32[64,16]{0,1:T(8,128)S(1)} %bitcast_reduce_fusion), channel_id=1, source_target_pairs={{0,8},{8,0},{16,24},{24,16},{32,40},{40,32},{48,56},{56,48},{64,72... | collective-permute-start | bytes 12296 | tf_op jit(solution)/shard_map/ppermute | solution.py:30
  93.3 3.7 %collective-permute-start.6 = (f32[64,16]{0,1:T(8,128)S(1)}, f32[64,16]{0,1:T(8,128)S(1)}, u32[]{:S(2)}, u32[]{:S(2)}) collective-permute-start(f32[64,16]{0,1:T(8,128)S(1)} %add.39), channel_id=1, source_target_pairs={{0,16},{8,24},{16,0},{24,8},{32,48},{40,56},{48,32},{56,40},{64,80... | collective-permute-start | bytes 12296 | tf_op jit(solution)/shard_map/ppermute | solution.py:30
  97.0 5.2 %collective-permute-start.7 = (f32[64,16]{0,1:T(8,128)S(1)}, f32[64,16]{0,1:T(8,128)S(1)}, u32[]{:S(2)}, u32[]{:S(2)}) collective-permute-start(f32[64,16]{0,1:T(8,128)S(1)} %add.40), channel_id=1, source_target_pairs={{0,32},{8,40},{16,48},{24,56},{32,0},{40,8},{48,16},{56,24},{64,96... | collective-permute-start | bytes 12296 | tf_op jit(solution)/shard_map/ppermute | solution.py:30
  102.1 4.5 %collective-permute-start.8 = (f32[64,16]{0,1:T(8,128)S(1)}, f32[64,16]{0,1:T(8,128)S(1)}, u32[]{:S(2)}, u32[]{:S(2)}) collective-permute-start(f32[64,16]{0,1:T(8,128)S(1)} %add.41), channel_id=1, source_target_pairs={{0,64},{8,72},{16,80},{24,88},{32,96},{40,104},{48,112},{56,120},{... | collective-permute-start | bytes 12296 | tf_op jit(solution)/shard_map/ppermute | solution.py:30
  106.7 7.6 %collective-permute-start.9 = (f32[64,16]{0,1:T(8,128)S(1)}, f32[64,16]{0,1:T(8,128)S(1)}, u32[]{:S(2)}, u32[]{:S(2)}) collective-permute-start(f32[64,16]{0,1:T(8,128)S(1)} %add.42), channel_id=1, source_target_pairs={{0,128},{8,136},{16,144},{24,152},{32,160},{40,168},{48,176},{56,1... | collective-permute-start | bytes 12296 | tf_op jit(solution)/shard_map/ppermute | solution.py:30

commit v7 on v5

--- a/solution.py
+++ b/solution.py
@@ -67,13 +67,17 @@
     outer = outer.reshape(ex_local, 2, rank * rank)
     query = (outer / jnp.sqrt(jnp.float32(seq_len))).astype(jnp.bfloat16)
     piece = _doubling_gather(query, "dp", n_dp, 0, list(reversed(range(dp_bits))))
+    member = (store_group[:, None] == jnp.arange(GROUPS, dtype=jnp.int32)[None, :]).astype(
+        jnp.bfloat16
+    )
+    group_rows = jnp.einsum("rg,crk->cgk", member, store, preferred_element_type=jnp.float32)
+    by_ckpt = jnp.einsum(
+        "qck,cgk->cqg", piece.astype(jnp.float32), group_rows, precision=lax.Precision.HIGHEST
+    )
+    partial_totals = ckpt_rate[0] * by_ckpt[0] + ckpt_rate[1] * by_ckpt[1]
     first = jnp.einsum("qk,rk->qr", piece[:, 0], store[0], preferred_element_type=jnp.float32)
     second = jnp.einsum("qk,rk->qr", piece[:, 1], store[1], preferred_element_type=jnp.float32)
     scores = ckpt_rate[0] * first + ckpt_rate[1] * second
-    member = (store_group[:, None] == jnp.arange(GROUPS, dtype=jnp.int32)[None, :]).astype(
-        jnp.float32
-    )
-    partial_totals = jnp.dot(scores, member, precision=lax.Precision.HIGHEST)
     copies = jnp.broadcast_to(partial_totals[None], (n_mp,) + partial_totals.shape)
     totals = lax.all_to_all(copies, "mp", 0, 0, tiled=True).sum(0)
     totals = _butterfly_sum(totals, "dp", n_dp, list(range(dp_bits)))

time: 106 us -> 108 us (1.019)
  matrix products: 10 us -> 15.1 us
  waiting for transfers between devices: 30.1 us -> 25.1 us
  other arithmetic: 1.43 us -> 3.9 us
    ppermute x5, waiting for transfers between devices: 11.7 us -> 8 us  [_butterfly_sum(): x = x + lax.ppermute(x, axis, _swap(n, bit))]
    dot_general x1 -> x2, matrix products: 0.31 us -> 3.77 us  [the longest x1 2.84 us: shards(): jnp.einsum('rg,crk->cgk', member, store, preferred_element_type=jnp.float32)]
    dot_general x1, matrix products: 1.41 us -> 3 us  [shards(): jnp.einsum('qk,rk->qr', piece[:, 0], store[0], preferred_element_type=jnp...]
    broadcast_in_dim x0 -> x1, other arithmetic: none -> 1.31 us  [shards(): jnp.broadcast_to(partial_totals[None], (n_mp,) + partial_totals.shape)]
    ppermute x5, waiting for transfers between devices: 18.4 us -> 17.1 us  [_doubling_gather(): x = _join(x, lax.ppermute(x, axis, _swap(n, bit)), upper, dim)]
    select_n x5, other arithmetic: 0.58 us -> 1.83 us  [_join(): jnp.where(upper, jnp.concatenate([other, x], dim), jnp.concatenate([x, ot...]
  transfers between devices with their start and end apart: 10 -> 10, of which waited for: 10 -> 7; matrix products, arithmetic and copies ran while one was open for 1% -> 9% of each run, Pallas kernels for 0% -> 0%
where the time goes in v7:
time: 108 us; the launch traced here: 107 us
  blocking collectives  37.8 us (35%)
  waiting for transfers between devices  25.1 us (23%)
  starting transfers between devices  21 us (19%)
  matrix products  15.1 us (14%)
  other arithmetic  3.9 us (4%)
  local copies, waits for them, and re-layouts  3.53 us (3%)
    all_to_all x1, blocking collectives, shards(): lax.all_to_all(stacked.reshape(c, e, n_mp, t // n_mp, r), 'mp', 2, 2, til...  18.4 us
    ppermute x5, waiting for transfers between devices, _doubling_gather(): x = _join(x, lax.ppermute(x, axis, _swap(n, bit)), upper, dim)  17.1 us
    ppermute x5, starting transfers between devices, _doubling_gather(): x = _join(x, lax.ppermute(x, axis, _swap(n, bit)), upper, dim)  11.8 us
    all_to_all x1, blocking collectives, shards(): low = lax.all_to_all(copies, 'mp', 2, 2, tiled=True).reshape(c, e, t, r)  10.7 us
    ppermute x5, starting transfers between devices, _butterfly_sum(): x = x + lax.ppermute(x, axis, _swap(n, bit))  9.21 us
    all_to_all x1, blocking collectives, shards(): totals = lax.all_to_all(copies, 'mp', 0, 0, tiled=True).sum(0)  8.63 us
    ppermute x5, waiting for transfers between devices, _butterfly_sum(): x = x + lax.ppermute(x, axis, _swap(n, bit))  8 us
    dot_general x1, matrix products, shards(): jnp.einsum('cesf,fr->cesr', activations, proj_in, preferred_element_type=...  4.44 us
  transfers between devices with their start and end apart: 10, of which 7 were waited for; matrix products, arithmetic and copies ran while one was open for 9% of the time, Pallas kernels for 0%

profile of v7, /device:TPU:24, one launch (start us, length us, event | category | flops | bytes accessed | tf_op | source)
XLA Modules:
  0.0 107.2 jit_solution(8874394659914780900)
XLA Ops:
  0.7 4.4 %fusion.18 = f32[2,2,384,64]{2,3,1,0:T(8,128)S(1)} fusion(bf16[2,2,384,1792]{3,2,1,0:T(8,128)(2,1)} %param.7, bf16[1792,64]{0,1:T(8,128)(2,1)} %param.9), kind=kOutput, calls=%fused_computation.20 | convolution fusion | flops 352321536 | bytes 6127616 | tf_op jit(solution)/shard_map/cesf,fr->cesr/dot_general | solution.py:54
  6.1 18.4 %all_to_all.15 = f32[2,2,8,48,128]{4,3,1,0,2:T(8,128)S(1)} all-to-all(f32[2,2,8,48,128]{4,3,1,0,2:T(8,128)S(1)} %copy.36), channel_id=1, replica_groups=mesh['dp'=32,'mp'=8] {'mp'}, dimensions={2} | all-to-all | bytes 1572864 | tf_op jit(solution)/shard_map/all_to_all | solution.py:58
  24.7 10.7 %all_to_all.16 = bf16[2,2,8,48,128]{4,3,1,0,2:T(8,128)(2,1)S(1)} all-to-all(bf16[2,2,8,48,128]{4,3,1,0,2:T(8,128)(2,1)S(1)} %broadcast_in_dim.6), channel_id=1, replica_groups=mesh['dp'=32,'mp'=8] {'mp'}, dimensions={2} | all-to-all | bytes 786432 | tf_op jit(solution)/shard_map/all_to_all | solution.py:63
  36.1 6.4 %collective-permute-start = (bf16[2,2,4096]{2,0,1:T(2,128)(2,1)S(1)}, bf16[2,2,4096]{2,0,1:T(2,128)(2,1)S(1)}, u32[]{:S(2)}, u32[]{:S(2)}) collective-permute-start(bf16[2,2,4096]{2,0,1:T(2,128)(2,1)S(1)} %copy.40), channel_id=1, source_target_pairs={{0,128},{8,136},{16,144},{24,152},{32,160},{40,168},{48,176},{56,1... | collective-permute-start | bytes 98312 | tf_op jit(solution)/shard_map/ppermute | solution.py:42
  42.4 1.9 %collective-permute-done = bf16[2,2,4096]{2,0,1:T(2,128)(2,1)S(1)} collective-permute-done((bf16[2,2,4096]{2,0,1:T(2,128)(2,1)S(1)}, bf16[2,2,4096]{2,0,1:T(2,128)(2,1)S(1)}, u32[]{:S(2)}, u32[]{:S(2)}) %collective-permute-start) | collective-permute-done | bytes 32800 | tf_op jit(solution)/shard_map/ppermute | solution.py:42
  44.5 3.1 %collective-permute-start.1 = (bf16[4,2,4096]{2,0,1:T(4,128)(2,1)S(1)}, bf16[4,2,4096]{2,0,1:T(4,128)(2,1)S(1)}, u32[]{:S(2)}, u32[]{:S(2)}) collective-permute-start(bf16[4,2,4096]{2,0,1:T(4,128)(2,1)S(1)} %maximum_select_fusion.4), channel_id=1, source_target_pairs={{0,64},{8,72},{16,80},{24,88},{32,96},{40,104},{48,112},{56,120},{... | collective-permute-start | bytes 196616 | tf_op jit(solution)/shard_map/ppermute | solution.py:42
  47.6 2.9 %collective-permute-done.1 = bf16[4,2,4096]{2,0,1:T(4,128)(2,1)S(1)} collective-permute-done((bf16[4,2,4096]{2,0,1:T(4,128)(2,1)S(1)}, bf16[4,2,4096]{2,0,1:T(4,128)(2,1)S(1)}, u32[]{:S(2)}, u32[]{:S(2)}) %collective-permute-start.1) | collective-permute-done | bytes 65568 | tf_op jit(solution)/shard_map/ppermute | solution.py:42
  50.7 1.3 %collective-permute-start.2 = (bf16[8,2,4096]{2,0,1:T(8,128)(2,1)S(1)}, bf16[8,2,4096]{2,0,1:T(8,128)(2,1)S(1)}, u32[]{:S(2)}, u32[]{:S(2)}) collective-permute-start(bf16[8,2,4096]{2,0,1:T(8,128)(2,1)S(1)} %maximum_select_fusion.3), channel_id=1, source_target_pairs={{0,32},{8,40},{16,48},{24,56},{32,0},{40,8},{48,16},{56,24},{64,96... | collective-permute-start | bytes 393224 | tf_op jit(solution)/shard_map/ppermute | solution.py:42
  52.0 6.6 %collective-permute-done.2 = bf16[8,2,4096]{2,0,1:T(8,128)(2,1)S(1)} collective-permute-done((bf16[8,2,4096]{2,0,1:T(8,128)(2,1)S(1)}, bf16[8,2,4096]{2,0,1:T(8,128)(2,1)S(1)}, u32[]{:S(2)}, u32[]{:S(2)}) %collective-permute-start.2) | collective-permute-done | bytes 131104 | tf_op jit(solution)/shard_map/ppermute | solution.py:42
  58.7 0.8 collective-permute-start.3
  59.5 5.6 %collective-permute-done.3 = bf16[16,2,4096]{2,0,1:T(8,128)(2,1)S(1)} collective-permute-done((bf16[16,2,4096]{2,0,1:T(8,128)(2,1)S(1)}, bf16[16,2,4096]{2,0,1:T(8,128)(2,1)S(1)}, u32[]{:S(2)}, u32[]{:S(2)}) %collective-permute-start.3) | collective-permute-done | bytes 262176 | tf_op jit(solution)/shard_map/ppermute | solution.py:42
  65.9 2.8 %convolution_bitcast_fusion = f32[2,4096,16]{1,2,0:T(8,128)S(1)} fusion(bf16[2,256,4096]{2,1,0:T(8,128)(2,1)} %param.11, s32[256]{0:T(256)S(1)} %copy-done.3), kind=kOutput, calls=%fused_computation | convolution fusion | flops 67112960 | bytes 4719616 | tf_op jit(solution)/shard_map/rg,crk->cgk/dot_general | solution.py:73
  68.8 1.5 %maximum_select_fusion = bf16[64,2,4096]{2,0,1:T(8,128)(2,1)S(1)} fusion(bf16[32,2,4096]{2,0,1:T(8,128)(2,1)S(1)} %maximum_select_fusion.1, bf16[32,2,4096]{2,0,1:T(8,128)(2,1)} %collective-permute-done.4, pred[]{:T(512)S(6)} %eq.28), kind=kLoop, calls=%fused_computation.12 | loop fusion | flops 4718592 | bytes 2097153 | tf_op jit(solution)/shard_map/jit(_where)/select_n | solution.py:35
  70.2 0.9 fusion.29
  71.2 1.3 %fusion.25 = f32[64,16]{0,1:T(8,128)S(1)} fusion(f32[2,64,16]{1,2,0:T(8,128)S(1)} %fusion.29, f32[]{:T(128)} %bitcast.9, f32[]{:T(128)} %bitcast), kind=kLoop, calls=%fused_computation.30 | loop fusion | flops 3072 | bytes 12296 | tf_op jit(solution)/shard_map/broadcast_in_dim | solution.py:81
  72.6 8.6 %all_to_all.17 = f32[8,1,1024]{2,1,0:T(1,128)S(1)} all-to-all(f32[8,1,1024]{2,1,0:T(1,128)S(1)} %reshape.37), channel_id=1, replica_groups=mesh['dp'=32,'mp'=8] {'mp'}, dimensions={0} | all-to-all | bytes 65536 | tf_op jit(solution)/shard_map/all_to_all | solution.py:82
  82.6 1.2 %collective-permute-done.5 = f32[64,16]{0,1:T(8,128)S(1)} collective-permute-done((f32[64,16]{0,1:T(8,128)S(1)}, f32[64,16]{0,1:T(8,128)S(1)}, u32[]{:S(2)}, u32[]{:S(2)}) %collective-permute-start.5) | collective-permute-done | bytes 4128 | tf_op jit(solution)/shard_map/ppermute | solution.py:30
  84.5 2.9 %collective-permute-done.6 = f32[64,16]{0,1:T(8,128)S(1)} collective-permute-done((f32[64,16]{0,1:T(8,128)S(1)}, f32[64,16]{0,1:T(8,128)S(1)}, u32[]{:S(2)}, u32[]{:S(2)}) %collective-permute-start.6) | collective-permute-done | bytes 4128 | tf_op jit(solution)/shard_map/ppermute | solution.py:30
  87.4 1.2 %collective-permute-start.7 = (f32[64,16]{0,1:T(8,128)S(1)}, f32[64,16]{0,1:T(8,128)S(1)}, u32[]{:S(2)}, u32[]{:S(2)}) collective-permute-start(f32[64,16]{0,1:T(8,128)S(1)} %add.25), channel_id=1, source_target_pairs={{0,32},{8,40},{16,48},{24,56},{32,0},{40,8},{48,16},{56,24},{64,96... | collective-permute-start | bytes 12296 | tf_op jit(solution)/shard_map/ppermute | solution.py:30
  88.6 3.9 %collective-permute-done.7 = f32[64,16]{0,1:T(8,128)S(1)} collective-permute-done((f32[64,16]{0,1:T(8,128)S(1)}, f32[64,16]{0,1:T(8,128)S(1)}, u32[]{:S(2)}, u32[]{:S(2)}) %collective-permute-start.7) | collective-permute-done | bytes 4128 | tf_op jit(solution)/shard_map/ppermute | solution.py:30
  92.5 2.3 %collective-permute-start.8 = (f32[64,16]{0,1:T(8,128)S(1)}, f32[64,16]{0,1:T(8,128)S(1)}, u32[]{:S(2)}, u32[]{:S(2)}) collective-permute-start(f32[64,16]{0,1:T(8,128)S(1)} %add.26), channel_id=1, source_target_pairs={{0,64},{8,72},{16,80},{24,88},{32,96},{40,104},{48,112},{56,120},{... | collective-permute-start | bytes 12296 | tf_op jit(solution)/shard_map/ppermute | solution.py:30
  94.8 3.0 %fusion.13 = f32[64,256]{1,0:T(8,128)S(1)} fusion(bf16[2,256,4096]{2,1,0:T(8,128)(2,1)} %param.11, bf16[64,2,4096]{2,0,1:T(8,128)(2,1)S(1)} %maximum_select_fusion, f32[]{:T(128)} %bitcast.9), kind=kOutput, calls=%fused_computation.11 | convolution fusion | flops 134234112 | bytes 2687488 | tf_op jit(solution)/shard_map/qk,rk->qr/dot_general | solution.py:79
  97.9 4.8 %collective-permute-start.9 = (f32[64,16]{0,1:T(8,128)S(1)}, f32[64,16]{0,1:T(8,128)S(1)}, u32[]{:S(2)}, u32[]{:S(2)}) collective-permute-start(f32[64,16]{0,1:T(8,128)S(1)} %add.27), channel_id=1, source_target_pairs={{0,128},{8,136},{16,144},{24,152},{32,160},{40,168},{48,176},{56,1... | collective-permute-start | bytes 12296 | tf_op jit(solution)/shard_map/ppermute | solution.py:30
  102.7 3.0 %fusion.10 = f32[64,256]{1,0:T(8,128)S(1)} fusion(f32[64,256]{1,0:T(8,128)S(1)} %fusion.13, bf16[2,256,4096]{2,1,0:T(8,128)(2,1)} %param.11, bf16[64,2,4096]{2,0,1:T(8,128)(2,1)S(1)} %maximum_select_fusion, f32[]{:T(128)} %bitcast), kind=kOutput, calls=%fused_computation.10 | convolution fusion | flops 134250496 | bytes 2753024 | tf_op jit(solution)/shard_map/qk,rk->qr/dot_general | solution.py:78
  (47 shorter events, 6.5 us)
Async XLA Ops:
  0.6 4.5 %copy-start = (bf16[2,2,384,512]{3,2,1,0:T(8,128)(2,1)S(1)}, bf16[2,2,384,512]{3,2,1,0:T(8,128)(2,1)}, u32[]{:S(2)}) copy-start(bf16[2,2,384,512]{3,2,1,0:T(8,128)(2,1)} %param.8) | copy-start | bytes 4718596
  0.6 4.5 %copy-start.1 = (bf16[512,64]{0,1:T(8,128)(2,1)S(1)}, bf16[512,64]{0,1:T(8,128)(2,1)}, u32[]{:S(2)}) copy-start(bf16[512,64]{0,1:T(8,128)(2,1)} %param.10) | copy-start | bytes 196612
  35.4 29.9 %copy-start.2 = (f32[2]{0:T(128)S(1)}, f32[2]{0:T(128)}, u32[]{:S(2)}) copy-start(f32[2]{0:T(128)} %param.12) | copy-start | bytes 28
  35.4 30.5 %copy-start.3 = (s32[256]{0:T(256)S(1)}, s32[256]{0:T(256)}, u32[]{:S(2)}) copy-start(s32[256]{0:T(256)} %param.13) | copy-start | bytes 3076
  36.1 8.3 %collective-permute-start = (bf16[2,2,4096]{2,0,1:T(2,128)(2,1)S(1)}, bf16[2,2,4096]{2,0,1:T(2,128)(2,1)S(1)}, u32[]{:S(2)}, u32[]{:S(2)}) collective-permute-start(bf16[2,2,4096]{2,0,1:T(2,128)(2,1)S(1)} %copy.40), channel_id=1, source_target_pairs={{0,128},{8,136},{16,144},{24,152},{32,160},{40,168},{48,176},{56,1... | collective-permute-start | bytes 98312 | tf_op jit(solution)/shard_map/ppermute | solution.py:42
  44.5 6.1 %collective-permute-start.1 = (bf16[4,2,4096]{2,0,1:T(4,128)(2,1)S(1)}, bf16[4,2,4096]{2,0,1:T(4,128)(2,1)S(1)}, u32[]{:S(2)}, u32[]{:S(2)}) collective-permute-start(bf16[4,2,4096]{2,0,1:T(4,128)(2,1)S(1)} %maximum_select_fusion.4), channel_id=1, source_target_pairs={{0,64},{8,72},{16,80},{24,88},{32,96},{40,104},{48,112},{56,120},{... | collective-permute-start | bytes 196616 | tf_op jit(solution)/shard_map/ppermute | solution.py:42
  50.7 8.0 %collective-permute-start.2 = (bf16[8,2,4096]{2,0,1:T(8,128)(2,1)S(1)}, bf16[8,2,4096]{2,0,1:T(8,128)(2,1)S(1)}, u32[]{:S(2)}, u32[]{:S(2)}) collective-permute-start(bf16[8,2,4096]{2,0,1:T(8,128)(2,1)S(1)} %maximum_select_fusion.3), channel_id=1, source_target_pairs={{0,32},{8,40},{16,48},{24,56},{32,0},{40,8},{48,16},{56,24},{64,96... | collective-permute-start | bytes 393224 | tf_op jit(solution)/shard_map/ppermute | solution.py:42
  58.7 6.5 %collective-permute-start.3 = (bf16[16,2,4096]{2,0,1:T(8,128)(2,1)S(1)}, bf16[16,2,4096]{2,0,1:T(8,128)(2,1)S(1)}, u32[]{:S(2)}, u32[]{:S(2)}) collective-permute-start(bf16[16,2,4096]{2,0,1:T(8,128)(2,1)S(1)} %maximum_select_fusion.2), channel_id=1, source_target_pairs={{0,16},{8,24},{16,0},{24,8},{32,48},{40,56},{48,32},{56,40},{64,80... | collective-permute-start | bytes 786440 | tf_op jit(solution)/shard_map/ppermute | solution.py:42
  65.2 3.5 %collective-permute-start.4 = (bf16[32,2,4096]{2,0,1:T(8,128)(2,1)S(1)}, bf16[32,2,4096]{2,0,1:T(8,128)(2,1)}, u32[]{:S(2)}, u32[]{:S(2)}) collective-permute-start(bf16[32,2,4096]{2,0,1:T(8,128)(2,1)S(1)} %maximum_select_fusion.1), channel_id=1, source_target_pairs={{0,8},{8,0},{16,24},{24,16},{32,40},{40,32},{48,56},{56,48},{64,72... | collective-permute-start | bytes 1572872 | tf_op jit(solution)/shard_map/ppermute | solution.py:42
  82.5 1.3 %collective-permute-start.5 = (f32[64,16]{0,1:T(8,128)S(1)}, f32[64,16]{0,1:T(8,128)S(1)}, u32[]{:S(2)}, u32[]{:S(2)}) collective-permute-start(f32[64,16]{0,1:T(8,128)S(1)} %bitcast_reduce_fusion), channel_id=1, source_target_pairs={{0,8},{8,0},{16,24},{24,16},{32,40},{40,32},{48,56},{56,48},{64,72... | collective-permute-start | bytes 12296 | tf_op jit(solution)/shard_map/ppermute | solution.py:30
  83.7 3.7 %collective-permute-start.6 = (f32[64,16]{0,1:T(8,128)S(1)}, f32[64,16]{0,1:T(8,128)S(1)}, u32[]{:S(2)}, u32[]{:S(2)}) collective-permute-start(f32[64,16]{0,1:T(8,128)S(1)} %add.24), channel_id=1, source_target_pairs={{0,16},{8,24},{16,0},{24,8},{32,48},{40,56},{48,32},{56,40},{64,80... | collective-permute-start | bytes 12296 | tf_op jit(solution)/shard_map/ppermute | solution.py:30
  87.4 5.2 %collective-permute-start.7 = (f32[64,16]{0,1:T(8,128)S(1)}, f32[64,16]{0,1:T(8,128)S(1)}, u32[]{:S(2)}, u32[]{:S(2)}) collective-permute-start(f32[64,16]{0,1:T(8,128)S(1)} %add.25), channel_id=1, source_target_pairs={{0,32},{8,40},{16,48},{24,56},{32,0},{40,8},{48,16},{56,24},{64,96... | collective-permute-start | bytes 12296 | tf_op jit(solution)/shard_map/ppermute | solution.py:30
  92.5 5.3 %collective-permute-start.8 = (f32[64,16]{0,1:T(8,128)S(1)}, f32[64,16]{0,1:T(8,128)S(1)}, u32[]{:S(2)}, u32[]{:S(2)}) collective-permute-start(f32[64,16]{0,1:T(8,128)S(1)} %add.26), channel_id=1, source_target_pairs={{0,64},{8,72},{16,80},{24,88},{32,96},{40,104},{48,112},{56,120},{... | collective-permute-start | bytes 12296 | tf_op jit(solution)/shard_map/ppermute | solution.py:30
  97.9 8.6 %collective-permute-start.9 = (f32[64,16]{0,1:T(8,128)S(1)}, f32[64,16]{0,1:T(8,128)S(1)}, u32[]{:S(2)}, u32[]{:S(2)}) collective-permute-start(f32[64,16]{0,1:T(8,128)S(1)} %add.27), channel_id=1, source_target_pairs={{0,128},{8,136},{16,144},{24,152},{32,160},{40,168},{48,176},{56,1... | collective-permute-start | bytes 12296 | tf_op jit(solution)/shard_map/ppermute | solution.py:30

commit v8 on v5

--- a/solution.py
+++ b/solution.py
@@ -67,9 +67,8 @@
     outer = outer.reshape(ex_local, 2, rank * rank)
     query = (outer / jnp.sqrt(jnp.float32(seq_len))).astype(jnp.bfloat16)
     piece = _doubling_gather(query, "dp", n_dp, 0, list(reversed(range(dp_bits))))
-    first = jnp.einsum("qk,rk->qr", piece[:, 0], store[0], preferred_element_type=jnp.float32)
-    second = jnp.einsum("qk,rk->qr", piece[:, 1], store[1], preferred_element_type=jnp.float32)
-    scores = ckpt_rate[0] * first + ckpt_rate[1] * second
+    by_ckpt = jnp.einsum("qck,crk->cqr", piece, store, preferred_element_type=jnp.float32)
+    scores = ckpt_rate[0] * by_ckpt[0] + ckpt_rate[1] * by_ckpt[1]
     member = (store_group[:, None] == jnp.arange(GROUPS, dtype=jnp.int32)[None, :]).astype(
         jnp.float32
     )

time: 106 us -> 108 us (1.019)
  local copies, waits for them, and re-layouts: 3.56 us -> 4.94 us
  other arithmetic: 1.43 us -> 2.53 us
    unnamed x14 -> x12, local copies, waits for them, and re-layouts: 0.9 us -> 2.28 us
    add x0 -> x1, other arithmetic: none -> 1.31 us  [shards(): scores = ckpt_rate[0] * by_ckpt[0] + ckpt_rate[1] * by_ckpt[1]]
    dot_general x2 -> x1, matrix products: 4.41 us -> 3.58 us  [shards(): jnp.einsum('qck,crk->cqr', piece, store, preferred_element_type=jnp.float32)]
where the time goes in v8:
time: 108 us
  blocking collectives  37.8 us (35%)
  waiting for transfers between devices  30 us (28%)
  starting transfers between devices  21.6 us (20%)
  matrix products  9.93 us (9%)
  local copies, waits for them, and re-layouts  4.94 us (5%)
  other arithmetic  2.53 us (2%)
    all_to_all x1, blocking collectives, shards(): lax.all_to_all(stacked.reshape(c, e, n_mp, t // n_mp, r), 'mp', 2, 2, til...  18.4 us
    ppermute x5, waiting for transfers between devices, _doubling_gather(): x = _join(x, lax.ppermute(x, axis, _swap(n, bit)), upper, dim)  18.3 us
    ppermute x5, starting transfers between devices, _doubling_gather(): x = _join(x, lax.ppermute(x, axis, _swap(n, bit)), upper, dim)  11.8 us
    ppermute x5, waiting for transfers between devices, _butterfly_sum(): x = x + lax.ppermute(x, axis, _swap(n, bit))  11.7 us
    all_to_all x1, blocking collectives, shards(): low = lax.all_to_all(copies, 'mp', 2, 2, tiled=True).reshape(c, e, t, r)  10.7 us
    ppermute x5, starting transfers between devices, _butterfly_sum(): x = x + lax.ppermute(x, axis, _swap(n, bit))  9.83 us
    all_to_all x1, blocking collectives, shards(): totals = lax.all_to_all(copies, 'mp', 0, 0, tiled=True).sum(0)  8.63 us
    dot_general x1, matrix products, shards(): jnp.einsum('cesf,fr->cesr', activations, proj_in, preferred_element_type=...  4.32 us
  transfers between devices with their start and end apart: 10, of which 10 were waited for; matrix products, arithmetic and copies ran while one was open for 1% of the time, Pallas kernels for 0%

profile of v8, /device:TPU:24, one launch (start us, length us, event | category | flops | bytes accessed | tf_op | source)
XLA Modules:
  0.0 107.6 jit_solution(13550162698357629780)
XLA Ops:
  0.7 1.4 %copy-done = bf16[2,2,384,512]{3,2,1,0:T(8,128)(2,1)S(1)} copy-done((bf16[2,2,384,512]{3,2,1,0:T(8,128)(2,1)S(1)}, bf16[2,2,384,512]{3,2,1,0:T(8,128)(2,1)}, u32[]{:S(2)}) %copy-start) | copy-done | bytes 1572888
  2.0 1.4 %fusion.14 = f32[2,2,384,64]{2,3,1,0:T(8,128)S(1)} fusion(bf16[2,2,384,512]{3,2,1,0:T(8,128)(2,1)S(1)} %copy-done, bf16[512,64]{0,1:T(8,128)(2,1)} %param.10), kind=kOutput, calls=%fused_computation.24 | convolution fusion | flops 100663296 | bytes 2031616 | tf_op jit(solution)/shard_map/cesf,fr->cesr/dot_general | solution.py:55
  3.5 4.3 %fusion.10 = f32[2,2,384,64]{2,3,1,0:T(8,128)S(1)} fusion(bf16[2,2,384,1792]{3,2,1,0:T(8,128)(2,1)} %param.7, bf16[1792,64]{0,1:T(8,128)(2,1)S(1)} %copy-done.1), kind=kOutput, calls=%fused_computation.15 | convolution fusion | flops 352321536 | bytes 6127616 | tf_op jit(solution)/shard_map/cesf,fr->cesr/dot_general | solution.py:54
  8.2 18.4 %all_to_all.15 = f32[2,2,8,48,128]{4,3,1,0,2:T(8,128)S(1)} all-to-all(f32[2,2,8,48,128]{4,3,1,0,2:T(8,128)S(1)} %copy.36), channel_id=1, replica_groups=mesh['dp'=32,'mp'=8] {'mp'}, dimensions={2} | all-to-all | bytes 1572864 | tf_op jit(solution)/shard_map/all_to_all | solution.py:58
  26.8 10.7 %all_to_all.16 = bf16[2,2,8,48,128]{4,3,1,0,2:T(8,128)(2,1)S(1)} all-to-all(bf16[2,2,8,48,128]{4,3,1,0,2:T(8,128)(2,1)S(1)} %broadcast_in_dim.4), channel_id=1, replica_groups=mesh['dp'=32,'mp'=8] {'mp'}, dimensions={2} | all-to-all | bytes 786432 | tf_op jit(solution)/shard_map/all_to_all | solution.py:63
  38.1 6.4 %collective-permute-start = (bf16[2,2,4096]{2,0,1:T(2,128)(2,1)S(1)}, bf16[2,2,4096]{2,0,1:T(2,128)(2,1)S(1)}, u32[]{:S(2)}, u32[]{:S(2)}) collective-permute-start(bf16[2,2,4096]{2,0,1:T(2,128)(2,1)S(1)} %copy.40), channel_id=1, source_target_pairs={{0,128},{8,136},{16,144},{24,152},{32,160},{40,168},{48,176},{56,1... | collective-permute-start | bytes 98312 | tf_op jit(solution)/shard_map/ppermute | solution.py:42
  44.5 1.9 %collective-permute-done = bf16[2,2,4096]{2,0,1:T(2,128)(2,1)S(1)} collective-permute-done((bf16[2,2,4096]{2,0,1:T(2,128)(2,1)S(1)}, bf16[2,2,4096]{2,0,1:T(2,128)(2,1)S(1)}, u32[]{:S(2)}, u32[]{:S(2)}) %collective-permute-start) | collective-permute-done | bytes 32800 | tf_op jit(solution)/shard_map/ppermute | solution.py:42
  46.5 3.1 %collective-permute-start.1 = (bf16[4,2,4096]{2,0,1:T(4,128)(2,1)S(1)}, bf16[4,2,4096]{2,0,1:T(4,128)(2,1)S(1)}, u32[]{:S(2)}, u32[]{:S(2)}) collective-permute-start(bf16[4,2,4096]{2,0,1:T(4,128)(2,1)S(1)} %maximum_select_fusion.5), channel_id=1, source_target_pairs={{0,64},{8,72},{16,80},{24,88},{32,96},{40,104},{48,112},{56,120},{... | collective-permute-start | bytes 196616 | tf_op jit(solution)/shard_map/ppermute | solution.py:42
  49.7 2.9 %collective-permute-done.1 = bf16[4,2,4096]{2,0,1:T(4,128)(2,1)S(1)} collective-permute-done((bf16[4,2,4096]{2,0,1:T(4,128)(2,1)S(1)}, bf16[4,2,4096]{2,0,1:T(4,128)(2,1)S(1)}, u32[]{:S(2)}, u32[]{:S(2)}) %collective-permute-start.1) | collective-permute-done | bytes 65568 | tf_op jit(solution)/shard_map/ppermute | solution.py:42
  52.7 1.4 %collective-permute-start.2 = (bf16[8,2,4096]{2,0,1:T(8,128)(2,1)S(1)}, bf16[8,2,4096]{2,0,1:T(8,128)(2,1)S(1)}, u32[]{:S(2)}, u32[]{:S(2)}) collective-permute-start(bf16[8,2,4096]{2,0,1:T(8,128)(2,1)S(1)} %maximum_select_fusion.4), channel_id=1, source_target_pairs={{0,32},{8,40},{16,48},{24,56},{32,0},{40,8},{48,16},{56,24},{64,96... | collective-permute-start | bytes 393224 | tf_op jit(solution)/shard_map/ppermute | solution.py:42
  54.1 6.6 %collective-permute-done.2 = bf16[8,2,4096]{2,0,1:T(8,128)(2,1)S(1)} collective-permute-done((bf16[8,2,4096]{2,0,1:T(8,128)(2,1)S(1)}, bf16[8,2,4096]{2,0,1:T(8,128)(2,1)S(1)}, u32[]{:S(2)}, u32[]{:S(2)}) %collective-permute-start.2) | collective-permute-done | bytes 131104 | tf_op jit(solution)/shard_map/ppermute | solution.py:42
  61.6 5.6 %collective-permute-done.3 = bf16[16,2,4096]{2,0,1:T(8,128)(2,1)S(1)} collective-permute-done((bf16[16,2,4096]{2,0,1:T(8,128)(2,1)S(1)}, bf16[16,2,4096]{2,0,1:T(8,128)(2,1)S(1)}, u32[]{:S(2)}, u32[]{:S(2)}) %collective-permute-start.3) | collective-permute-done | bytes 262176 | tf_op jit(solution)/shard_map/ppermute | solution.py:42
  68.0 1.3 %collective-permute-done.4 = bf16[32,2,4096]{2,0,1:T(8,128)(2,1)S(1)} collective-permute-done((bf16[32,2,4096]{2,0,1:T(8,128)(2,1)S(1)}, bf16[32,2,4096]{2,0,1:T(8,128)(2,1)S(1)}, u32[]{:S(2)}, u32[]{:S(2)}) %collective-permute-start.4) | collective-permute-done | bytes 524320 | tf_op jit(solution)/shard_map/ppermute | solution.py:42
  69.3 3.6 %fusion.1 = f32[2,64,256]{2,1,0:T(8,128)S(1)} fusion(bf16[2,256,4096]{2,1,0:T(8,128)(2,1)} %param.11, bf16[32,2,4096]{2,0,1:T(8,128)(2,1)S(1)} %maximum_select_fusion.2, bf16[32,2,4096]{2,0,1:T(8,128)(2,1)S(1)} %collective-permute-done.4, pred[]{:T(512)S(6)} %eq.28), kind=kOutput, calls=%fused_computation.3 | convolution fusion | flops 273154048 | bytes 5373953 | tf_op jit(solution)/shard_map/qck,crk->cqr/dot_general | solution.py:70
  72.9 1.3 %fusion.13 = f32[1,64,256]{2,1,0:T(8,128)S(1)} fusion(f32[2,64,256]{2,1,0:T(8,128)S(1)} %fusion.1, f32[]{:T(128)} %bitcast.7, f32[]{:T(128)} %bitcast), kind=kLoop, calls=%fused_computation.21 | loop fusion | flops 49152 | bytes 196616 | tf_op jit(solution)/shard_map/add | solution.py:71
  74.6 8.6 %all_to_all.17 = f32[8,1,1024]{2,1,0:T(1,128)S(1)} all-to-all(f32[8,1,1024]{2,1,0:T(1,128)S(1)} %reshape.46), channel_id=1, replica_groups=mesh['dp'=32,'mp'=8] {'mp'}, dimensions={0} | all-to-all | bytes 65536 | tf_op jit(solution)/shard_map/all_to_all | solution.py:77
  84.7 1.2 %collective-permute-done.5 = f32[64,16]{0,1:T(8,128)S(1)} collective-permute-done((f32[64,16]{0,1:T(8,128)S(1)}, f32[64,16]{0,1:T(8,128)S(1)}, u32[]{:S(2)}, u32[]{:S(2)}) %collective-permute-start.5) | collective-permute-done | bytes 4128 | tf_op jit(solution)/shard_map/ppermute | solution.py:30
  86.6 2.9 %collective-permute-done.6 = f32[64,16]{0,1:T(8,128)S(1)} collective-permute-done((f32[64,16]{0,1:T(8,128)S(1)}, f32[64,16]{0,1:T(8,128)S(1)}, u32[]{:S(2)}, u32[]{:S(2)}) %collective-permute-start.6) | collective-permute-done | bytes 4128 | tf_op jit(solution)/shard_map/ppermute | solution.py:30
  89.5 1.3 %collective-permute-start.7 = (f32[64,16]{0,1:T(8,128)S(1)}, f32[64,16]{0,1:T(8,128)S(1)}, u32[]{:S(2)}, u32[]{:S(2)}) collective-permute-start(f32[64,16]{0,1:T(8,128)S(1)} %add.29), channel_id=1, source_target_pairs={{0,32},{8,40},{16,48},{24,56},{32,0},{40,8},{48,16},{56,24},{64,96... | collective-permute-start | bytes 12296 | tf_op jit(solution)/shard_map/ppermute | solution.py:30
  90.8 3.9 %collective-permute-done.7 = f32[64,16]{0,1:T(8,128)S(1)} collective-permute-done((f32[64,16]{0,1:T(8,128)S(1)}, f32[64,16]{0,1:T(8,128)S(1)}, u32[]{:S(2)}, u32[]{:S(2)}) %collective-permute-start.7) | collective-permute-done | bytes 4128 | tf_op jit(solution)/shard_map/ppermute | solution.py:30
  94.7 2.3 %collective-permute-start.8 = (f32[64,16]{0,1:T(8,128)S(1)}, f32[64,16]{0,1:T(8,128)S(1)}, u32[]{:S(2)}, u32[]{:S(2)}) collective-permute-start(f32[64,16]{0,1:T(8,128)S(1)} %add.30), channel_id=1, source_target_pairs={{0,64},{8,72},{16,80},{24,88},{32,96},{40,104},{48,112},{56,120},{... | collective-permute-start | bytes 12296 | tf_op jit(solution)/shard_map/ppermute | solution.py:30
  97.0 2.2 %collective-permute-done.8 = f32[64,16]{0,1:T(8,128)S(1)} collective-permute-done((f32[64,16]{0,1:T(8,128)S(1)}, f32[64,16]{0,1:T(8,128)S(1)}, u32[]{:S(2)}, u32[]{:S(2)}) %collective-permute-start.8) | collective-permute-done | bytes 4128 | tf_op jit(solution)/shard_map/ppermute | solution.py:30
  99.2 5.4 %collective-permute-start.9 = (f32[64,16]{0,1:T(8,128)S(1)}, f32[64,16]{0,1:T(8,128)S(1)}, u32[]{:S(2)}, u32[]{:S(2)}) collective-permute-start(f32[64,16]{0,1:T(8,128)S(1)} %add.31), channel_id=1, source_target_pairs={{0,128},{8,136},{16,144},{24,152},{32,160},{40,168},{48,176},{56,1... | collective-permute-start | bytes 12296 | tf_op jit(solution)/shard_map/ppermute | solution.py:30
  105.3 1.5 %collective-permute-done.9 = f32[64,16]{0,1:T(8,128)S(1)} collective-permute-done((f32[64,16]{0,1:T(8,128)S(1)}, f32[64,16]{0,1:T(8,128)S(1)}, u32[]{:S(2)}, u32[]{:S(2)}) %collective-permute-start.9) | collective-permute-done | bytes 4128 | tf_op jit(solution)/shard_map/ppermute | solution.py:30
  (44 shorter events, 7.1 us)
Async XLA Ops:
  0.6 1.4 %copy-start = (bf16[2,2,384,512]{3,2,1,0:T(8,128)(2,1)S(1)}, bf16[2,2,384,512]{3,2,1,0:T(8,128)(2,1)}, u32[]{:S(2)}) copy-start(bf16[2,2,384,512]{3,2,1,0:T(8,128)(2,1)} %param.8) | copy-start | bytes 4718596
  0.6 2.8 %copy-start.1 = (bf16[1792,64]{0,1:T(8,128)(2,1)S(1)}, bf16[1792,64]{0,1:T(8,128)(2,1)}, u32[]{:S(2)}) copy-start(bf16[1792,64]{0,1:T(8,128)(2,1)} %param.9) | copy-start | bytes 688132
  37.5 29.9 %copy-start.2 = (f32[2]{0:T(128)S(1)}, f32[2]{0:T(128)}, u32[]{:S(2)}) copy-start(f32[2]{0:T(128)} %param.12) | copy-start | bytes 28
  38.1 8.3 %collective-permute-start = (bf16[2,2,4096]{2,0,1:T(2,128)(2,1)S(1)}, bf16[2,2,4096]{2,0,1:T(2,128)(2,1)S(1)}, u32[]{:S(2)}, u32[]{:S(2)}) collective-permute-start(bf16[2,2,4096]{2,0,1:T(2,128)(2,1)S(1)} %copy.40), channel_id=1, source_target_pairs={{0,128},{8,136},{16,144},{24,152},{32,160},{40,168},{48,176},{56,1... | collective-permute-start | bytes 98312 | tf_op jit(solution)/shard_map/ppermute | solution.py:42
  46.5 6.1 %collective-permute-start.1 = (bf16[4,2,4096]{2,0,1:T(4,128)(2,1)S(1)}, bf16[4,2,4096]{2,0,1:T(4,128)(2,1)S(1)}, u32[]{:S(2)}, u32[]{:S(2)}) collective-permute-start(bf16[4,2,4096]{2,0,1:T(4,128)(2,1)S(1)} %maximum_select_fusion.5), channel_id=1, source_target_pairs={{0,64},{8,72},{16,80},{24,88},{32,96},{40,104},{48,112},{56,120},{... | collective-permute-start | bytes 196616 | tf_op jit(solution)/shard_map/ppermute | solution.py:42
  52.7 8.0 %collective-permute-start.2 = (bf16[8,2,4096]{2,0,1:T(8,128)(2,1)S(1)}, bf16[8,2,4096]{2,0,1:T(8,128)(2,1)S(1)}, u32[]{:S(2)}, u32[]{:S(2)}) collective-permute-start(bf16[8,2,4096]{2,0,1:T(8,128)(2,1)S(1)} %maximum_select_fusion.4), channel_id=1, source_target_pairs={{0,32},{8,40},{16,48},{24,56},{32,0},{40,8},{48,16},{56,24},{64,96... | collective-permute-start | bytes 393224 | tf_op jit(solution)/shard_map/ppermute | solution.py:42
  60.7 6.5 %collective-permute-start.3 = (bf16[16,2,4096]{2,0,1:T(8,128)(2,1)S(1)}, bf16[16,2,4096]{2,0,1:T(8,128)(2,1)S(1)}, u32[]{:S(2)}, u32[]{:S(2)}) collective-permute-start(bf16[16,2,4096]{2,0,1:T(8,128)(2,1)S(1)} %maximum_select_fusion.3), channel_id=1, source_target_pairs={{0,16},{8,24},{16,0},{24,8},{32,48},{40,56},{48,32},{56,40},{64,80... | collective-permute-start | bytes 786440 | tf_op jit(solution)/shard_map/ppermute | solution.py:42
  67.3 2.0 %collective-permute-start.4 = (bf16[32,2,4096]{2,0,1:T(8,128)(2,1)S(1)}, bf16[32,2,4096]{2,0,1:T(8,128)(2,1)S(1)}, u32[]{:S(2)}, u32[]{:S(2)}) collective-permute-start(bf16[32,2,4096]{2,0,1:T(8,128)(2,1)S(1)} %maximum_select_fusion.2), channel_id=1, source_target_pairs={{0,8},{8,0},{16,24},{24,16},{32,40},{40,32},{48,56},{56,48},{64,72... | collective-permute-start | bytes 1572872 | tf_op jit(solution)/shard_map/ppermute | solution.py:42
  68.0 6.2 %copy-start.3 = (s32[256]{0:T(256)S(1)}, s32[256]{0:T(256)}, u32[]{:S(2)}) copy-start(s32[256]{0:T(256)} %param.13) | copy-start | bytes 3076
  84.6 1.3 %collective-permute-start.5 = (f32[64,16]{0,1:T(8,128)S(1)}, f32[64,16]{0,1:T(8,128)S(1)}, u32[]{:S(2)}, u32[]{:S(2)}) collective-permute-start(f32[64,16]{0,1:T(8,128)S(1)} %bitcast_reduce_fusion), channel_id=1, source_target_pairs={{0,8},{8,0},{16,24},{24,16},{32,40},{40,32},{48,56},{56,48},{64,72... | collective-permute-start | bytes 12296 | tf_op jit(solution)/shard_map/ppermute | solution.py:30
  85.9 3.7 %collective-permute-start.6 = (f32[64,16]{0,1:T(8,128)S(1)}, f32[64,16]{0,1:T(8,128)S(1)}, u32[]{:S(2)}, u32[]{:S(2)}) collective-permute-start(f32[64,16]{0,1:T(8,128)S(1)} %add.28), channel_id=1, source_target_pairs={{0,16},{8,24},{16,0},{24,8},{32,48},{40,56},{48,32},{56,40},{64,80... | collective-permute-start | bytes 12296 | tf_op jit(solution)/shard_map/ppermute | solution.py:30
  89.5 5.2 %collective-permute-start.7 = (f32[64,16]{0,1:T(8,128)S(1)}, f32[64,16]{0,1:T(8,128)S(1)}, u32[]{:S(2)}, u32[]{:S(2)}) collective-permute-start(f32[64,16]{0,1:T(8,128)S(1)} %add.29), channel_id=1, source_target_pairs={{0,32},{8,40},{16,48},{24,56},{32,0},{40,8},{48,16},{56,24},{64,96... | collective-permute-start | bytes 12296 | tf_op jit(solution)/shard_map/ppermute | solution.py:30
  94.7 4.5 %collective-permute-start.8 = (f32[64,16]{0,1:T(8,128)S(1)}, f32[64,16]{0,1:T(8,128)S(1)}, u32[]{:S(2)}, u32[]{:S(2)}) collective-permute-start(f32[64,16]{0,1:T(8,128)S(1)} %add.30), channel_id=1, source_target_pairs={{0,64},{8,72},{16,80},{24,88},{32,96},{40,104},{48,112},{56,120},{... | collective-permute-start | bytes 12296 | tf_op jit(solution)/shard_map/ppermute | solution.py:30
  99.2 7.6 %collective-permute-start.9 = (f32[64,16]{0,1:T(8,128)S(1)}, f32[64,16]{0,1:T(8,128)S(1)}, u32[]{:S(2)}, u32[]{:S(2)}) collective-permute-start(f32[64,16]{0,1:T(8,128)S(1)} %add.31), channel_id=1, source_target_pairs={{0,128},{8,136},{16,144},{24,152},{32,160},{40,168},{48,176},{56,1... | collective-permute-start | bytes 12296 | tf_op jit(solution)/shard_map/ppermute | solution.py:30

commit v9 on v5

--- a/solution.py
+++ b/solution.py
@@ -43,6 +43,31 @@
     return x
 
 
+def _dp_steps(n):
+    bits = _bits(n)
+    steps = []
+    lo = bits - 2
+    while lo >= 1:
+        steps += [(3 << lo, (lo + 1,)), (1 << lo, (lo, lo + 1))]
+        lo -= 2
+    for b in reversed(range(lo + 2)):
+        steps.append((1 << b, (b,)))
+    return steps
+
+
+def _natural_rows(steps, n, ex_local):
+    held = [[d] for d in range(n)]
+    for mask, upper_bits in steps:
+        held = [
+            held[d ^ mask] + held[d] if sum(d >> b for b in upper_bits) & 1 else held[d] + held[d ^ mask]
+            for d in range(n)
+        ]
+    order = held[0]
+    assert all(h == order for h in held) and sorted(order) == list(range(n))
+    where = {d: p for p, d in enumerate(order)}
+    return [where[d] * ex_local + e for d in range(n) for e in range(ex_local)]
+
+
 def shards(activations, out_grads, proj_in, proj_out, store, ckpt_rate, store_group):
     n_dp = lax.axis_size("dp")
     n_mp = lax.axis_size("mp")
@@ -66,7 +91,13 @@
     )
     outer = outer.reshape(ex_local, 2, rank * rank)
     query = (outer / jnp.sqrt(jnp.float32(seq_len))).astype(jnp.bfloat16)
-    piece = _doubling_gather(query, "dp", n_dp, 0, list(reversed(range(dp_bits))))
+    steps = _dp_steps(n_dp)
+    me = lax.axis_index("dp")
+    piece = query
+    for mask, upper_bits in steps:
+        upper = (sum((me >> b) for b in upper_bits) & 1) == 1
+        other = lax.ppermute(piece, "dp", [(i, i ^ mask) for i in range(n_dp)])
+        piece = _join(piece, other, upper, 0)
     first = jnp.einsum("qk,rk->qr", piece[:, 0], store[0], preferred_element_type=jnp.float32)
     second = jnp.einsum("qk,rk->qr", piece[:, 1], store[1], preferred_element_type=jnp.float32)
     scores = ckpt_rate[0] * first + ckpt_rate[1] * second
@@ -76,12 +107,13 @@
     partial_totals = jnp.dot(scores, member, precision=lax.Precision.HIGHEST)
     copies = jnp.broadcast_to(partial_totals[None], (n_mp,) + partial_totals.shape)
     totals = lax.all_to_all(copies, "mp", 0, 0, tiled=True).sum(0)
-    totals = _butterfly_sum(totals, "dp", n_dp, list(range(dp_bits)))
+    for mask, _ in reversed(steps):
+        totals = totals + lax.ppermute(totals, "dp", [(i, i ^ mask) for i in range(n_dp)])
+
+    rows = jnp.asarray(_natural_rows(steps, n_dp, ex_local), jnp.int32)
 
     def natural(x):
-        x = x.reshape((2,) * dp_bits + (ex_local,) + x.shape[1:])
-        perm = list(reversed(range(dp_bits))) + list(range(dp_bits, x.ndim))
-        return jnp.transpose(x, perm).reshape((n_dp * ex_local,) + x.shape[dp_bits + 1 :])
+        return jnp.take(x, rows, axis=0)
 
     scores = natural(scores)
     store_rows = store.shape[1] * n_dp * n_mp

time: 106 us -> 103 us (0.972)
  starting transfers between devices: 21.5 us -> 14.5 us
  waiting for transfers between devices: 30.1 us -> 33.1 us
  local copies, waits for them, and re-layouts: 3.56 us -> 4.7 us
    ppermute x10, starting transfers between devices: 21.5 us -> 14.5 us  [the longest x5 8.43 us: shards(): other = lax.ppermute(piece, 'dp', [(i, i ^ mask) for i in range(n_dp)])]
    ppermute x10, waiting for transfers between devices: 30.1 us -> 33.1 us  [the longest x5 19 us: shards(): other = lax.ppermute(piece, 'dp', [(i, i ^ mask) for i in range(n_dp)])]
    gather x0 -> x2, local copies, waits for them, and re-layouts: none -> 1.87 us  [natural(): return jnp.take(x, rows, axis=0)]
  transfers between devices with their start and end apart: 10 -> 10, of which waited for: 10 -> 10; matrix products, arithmetic and copies ran while one was open for 1% -> 2% of each run, Pallas kernels for 0% -> 0%
where the time goes in v9:
time: 103 us; the launch traced here: 102 us
  blocking collectives  37.8 us (37%)
  waiting for transfers between devices  33.1 us (32%)
  starting transfers between devices  14.5 us (14%)
  matrix products  10 us (10%)
  local copies, waits for them, and re-layouts  4.7 us (5%)
  other arithmetic  1.45 us (1%)
    ppermute x5, waiting for transfers between devices, shards(): other = lax.ppermute(piece, 'dp', [(i, i ^ mask) for i in range(n_dp)])  19 us
    all_to_all x1, blocking collectives, shards(): lax.all_to_all(stacked.reshape(c, e, n_mp, t // n_mp, r), 'mp', 2, 2, til...  18.4 us
    ppermute x5, waiting for transfers between devices, shards(): lax.ppermute(totals, 'dp', [(i, i ^ mask) for i in range(n_dp)])  14.1 us
    all_to_all x1, blocking collectives, shards(): low = lax.all_to_all(copies, 'mp', 2, 2, tiled=True).reshape(c, e, t, r)  10.7 us
    all_to_all x1, blocking collectives, shards(): totals = lax.all_to_all(copies, 'mp', 0, 0, tiled=True).sum(0)  8.63 us
    ppermute x5, starting transfers between devices, shards(): other = lax.ppermute(piece, 'dp', [(i, i ^ mask) for i in range(n_dp)])  8.43 us
    ppermute x5, starting transfers between devices, shards(): lax.ppermute(totals, 'dp', [(i, i ^ mask) for i in range(n_dp)])  6.11 us
    dot_general x1, matrix products, shards(): jnp.einsum('cesf,fr->cesr', activations, proj_in, preferred_element_type=...  4.44 us
  transfers between devices with their start and end apart: 10, of which 10 were waited for; matrix products, arithmetic and copies ran while one was open for 2% of the time, Pallas kernels for 0%

profile of v9, /device:TPU:24, one launch (start us, length us, event | category | flops | bytes accessed | tf_op | source)
XLA Modules:
  0.0 102.5 jit_solution(9470868222866997260)
XLA Ops:
  0.7 4.4 %fusion.18 = f32[2,2,384,64]{2,3,1,0:T(8,128)S(1)} fusion(bf16[2,2,384,1792]{3,2,1,0:T(8,128)(2,1)} %param.8, bf16[1792,64]{0,1:T(8,128)(2,1)} %param.10), kind=kOutput, calls=%fused_computation.21 | convolution fusion | flops 352321536 | bytes 6127616 | tf_op jit(solution)/shard_map/cesf,fr->cesr/dot_general | solution.py:79
  6.1 18.4 %all_to_all.15 = f32[2,2,8,48,128]{4,3,1,0,2:T(8,128)S(1)} all-to-all(f32[2,2,8,48,128]{4,3,1,0,2:T(8,128)S(1)} %copy.30), channel_id=1, replica_groups=mesh['dp'=32,'mp'=8] {'mp'}, dimensions={2} | all-to-all | bytes 1572864 | tf_op jit(solution)/shard_map/all_to_all | solution.py:83
  24.7 10.7 %all_to_all.16 = bf16[2,2,8,48,128]{4,3,1,0,2:T(8,128)(2,1)S(1)} all-to-all(bf16[2,2,8,48,128]{4,3,1,0,2:T(8,128)(2,1)S(1)} %broadcast_in_dim.37), channel_id=1, replica_groups=mesh['dp'=32,'mp'=8] {'mp'}, dimensions={2} | all-to-all | bytes 786432 | tf_op jit(solution)/shard_map/all_to_all | solution.py:88
  36.0 5.5 %collective-permute-start = (bf16[2,2,4096]{2,0,1:T(2,128)(2,1)S(1)}, bf16[2,2,4096]{2,0,1:T(2,128)(2,1)S(1)}, u32[]{:S(2)}, u32[]{:S(2)}) collective-permute-start(bf16[2,2,4096]{2,0,1:T(2,128)(2,1)S(1)} %copy.34), channel_id=1, source_target_pairs={{0,192},{8,200},{16,208},{24,216},{32,224},{40,232},{48,240},{56,2... | collective-permute-start | bytes 98312 | tf_op jit(solution)/shard_map/ppermute | solution.py:99
  41.5 1.9 %collective-permute-done = bf16[2,2,4096]{2,0,1:T(2,128)(2,1)S(1)} collective-permute-done((bf16[2,2,4096]{2,0,1:T(2,128)(2,1)S(1)}, bf16[2,2,4096]{2,0,1:T(2,128)(2,1)S(1)}, u32[]{:S(2)}, u32[]{:S(2)}) %collective-permute-start) | collective-permute-done | bytes 32800 | tf_op jit(solution)/shard_map/ppermute | solution.py:99
  43.6 2.4 %collective-permute-start.1 = (bf16[4,2,4096]{2,0,1:T(4,128)(2,1)S(1)}, bf16[4,2,4096]{2,0,1:T(4,128)(2,1)S(1)}, u32[]{:S(2)}, u32[]{:S(2)}) collective-permute-start(bf16[4,2,4096]{2,0,1:T(4,128)(2,1)S(1)} %maximum_select_fusion.4), channel_id=1, source_target_pairs={{0,64},{8,72},{16,80},{24,88},{32,96},{40,104},{48,112},{56,120},{... | collective-permute-start | bytes 196616 | tf_op jit(solution)/shard_map/ppermute | solution.py:99
  46.0 3.5 %collective-permute-done.1 = bf16[4,2,4096]{2,0,1:T(4,128)(2,1)S(1)} collective-permute-done((bf16[4,2,4096]{2,0,1:T(4,128)(2,1)S(1)}, bf16[4,2,4096]{2,0,1:T(4,128)(2,1)S(1)}, u32[]{:S(2)}, u32[]{:S(2)}) %collective-permute-start.1) | collective-permute-done | bytes 65568 | tf_op jit(solution)/shard_map/ppermute | solution.py:99
  50.0 6.0 %collective-permute-done.2 = bf16[8,2,4096]{2,0,1:T(8,128)(2,1)S(1)} collective-permute-done((bf16[8,2,4096]{2,0,1:T(8,128)(2,1)S(1)}, bf16[8,2,4096]{2,0,1:T(8,128)(2,1)S(1)}, u32[]{:S(2)}, u32[]{:S(2)}) %collective-permute-start.2) | collective-permute-done | bytes 131104 | tf_op jit(solution)/shard_map/ppermute | solution.py:99
  56.1 6.4 %collective-permute-done.3 = bf16[16,2,4096]{2,0,1:T(8,128)(2,1)S(1)} collective-permute-done((bf16[16,2,4096]{2,0,1:T(8,128)(2,1)S(1)}, bf16[16,2,4096]{2,0,1:T(8,128)(2,1)S(1)}, u32[]{:S(2)}, u32[]{:S(2)}) %collective-permute-start.3) | collective-permute-done | bytes 262176 | tf_op jit(solution)/shard_map/ppermute | solution.py:99
  63.2 1.3 %collective-permute-done.4 = bf16[32,2,4096]{2,0,1:T(8,128)(2,1)S(1)} collective-permute-done((bf16[32,2,4096]{2,0,1:T(8,128)(2,1)S(1)}, bf16[32,2,4096]{2,0,1:T(8,128)(2,1)S(1)}, u32[]{:S(2)}, u32[]{:S(2)}) %collective-permute-start.4) | collective-permute-done | bytes 524320 | tf_op jit(solution)/shard_map/ppermute | solution.py:99
  64.7 3.0 %fusion.13 = f32[64,256]{1,0:T(8,128)S(1)} fusion(bf16[2,256,4096]{2,1,0:T(8,128)(2,1)} %param.12, bf16[64,2,4096]{2,0,1:T(8,128)(2,1)S(1)} %maximum_select_fusion, f32[]{:T(128)} %bitcast.9), kind=kOutput, calls=%fused_computation.12 | convolution fusion | flops 134234112 | bytes 2687488 | tf_op jit(solution)/shard_map/qk,rk->qr/dot_general | solution.py:102
  67.7 1.4 %fusion.10 = f32[64,256]{1,0:T(8,128)S(1)} fusion(f32[64,256]{1,0:T(8,128)S(1)} %fusion.13, bf16[2,256,4096]{2,1,0:T(8,128)(2,1)S(1)} %copy-done.5, bf16[64,2,4096]{2,0,1:T(8,128)(2,1)S(1)} %maximum_select_fusion, f32[]{:T(128)} %bitcast), kind=kOutput, calls=%fused_computation.11 | convolution fusion | flops 134250496 | bytes 2752516 | tf_op jit(solution)/shard_map/qk,rk->qr/dot_general | solution.py:101
  69.6 8.6 %all_to_all.17 = f32[8,1,1024]{2,1,0:T(1,128)S(1)} all-to-all(f32[8,1,1024]{2,1,0:T(1,128)S(1)} %reshape.44), channel_id=1, replica_groups=mesh['dp'=32,'mp'=8] {'mp'}, dimensions={0} | all-to-all | bytes 65536 | tf_op jit(solution)/shard_map/all_to_all | solution.py:109
  78.7 0.7 reduce
  79.7 1.2 %collective-permute-done.5 = f32[64,16]{1,0:T(8,128)S(1)} collective-permute-done((f32[64,16]{1,0:T(8,128)S(1)}, f32[64,16]{1,0:T(8,128)S(1)}, u32[]{:S(2)}, u32[]{:S(2)}) %collective-permute-start.5) | collective-permute-done | bytes 4128 | tf_op jit(solution)/shard_map/ppermute | solution.py:111
  80.9 3.9 %collective-permute-done.6 = f32[64,16]{1,0:T(8,128)S(1)} collective-permute-done((f32[64,16]{1,0:T(8,128)S(1)}, f32[64,16]{1,0:T(8,128)S(1)}, u32[]{:S(2)}, u32[]{:S(2)}) %collective-permute-start.6) | collective-permute-done | bytes 4128 | tf_op jit(solution)/shard_map/ppermute | solution.py:111
  85.1 4.9 %collective-permute-done.7 = f32[64,16]{1,0:T(8,128)S(1)} collective-permute-done((f32[64,16]{1,0:T(8,128)S(1)}, f32[64,16]{1,0:T(8,128)S(1)}, u32[]{:S(2)}, u32[]{:S(2)}) %collective-permute-start.7) | collective-permute-done | bytes 4128 | tf_op jit(solution)/shard_map/ppermute | solution.py:111
  90.0 1.6 %collective-permute-start.8 = (f32[64,16]{1,0:T(8,128)S(1)}, f32[64,16]{1,0:T(8,128)S(1)}, u32[]{:S(2)}, u32[]{:S(2)}) collective-permute-start(f32[64,16]{1,0:T(8,128)S(1)} %add.43), channel_id=1, source_target_pairs={{0,64},{8,72},{16,80},{24,88},{32,96},{40,104},{48,112},{56,120},{... | collective-permute-start | bytes 12296 | tf_op jit(solution)/shard_map/ppermute | solution.py:111
  91.6 3.5 %collective-permute-done.8 = f32[64,16]{1,0:T(8,128)S(1)} collective-permute-done((f32[64,16]{1,0:T(8,128)S(1)}, f32[64,16]{1,0:T(8,128)S(1)}, u32[]{:S(2)}, u32[]{:S(2)}) %collective-permute-start.8) | collective-permute-done | bytes 4128 | tf_op jit(solution)/shard_map/ppermute | solution.py:111
  95.1 4.2 %collective-permute-start.9 = (f32[64,16]{1,0:T(8,128)S(1)}, f32[64,16]{1,0:T(8,128)S(1)}, u32[]{:S(2)}, u32[]{:S(2)}) collective-permute-start(f32[64,16]{1,0:T(8,128)S(1)} %add.44), channel_id=1, source_target_pairs={{0,192},{8,200},{16,208},{24,216},{32,224},{40,232},{48,240},{56,2... | collective-permute-start | bytes 12296 | tf_op jit(solution)/shard_map/ppermute | solution.py:111
  99.3 1.3 %gather_fusion = f32[64,256]{1,0:T(8,128)} fusion(f32[64,256]{1,0:T(8,128)S(1)} %fusion.10, s32[1024]{0:T(1024)S(1)} %pad_clamp_fusion), kind=kCustom, calls=%fused_computation | custom fusion | bytes 131328 | tf_op jit(solution)/shard_map/jit(_take)/gather | solution.py:116
  100.6 0.6 collective-permute-done.9
  101.2 0.6 gather_fusion.1
  101.8 0.7 copy.39
  (49 shorter events, 4.9 us)
Async XLA Ops:
  0.6 4.5 %copy-start = (bf16[2,2,384,512]{3,2,1,0:T(8,128)(2,1)S(1)}, bf16[2,2,384,512]{3,2,1,0:T(8,128)(2,1)}, u32[]{:S(2)}) copy-start(bf16[2,2,384,512]{3,2,1,0:T(8,128)(2,1)} %param.9) | copy-start | bytes 4718596
  0.6 4.5 %copy-start.1 = (bf16[512,64]{0,1:T(8,128)(2,1)S(1)}, bf16[512,64]{0,1:T(8,128)(2,1)}, u32[]{:S(2)}) copy-start(bf16[512,64]{0,1:T(8,128)(2,1)} %param.11) | copy-start | bytes 196612
  35.4 27.2 %copy-start.2 = (f32[2]{0:T(128)S(1)}, f32[2]{0:T(128)}, u32[]{:S(2)}) copy-start(f32[2]{0:T(128)} %param.13) | copy-start | bytes 28
  36.0 7.4 %collective-permute-start = (bf16[2,2,4096]{2,0,1:T(2,128)(2,1)S(1)}, bf16[2,2,4096]{2,0,1:T(2,128)(2,1)S(1)}, u32[]{:S(2)}, u32[]{:S(2)}) collective-permute-start(bf16[2,2,4096]{2,0,1:T(2,128)(2,1)S(1)} %copy.34), channel_id=1, source_target_pairs={{0,192},{8,200},{16,208},{24,216},{32,224},{40,232},{48,240},{56,2... | collective-permute-start | bytes 98312 | tf_op jit(solution)/shard_map/ppermute | solution.py:99
  43.6 6.0 %collective-permute-start.1 = (bf16[4,2,4096]{2,0,1:T(4,128)(2,1)S(1)}, bf16[4,2,4096]{2,0,1:T(4,128)(2,1)S(1)}, u32[]{:S(2)}, u32[]{:S(2)}) collective-permute-start(bf16[4,2,4096]{2,0,1:T(4,128)(2,1)S(1)} %maximum_select_fusion.4), channel_id=1, source_target_pairs={{0,64},{8,72},{16,80},{24,88},{32,96},{40,104},{48,112},{56,120},{... | collective-permute-start | bytes 196616 | tf_op jit(solution)/shard_map/ppermute | solution.py:99
  49.6 6.3 %collective-permute-start.2 = (bf16[8,2,4096]{2,0,1:T(8,128)(2,1)S(1)}, bf16[8,2,4096]{2,0,1:T(8,128)(2,1)S(1)}, u32[]{:S(2)}, u32[]{:S(2)}) collective-permute-start(bf16[8,2,4096]{2,0,1:T(8,128)(2,1)S(1)} %maximum_select_fusion.3), channel_id=1, source_target_pairs={{0,48},{8,56},{16,32},{24,40},{32,16},{40,24},{48,0},{56,8},{64,11... | collective-permute-start | bytes 393224 | tf_op jit(solution)/shard_map/ppermute | solution.py:99
  56.0 6.5 %collective-permute-start.3 = (bf16[16,2,4096]{2,0,1:T(8,128)(2,1)S(1)}, bf16[16,2,4096]{2,0,1:T(8,128)(2,1)S(1)}, u32[]{:S(2)}, u32[]{:S(2)}) collective-permute-start(bf16[16,2,4096]{2,0,1:T(8,128)(2,1)S(1)} %maximum_select_fusion.2), channel_id=1, source_target_pairs={{0,16},{8,24},{16,0},{24,8},{32,48},{40,56},{48,32},{56,40},{64,80... | collective-permute-start | bytes 786440 | tf_op jit(solution)/shard_map/ppermute | solution.py:99
  62.5 2.0 %collective-permute-start.4 = (bf16[32,2,4096]{2,0,1:T(8,128)(2,1)S(1)}, bf16[32,2,4096]{2,0,1:T(8,128)(2,1)S(1)}, u32[]{:S(2)}, u32[]{:S(2)}) collective-permute-start(bf16[32,2,4096]{2,0,1:T(8,128)(2,1)S(1)} %maximum_select_fusion.1), channel_id=1, source_target_pairs={{0,8},{8,0},{16,24},{24,16},{32,40},{40,32},{48,56},{56,48},{64,72... | collective-permute-start | bytes 1572872 | tf_op jit(solution)/shard_map/ppermute | solution.py:99
  63.2 4.5 %copy-start.5 = (bf16[2,256,4096]{2,1,0:T(8,128)(2,1)S(1)}, bf16[2,256,4096]{2,1,0:T(8,128)(2,1)}, u32[]{:S(2)}) copy-start(bf16[2,256,4096]{2,1,0:T(8,128)(2,1)} %param.12) | copy-start | bytes 12582916
  67.7 1.4 %copy-start.3 = (s32[256]{0:T(256)S(1)}, s32[256]{0:T(256)}, u32[]{:S(2)}) copy-start(s32[256]{0:T(256)} %param.14) | copy-start | bytes 3076
  67.7 31.6 %copy-start.4 = (s32[64]{0:T(128)S(1)}, s32[64]{0:T(128)}, u32[]{:S(2)}) copy-start(s32[64]{0:T(128)} %constant.64) | copy-start | bytes 772
  79.7 1.3 %collective-permute-start.5 = (f32[64,16]{1,0:T(8,128)S(1)}, f32[64,16]{1,0:T(8,128)S(1)}, u32[]{:S(2)}, u32[]{:S(2)}) collective-permute-start(f32[64,16]{1,0:T(8,128)S(1)} %copy.38), channel_id=1, source_target_pairs={{0,8},{8,0},{16,24},{24,16},{32,40},{40,32},{48,56},{56,48},{64,72... | collective-permute-start | bytes 12296 | tf_op jit(solution)/shard_map/ppermute | solution.py:111
  80.9 3.9 %collective-permute-start.6 = (f32[64,16]{1,0:T(8,128)S(1)}, f32[64,16]{1,0:T(8,128)S(1)}, u32[]{:S(2)}, u32[]{:S(2)}) collective-permute-start(f32[64,16]{1,0:T(8,128)S(1)} %add.41), channel_id=1, source_target_pairs={{0,16},{8,24},{16,0},{24,8},{32,48},{40,56},{48,32},{56,40},{64,80... | collective-permute-start | bytes 12296 | tf_op jit(solution)/shard_map/ppermute | solution.py:111
  84.8 5.1 %collective-permute-start.7 = (f32[64,16]{1,0:T(8,128)S(1)}, f32[64,16]{1,0:T(8,128)S(1)}, u32[]{:S(2)}, u32[]{:S(2)}) collective-permute-start(f32[64,16]{1,0:T(8,128)S(1)} %add.42), channel_id=1, source_target_pairs={{0,48},{8,56},{16,32},{24,40},{32,16},{40,24},{48,0},{56,8},{64,11... | collective-permute-start | bytes 12296 | tf_op jit(solution)/shard_map/ppermute | solution.py:111
  90.0 5.2 %collective-permute-start.8 = (f32[64,16]{1,0:T(8,128)S(1)}, f32[64,16]{1,0:T(8,128)S(1)}, u32[]{:S(2)}, u32[]{:S(2)}) collective-permute-start(f32[64,16]{1,0:T(8,128)S(1)} %add.43), channel_id=1, source_target_pairs={{0,64},{8,72},{16,80},{24,88},{32,96},{40,104},{48,112},{56,120},{... | collective-permute-start | bytes 12296 | tf_op jit(solution)/shard_map/ppermute | solution.py:111
  95.1 6.1 %collective-permute-start.9 = (f32[64,16]{1,0:T(8,128)S(1)}, f32[64,16]{1,0:T(8,128)S(1)}, u32[]{:S(2)}, u32[]{:S(2)}) collective-permute-start(f32[64,16]{1,0:T(8,128)S(1)} %add.44), channel_id=1, source_target_pairs={{0,192},{8,200},{16,208},{24,216},{32,224},{40,232},{48,240},{56,2... | collective-permute-start | bytes 12296 | tf_op jit(solution)/shard_map/ppermute | solution.py:111
